TPU v7x, 128 devices: a whole 4x4x4 slice. The times are simulated.
128 devices in a mesh: row: 16 (over z_lo, y, core), col: 8 (over x, z_hi).
Axes of the slice: x: 4, y: 4, z: 4 (z_hi: 2, z_lo: 2; z = z_hi * 2 + z_lo), core: 2. Of those that a mesh axis runs over, the one named last changes fastest.
Arguments:
- frames: bfloat16 [4, 4096, 512], P(None, 'row'), may hold values from -6 to 6
- orders: int32 [2, 2], replicated, may hold values from 1 to 16
- owners: int32 [16384, 1], P(('row', 'col')), may hold values from 0 to 127; in each aligned block of 128 rows (0 to 127, 128 to 255, ...) at most 2 rows name the same one
- templates: bfloat16 [128, 512, 128], P(('row', 'col')), may hold values from -0.25 to 0.25
Outputs:
- spectrum: bfloat16 [2, 4, 4, 2048, 4096], P(None, None, None, ('row', 'col'))
- detections: bfloat16 [128, 128, 2, 16, 128], P(('row', 'col'))
Inputs may be any that keep to these rules, and one draw needn't show every extreme that they name: `owners`: rows 128 * i to 128 * (i + 1) - 1 hold the tiles of the device with index i along row+col. At most 2 tiles of one device name the same owner, and some device reaches that in every draw.
All inputs are finite; a program needn't handle non-finite values.
Results may differ from a plain program's by a relative error of at most 0.0078.
Values may be sent and summed in bfloat16 or wider, within the bound.
No kernel may reach another device: no remote copies, remote signals or barrier semaphores. Data moves between devices by JAX's collectives and lax.ppermute only.
A program may use at most 128 MiB of HBM per device.

v0:
```python
import math

import jax
import jax.numpy as jnp
from jax import lax
from jax.experimental import pallas as pl
from jax.experimental.pallas import tpu as pltpu
from jax.sharding import PartitionSpec as P
import numpy as np

RADIX = 8


def from_behind(block, axis, distance):
    devices = range(lax.axis_size(axis))
    route = [(i - distance, i) for i in devices if i - distance in devices]
    return lax.ppermute(block, axis, route)


def from_behind_2(value, axis, steps):
    count = lax.axis_size(axis)
    pairs = [(source, (source + steps) % count) for source in range(count)]
    return lax.ppermute(value, axis, pairs)


def channel_coefficients(n_total, channel_ids):
    position = jnp.arange(n_total, dtype=jnp.int32)
    turns = position[:, None] * channel_ids[None, :] % n_total
    phase_angle = 2.0 * math.pi / n_total * turns.astype(jnp.float32)
    window = 0.5 - 0.5 * jnp.cos(2.0 * math.pi / n_total * position.astype(jnp.float32))
    gain_factor = math.sqrt(8.0 / (3.0 * n_total))
    weighted = gain_factor * window[:, None]
    both = jnp.concatenate(
        [weighted * jnp.cos(phase_angle), weighted * jnp.sin(phase_angle)], axis=1
    )
    return both.astype(jnp.bfloat16)


def sub_coefficients(sub_total):
    index_a = jnp.arange(sub_total, dtype=jnp.int32)
    turns = index_a[:, None] * index_a[None, :] % sub_total
    phase_angle = 2.0 * math.pi / sub_total * turns.astype(jnp.float32)
    return jnp.concatenate([jnp.cos(phase_angle), jnp.sin(phase_angle)], axis=1).astype(
        jnp.bfloat16
    )


def quarter_turn(a_cos, a_sin, channel_ids, hop_ids):
    phase_step = channel_ids[:, None] % 4 * (hop_ids[None, :] % 4) % 4
    cos_quarter = (phase_step == 0).astype(jnp.float32) - (phase_step == 2).astype(jnp.float32)
    sin_quarter = (phase_step == 1).astype(jnp.float32) - (phase_step == 3).astype(jnp.float32)
    real_part = a_cos * cos_quarter - a_sin * sin_quarter
    imag_part = -a_sin * cos_quarter - a_cos * sin_quarter
    return (real_part, imag_part)


def finish_transform(first_real, first_imag, hops_total):
    radix_count = first_real.shape[-2]
    sub_total = first_real.shape[-1]
    index_b = jnp.arange(radix_count, dtype=jnp.int32)[:, None]
    index_p = jnp.arange(sub_total, dtype=jnp.int32)[None, :]
    twist_angle = 2.0 * math.pi / hops_total * (index_b * index_p % hops_total).astype(jnp.float32)
    twist_cos = jnp.cos(twist_angle)
    twist_sin = jnp.sin(twist_angle)
    twist_real = first_real * twist_cos + first_imag * twist_sin
    twist_imag = first_imag * twist_cos - first_real * twist_sin
    index_d = jnp.arange(radix_count, dtype=jnp.int32)[None, :]
    section_angle = (
        2.0 * math.pi / radix_count * (index_b * index_d % radix_count).astype(jnp.float32)
    )
    section_cos = jnp.cos(section_angle)
    section_sin = jnp.sin(section_angle)
    highest = lax.Precision.HIGHEST
    norm_factor = 1.0 / math.sqrt(hops_total)
    out_real = norm_factor * (
        jnp.einsum("...bq,bd->...dq", twist_real, section_cos, precision=highest)
        + jnp.einsum("...bq,bd->...dq", twist_imag, section_sin, precision=highest)
    )
    out_imag = norm_factor * (
        jnp.einsum("...bq,bd->...dq", twist_imag, section_cos, precision=highest)
        - jnp.einsum("...bq,bd->...dq", twist_real, section_sin, precision=highest)
    )
    return (out_real, out_imag)


def section_mixers(radix_count, rows_per):
    index_b = np.arange(radix_count)
    angle = 2.0 * np.pi / radix_count * ((index_b[:, None] * index_b[None, :]) % radix_count)
    mixers = []
    for table in (np.cos(angle).astype(np.float32), np.sin(angle).astype(np.float32)):
        full = np.zeros((radix_count * rows_per, rows_per * radix_count), np.float32)
        for d in range(radix_count):
            for b in range(radix_count):
                for k in range(rows_per):
                    full[d * rows_per + k, k * radix_count + b] = table[b, d]
        high = jnp.asarray(full).astype(jnp.bfloat16)
        low = (jnp.asarray(full) - high.astype(jnp.float32)).astype(jnp.bfloat16)
        mixers += [high, low]
    return jnp.stack(mixers)


def spectrum_kernel(prod_ref, cos_ref, sin_ref, twc_ref, tws_ref, mix_ref, spec_ref, tile_ref):
    f32 = jnp.float32
    prod_real = prod_ref[0, 0]
    prod_imag = prod_ref[1, 0]
    sub_cos = cos_ref[...]
    sub_sin = sin_ref[...]
    first_real = jnp.dot(prod_real, sub_cos, preferred_element_type=f32) + jnp.dot(
        prod_imag, sub_sin, preferred_element_type=f32
    )
    first_imag = jnp.dot(prod_imag, sub_cos, preferred_element_type=f32) - jnp.dot(
        prod_real, sub_sin, preferred_element_type=f32
    )
    twist_cos = twc_ref[...]
    twist_sin = tws_ref[...]
    twist_real = first_real * twist_cos + first_imag * twist_sin
    twist_imag = first_imag * twist_cos - first_real * twist_sin

    def split(value):
        high = value.astype(jnp.bfloat16)
        return high, (value - high.astype(f32)).astype(jnp.bfloat16)

    real_high, real_low = split(twist_real)
    imag_high, imag_low = split(twist_imag)

    def mix(table, high, low):
        return (
            jnp.dot(mix_ref[table], high, preferred_element_type=f32)
            + jnp.dot(mix_ref[table], low, preferred_element_type=f32)
            + jnp.dot(mix_ref[table + 1], high, preferred_element_type=f32)
        )

    out_real = mix(0, real_high, real_low) + mix(2, imag_high, imag_low)
    out_imag = mix(0, imag_high, imag_low) - mix(2, real_high, real_low)
    feature = jnp.log1p(out_real * out_real + out_imag * out_imag)
    rows_per = tile_ref.shape[1]
    sub_n = tile_ref.shape[2]
    for d in range(tile_ref.shape[0]):
        rows = slice(d * rows_per, (d + 1) * rows_per)
        lanes = slice(d * sub_n, (d + 1) * sub_n)
        spec_ref[0, 0, 0, :, lanes] = out_real[rows].astype(spec_ref.dtype)
        spec_ref[1, 0, 0, :, lanes] = out_imag[rows].astype(spec_ref.dtype)
        tile_ref[d] = feature[rows].astype(tile_ref.dtype)


def spectrum_call(products, table_sub, hops_total):
    _, sensors, combos, rows, sub_n = products.shape
    per_device = rows // RADIX
    blocks = sensors * combos
    flat = products.reshape(2, blocks, rows, sub_n)
    index_b = jnp.arange(RADIX, dtype=jnp.int32)[:, None]
    index_p = jnp.arange(sub_n, dtype=jnp.int32)[None, :]
    twist_angle = 2.0 * math.pi / hops_total * (index_b * index_p % hops_total).astype(jnp.float32)
    norm_factor = 1.0 / math.sqrt(hops_total)
    twist_cos = jnp.tile(norm_factor * jnp.cos(twist_angle), (per_device, 1))
    twist_sin = jnp.tile(norm_factor * jnp.sin(twist_angle), (per_device, 1))
    mixers = section_mixers(RADIX, per_device)
    spectrum, tiles = pl.pallas_call(
        spectrum_kernel,
        grid=(blocks,),
        in_specs=[
            pl.BlockSpec((2, 1, rows, sub_n), lambda i: (0, i, 0, 0)),
            pl.BlockSpec((sub_n, sub_n), lambda i: (0, 0)),
            pl.BlockSpec((sub_n, sub_n), lambda i: (0, 1)),
            pl.BlockSpec((rows, sub_n), lambda i: (0, 0)),
            pl.BlockSpec((rows, sub_n), lambda i: (0, 0)),
            pl.BlockSpec((4, rows, rows), lambda i: (0, 0, 0)),
        ],
        out_specs=[
            pl.BlockSpec(
                (2, 1, 1, per_device, RADIX * sub_n),
                lambda i: (0, i // combos, i % combos, 0, 0),
            ),
            pl.BlockSpec((RADIX, per_device, sub_n), lambda i: (i, 0, 0)),
        ],
        out_shape=[
            jax.ShapeDtypeStruct((2, sensors, combos, per_device, RADIX * sub_n), jnp.bfloat16),
            jax.ShapeDtypeStruct((blocks * RADIX, per_device, sub_n), jnp.bfloat16),
        ],
        compiler_params=pltpu.CompilerParams(vmem_limit_bytes=48 * 1024 * 1024),
        cost_estimate=pl.CostEstimate(
            flops=blocks * (8 * rows * sub_n * sub_n + 24 * rows * rows * sub_n),
            transcendentals=blocks * rows * sub_n,
            bytes_accessed=blocks * rows * sub_n * 2 * 5 + 4 * sub_n * sub_n,
        ),
    )(flat, table_sub, table_sub, twist_cos, twist_sin, mixers)
    return spectrum, tiles


def shards(frames, orders, owners, templates):
    rows_count = lax.axis_size("row")
    cols_count = lax.axis_size("col")
    devices_n = rows_count * cols_count
    sensors = frames.shape[0]
    hop_dev = frames.shape[1]
    frame_len = frames.shape[2]
    channels_n = 4 * frame_len
    hops_n = hop_dev * rows_count
    sub_n = hops_n // RADIX
    per_device = channels_n // devices_n
    local_channels = channels_n // cols_count
    combos = orders.shape[0] * orders.shape[1]
    feat_n = templates.shape[2]
    row_at = lax.axis_index("row")
    col_at = lax.axis_index("col")
    tail_frames = from_behind(frames[:, :3], "row", -1)
    padded = jnp.concatenate([frames, tail_frames], axis=1)
    column = jnp.arange(local_channels, dtype=jnp.int32)
    channel_ids = (column // per_device * cols_count + col_at) * per_device + column % per_device
    coefficients = channel_coefficients(channels_n, channel_ids)
    summed = jnp.zeros((sensors, 2 * local_channels, hop_dev), jnp.float32)
    for quarter in range(4):
        summed = summed + jnp.einsum(
            "shf,fk->skh",
            padded[:, quarter : quarter + hop_dev],
            coefficients[quarter * frame_len : (quarter + 1) * frame_len],
            preferred_element_type=jnp.float32,
        )
    hop_ids = row_at * hop_dev + jnp.arange(hop_dev, dtype=jnp.int32)
    real_part, imag_part = quarter_turn(
        summed[:, :local_channels], summed[:, local_channels:], channel_ids, hop_ids
    )
    demod = jnp.stack([real_part, imag_part]).astype(jnp.bfloat16)
    swapped = lax.all_to_all(demod, "row", split_axis=2, concat_axis=3, tiled=True)
    ordered = swapped.reshape(2, sensors, per_device, sub_n, RADIX).transpose(0, 1, 2, 4, 3)
    above = from_behind_2(ordered, ("row", "col"), -1)
    extended = jnp.concatenate([ordered, above], axis=2)
    own_real = ordered[0].astype(jnp.float32)
    own_imag = ordered[1].astype(jnp.float32)
    prod_real = []
    prod_imag = []
    for wheel in range(orders.shape[0]):
        for order_at in range(orders.shape[1]):
            partner = lax.dynamic_slice_in_dim(
                extended, orders[wheel, order_at], per_device, axis=2
            )
            partner = partner.astype(jnp.float32)
            prod_real.append(own_real * partner[0] + own_imag * partner[1])
            prod_imag.append(own_imag * partner[0] - own_real * partner[1])
    products = jnp.stack([jnp.stack(prod_real, axis=1), jnp.stack(prod_imag, axis=1)]).astype(
        jnp.bfloat16
    )
    table_sub = sub_coefficients(sub_n)
    spectrum, tiles = spectrum_call(
        products.reshape(2, sensors, combos, per_device * RADIX, sub_n), table_sub, hops_n
    )
    tiles_dev = sensors * combos * RADIX
    capacity = max(2, 2 * tiles_dev // devices_n)
    owner_ids = owners[:, 0]
    targets = jnp.arange(devices_n, dtype=jnp.int32)
    one_hot = (owner_ids[:, None] == targets[None, :]).astype(jnp.int32)
    before = jnp.cumsum(one_hot, axis=0) - one_hot
    slot_ids = jnp.sum(before * one_hot, axis=1)
    places = owner_ids * capacity + slot_ids
    slot_range = jnp.arange(devices_n * capacity, dtype=jnp.int32)
    placing = (places[None, :] == slot_range[:, None]).astype(jnp.bfloat16)
    outgoing = jnp.einsum("ot,tkq->okq", placing, tiles, preferred_element_type=jnp.float32)
    outgoing = outgoing.astype(jnp.bfloat16).reshape(devices_n, capacity * per_device, sub_n)
    arrived = lax.all_to_all(outgoing, ("row", "col"), split_axis=0, concat_axis=0, tiled=True)
    found = jnp.einsum(
        "tkq,qf->tkf", arrived, templates[0], preferred_element_type=jnp.float32
    ).astype(jnp.bfloat16)
    found = found.reshape(devices_n, capacity, per_device, feat_n)
    return (spectrum, found[None])


def solution(mesh):
    in_specs = (P(None, "row", None), P(), P(("row", "col"), None), P(("row", "col"), None, None))
    out_specs = (
        P(None, None, None, ("row", "col"), None),
        P(("row", "col"), None, None, None, None),
    )
    return jax.shard_map(shards, mesh=mesh, in_specs=in_specs, out_specs=out_specs, check_vma=False)
```

profile of v0, /device:TPU:0, one launch (start us, length us, event | category | flops | bytes accessed | tf_op | source)
XLA Modules:
  0.0 183.7 jit_solution(9722833989839572384)
XLA Ops:
  0.7 0.9 slice.82
  1.5 1.3 collective-permute-start
  2.9 9.1 %multiply_convert_fusion = (bf16[2048,256]{0,1:T(8,128)(2,1)S(1)}, bf16[2048,256]{0,1:T(8,128)(2,1)S(1)}) fusion(s32[256]{0:T(256)S(1)} %fusion.87, f32[2048]{0:T(1024)S(1)} %subtract_multiply_fusion), kind=kLoop, calls=%fused_computation.44 | loop fusion | flops 9437184 | bytes 2106368 | tf_op jit(solution)/shard_map/convert.27
  12.0 0.8 fusion.65
  12.7 0.3 convert_subtract_fusion.1
  13.1 0.8 fusion.43
  13.9 0.8 fusion.45
  14.6 0.8 add_bitcast_fusion
  15.5 0.4 fusion.50
  16.0 1.8 copy.57
  17.8 6.8 %all-to-all-start = ((bf16[2,4,256,256]{3,1,0,2:T(4,128)(2,1)}), bf16[2,4,256,256]{3,1,0,2:T(4,128)(2,1)S(1)}, u32[]{:S(2)}, u32[]{:S(2)}) async-start(bf16[2,4,256,256]{3,1,0,2:T(4,128)(2,1)} %copy.57), calls=%async_computation | async-start | bytes 2097152 | tf_op jit(solution)/shard_map/all_to_all | solution.py:224
  24.6 0.7 fusion.97
  30.4 0.2 reduce_window_sum.11
  33.1 7.9 %all-to-all-done = bf16[2,4,256,256]{3,1,0,2:T(4,128)(2,1)S(1)} async-done(((bf16[2,4,256,256]{3,1,0,2:T(4,128)(2,1)}), bf16[2,4,256,256]{3,1,0,2:T(4,128)(2,1)S(1)}, u32[]{:S(2)}, u32[]{:S(2)}) %all-to-all-start) | async-done | bytes 1048608 | tf_op jit(solution)/shard_map/all_to_all | solution.py:224
  41.0 5.9 %copy.58 = bf16[2,4,16,16,256]{3,4,2,1,0:T(8,128)(2,1)} copy(bf16[2,4,16,16,256]{4,1,0,3,2:T(4,128)(2,1)S(1)} %bitcast.85) | data formatting | bytes 2097152 | tf_op jit(solution)/shard_map/all_to_all | solution.py:224
  46.9 9.1 %copy.59 = bf16[2,4,16,512,8]{3,4,2,1,0:T(8,128)(2,1)S(1)} copy(bf16[2,4,16,512,8]{2,4,3,1,0:T(8,128)(2,1)} %bitcast.77) | data formatting | bytes 2097152 | tf_op jit(solution)/shard_map/reshape | solution.py:225
  56.0 4.8 %collective-permute-start.1 = (bf16[2,4,16,8,512]{4,3,2,1,0:T(8,128)(2,1)S(1)}, bf16[2,4,16,8,512]{4,3,2,1,0:T(8,128)(2,1)S(1)}, u32[]{:S(2)}, u32[]{:S(2)}) collective-permute-start(bf16[2,4,16,8,512]{4,3,2,1,0:T(8,128)(2,1)S(1)} %bitcast.79), channel_id=1, source_target_pairs={{0,127},{1,0},{2,1},{3,2},{4,3},{5,4},{6,5},{7,6},{8,7},{9,8},{10,... | collective-permute-start | bytes 3145736 | tf_op jit(solution)/shard_map/ppermute | solution.py:23
  61.0 0.2 select_reduce_fusion
  61.2 4.3 %sine_convert_fusion = (bf16[512,512]{1,0:T(8,128)(2,1)S(1)}, bf16[512,512]{1,0:T(8,128)(2,1)S(1)}) fusion(), kind=kLoop, calls=%fused_computation.88 | loop fusion | flops 4194304 | bytes 1048576 | tf_op jit(solution)/shard_map/convert.1
  65.7 18.0 %collective-permute-done.1 = bf16[2,4,16,8,512]{4,3,2,1,0:T(8,128)(2,1)S(1)} collective-permute-done((bf16[2,4,16,8,512]{4,3,2,1,0:T(8,128)(2,1)S(1)}, bf16[2,4,16,8,512]{4,3,2,1,0:T(8,128)(2,1)S(1)}, u32[]{:S(2)}, u32[]{:S(2)}) %collective-permute-start.1) | collective-permute-done | bytes 1048608 | tf_op jit(solution)/shard_map/ppermute | solution.py:23
  83.7 2.4 %fusion.34 = (f32[2,4,16,8,512]{4,3,2,1,0:T(8,128)S(1)}, f32[2,4,16,8,512]{4,3,2,1,0:T(8,128)S(1)}, f32[2,4,16,8,512]{4,3,2,1,0:T(8,128)S(1)}, f32[2,4,16,8,512]{4,3,2,1,0:T(8,128)S(1)}) fusion(s32[]{:T(128)S(6)} %select_n.110, bf16[2,4,16,8,512]{4,3,2,1,0:T(8,128)(2,1)S(1)} %bitcast.80, bf16[2,4,16,8,512]{4,3,2,1,0:T(8,128)(2,1)S(1)} %collective-permute-done.1, ...), kind=kLoop, calls=%fused_computation.75 | loop fusion | flops 4194304 | bytes 10485776 | tf_op jit(solution)/shard_map/convert_element_type | solution.py:237
  86.1 0.7 fusion.59
  86.8 0.8 fusion.58
  87.6 0.3 pad_maximum_fusion.2
  87.9 0.3 pad_maximum_fusion.1
  88.1 2.3 %pad_maximum_fusion.prod_ref = bf16[2,16,128,512]{3,2,1,0:T(8,128)(2,1)} fusion(bf16[1,16,128,512]{3,2,1,0:T(8,128)(2,1)S(1)} %bitcast.83, bf16[1,16,128,512]{3,2,1,0:T(8,128)(2,1)S(1)} %bitcast.84), kind=kLoop, calls=%fused_computation | loop fusion | flops 2097152 | bytes 8388608 | tf_op jit(solution)/shard_map/stack | solution.py:240
  90.5 20.7 %shard_map.77 = (bf16[2,4,4,16,4096]{4,3,2,1,0:T(8,128)(2,1)}, bf16[128,16,512]{2,1,0:T(8,128)(2,1)S(1)}) custom-call(bf16[2,16,128,512]{3,2,1,0:T(8,128)(2,1)} %pad_maximum_fusion.prod_ref, bf16[512,1024]{1,0:T(8,128)(2,1)S(1)} %pad_maximum_fusion.4.cos_ref.sin_ref, bf16[512,1024]{1,0:T(8,128)(2,1)S(1)} %pad_maximum_fusion.4.cos_ref.sin_ref, ...), custom_call_target="tpu_custom_call" | custom-call | flops 7516192768 | bytes 11534336 | tf_op jit(solution)/shard_map/pallas_call | solution.py:158
  111.1 3.0 %convolution_convert_fusion = bf16[256,16,512]{2,0,1:T(8,128)(2,1)S(1)} fusion(bf16[128,16,512]{2,1,0:T(8,128)(2,1)S(1)} %get-tuple-element.5, s32[128]{0:T(128)S(1)} %multiply_add_fusion), kind=kOutput, calls=%fused_computation.30 | convolution fusion | flops 539000832 | bytes 6291968 | tf_op jit(solution)/shard_map/ot,tkq->okq/dot_general | solution.py:257
  114.2 2.4 %copy.69 = bf16[256,16,512]{2,1,0:T(8,128)(2,1)S(1)} copy(bf16[256,16,512]{2,0,1:T(8,128)(2,1)S(1)} %convolution_convert_fusion) | data formatting | bytes 8388608 | tf_op jit(solution)/shard_map/convert_element_type | solution.py:258
  116.6 60.7 %all_to_all.20 = bf16[128,32,512]{2,1,0:T(8,128)(2,1)S(1)} all-to-all(bf16[128,32,512]{2,1,0:T(8,128)(2,1)S(1)} %bitcast.78), channel_id=1, replica_groups=mesh['row'=16,'col'=8] {'row','col'}, dimensions={0} | all-to-all | bytes 8388608 | tf_op jit(solution)/shard_map/all_to_all | solution.py:259
  177.3 4.7 %fusion.9 = bf16[128,32,128]{2,0,1:T(8,128)(2,1)S(1)} fusion(bf16[128,32,512]{2,1,0:T(8,128)(2,1)S(1)} %all_to_all.20, bf16[1,512,128]{2,1,0:T(8,128)(2,1)S(1)} %copy-done), kind=kOutput, calls=%fused_computation.52 | convolution fusion | flops 537395200 | bytes 5373952 | tf_op jit(solution)/shard_map/tkq,qf->tkf/dot_general | solution.py:260
  182.0 1.7 copy.71
  (23 shorter events, 0.7 us)
Async XLA Ops:
  0.6 176.6 %copy-start = (bf16[1,512,128]{2,1,0:T(8,128)(2,1)S(1)}, bf16[1,512,128]{2,1,0:T(8,128)(2,1)}, u32[]{:S(2)}) copy-start(bf16[1,512,128]{2,1,0:T(8,128)(2,1)} %param.9) | copy-start | bytes 393220
  0.6 11.3 %copy-start.2 = (bf16[4,256,512]{2,1,0:T(8,128)(2,1)S(1)}, bf16[4,256,512]{2,1,0:T(8,128)(2,1)}, u32[]{:S(2)}) copy-start(bf16[4,256,512]{2,1,0:T(8,128)(2,1)} %param.6) | copy-start | bytes 3145732
  1.5 11.6 %collective-permute-start = (bf16[4,3,512]{2,1,0:T(4,128)(2,1)S(1)}, bf16[4,3,512]{2,1,0:T(4,128)(2,1)S(1)}, u32[]{:S(2)}, u32[]{:S(2)}) collective-permute-start(bf16[4,3,512]{2,1,0:T(4,128)(2,1)S(1)} %slice.82), channel_id=1, source_target_pairs={{8,0},{16,8},{24,16},{32,24},{40,32},{48,40},{56,48},{64,56},{72,6... | collective-permute-start | bytes 36872 | tf_op jit(solution)/shard_map/ppermute | solution.py:17
  16.0 8.6 %copy-start.3 = (s32[2,2]{1,0:T(2,128)S(1)}, s32[2,2]{1,0:T(2,128)}, u32[]{:S(2)}) copy-start(s32[2,2]{1,0:T(2,128)} %param.7) | copy-start | bytes 52
  16.0 14.3 %copy-start.4 = (s32[128,1]{0,1:T(1,128)S(1)}, s32[128,1]{0,1:T(1,128)}, u32[]{:S(2)}) copy-start(s32[128,1]{0,1:T(1,128)} %param.8) | copy-start | bytes 1540
  17.8 23.2 %all-to-all-start = ((bf16[2,4,256,256]{3,1,0,2:T(4,128)(2,1)}), bf16[2,4,256,256]{3,1,0,2:T(4,128)(2,1)S(1)}, u32[]{:S(2)}, u32[]{:S(2)}) async-start(bf16[2,4,256,256]{3,1,0,2:T(4,128)(2,1)} %copy.57), calls=%async_computation | async-start | bytes 2097152 | tf_op jit(solution)/shard_map/all_to_all | solution.py:224
  56.0 27.7 %collective-permute-start.1 = (bf16[2,4,16,8,512]{4,3,2,1,0:T(8,128)(2,1)S(1)}, bf16[2,4,16,8,512]{4,3,2,1,0:T(8,128)(2,1)S(1)}, u32[]{:S(2)}, u32[]{:S(2)}) collective-permute-start(bf16[2,4,16,8,512]{4,3,2,1,0:T(8,128)(2,1)S(1)} %bitcast.79), channel_id=1, source_target_pairs={{0,127},{1,0},{2,1},{3,2},{4,3},{5,4},{6,5},{7,6},{8,7},{9,8},{10,... | collective-permute-start | bytes 3145736 | tf_op jit(solution)/shard_map/ppermute | solution.py:23
  88.1 2.3 %copy-start.1 = (bf16[4,128,128]{2,1,0:T(8,128)(2,1)S(1)}, bf16[4,128,128]{2,1,0:T(8,128)(2,1)}, u32[]{:S(2)}) copy-start(bf16[4,128,128]{2,1,0:T(8,128)(2,1)} %constant.166.mix_ref) | copy-start | bytes 393220
where the time goes:
time: 184 us
  blocking collectives  60.7 us (33%)
  waiting for transfers between devices  25.9 us (14%)
  local copies, waits for them, and re-layouts  22.6 us (12%)
  other arithmetic  21.6 us (12%)
  Pallas kernels  20.7 us (11%)
  starting transfers between devices  12.8 us (7%)
  matrix products  10.9 us (6%)
  between operations  8.53 us (5%)
    all_to_all x1, blocking collectives, shards(): lax.all_to_all(outgoing, ('row', 'col'), split_axis=0, concat_axis=0, til...  60.7 us
    pallas_call x1, Pallas kernels, spectrum_call(): pl.pallas_call(spectrum_kernel, grid=(blocks,), in_specs=[pl.BlockSpec((2...  20.7 us
    ppermute x1, waiting for transfers between devices, from_behind_2(): return lax.ppermute(value, axis, pairs)  18 us
    another operation x2, other arithmetic  13.4 us
    reshape x1, local copies, waits for them, and re-layouts, shards(): swapped.reshape(2, sensors, per_device, sub_n, RADIX)  9.14 us
    all_to_all x1, waiting for transfers between devices, shards(): lax.all_to_all(demod, 'row', split_axis=2, concat_axis=3, tiled=True)  7.91 us
    all_to_all x1, starting transfers between devices, shards(): lax.all_to_all(demod, 'row', split_axis=2, concat_axis=3, tiled=True)  6.77 us
    all_to_all x1, local copies, waits for them, and re-layouts, shards(): lax.all_to_all(demod, 'row', split_axis=2, concat_axis=3, tiled=True)  5.9 us
  transfers between devices with their start and end apart: 3, of which 2 were waited for; matrix products, arithmetic and copies ran while one was open for 9% of the time, Pallas kernels for 0%

commit v1 on v0

--- a/solution.py
+++ b/solution.py
@@ -256,7 +256,11 @@
     placing = (places[None, :] == slot_range[:, None]).astype(jnp.bfloat16)
     outgoing = jnp.einsum("ot,tkq->okq", placing, tiles, preferred_element_type=jnp.float32)
     outgoing = outgoing.astype(jnp.bfloat16).reshape(devices_n, capacity * per_device, sub_n)
-    arrived = lax.all_to_all(outgoing, ("row", "col"), split_axis=0, concat_axis=0, tiled=True)
+    rows_count_ = lax.axis_size("row")
+    staged = outgoing.reshape(rows_count_, cols_count, capacity * per_device, sub_n)
+    staged = lax.all_to_all(staged, "col", split_axis=1, concat_axis=1, tiled=True)
+    staged = lax.all_to_all(staged, "row", split_axis=0, concat_axis=0, tiled=True)
+    arrived = staged.reshape(devices_n, capacity * per_device, sub_n)
     found = jnp.einsum(
         "tkq,qf->tkf", arrived, templates[0], preferred_element_type=jnp.float32
     ).astype(jnp.bfloat16)

time: 184 us -> 237 us (1.29)
  blocking collectives: 60.7 us -> 112 us
    all_to_all x1 -> x2, blocking collectives: 60.7 us -> 112 us  [the longest x1 58.8 us: shards(): lax.all_to_all(staged, 'col', split_axis=1, concat_axis=1, tiled=True)]
  transfers between devices with their start and end apart: 3 -> 3, of which waited for: 2 -> 2; matrix products, arithmetic and copies ran while one was open for 9% -> 7% of each run, Pallas kernels for 0% -> 0%
where the time goes in v1:
time: 237 us; the launch traced here: 236 us
  blocking collectives  112 us (47%)
  waiting for transfers between devices  25.9 us (11%)
  local copies, waits for them, and re-layouts  23.7 us (10%)
  other arithmetic  21.6 us (9%)
  Pallas kernels  20.7 us (9%)
  starting transfers between devices  12.8 us (5%)
  matrix products  10.9 us (5%)
  between operations  8.54 us (4%)
    all_to_all x1, blocking collectives, shards(): lax.all_to_all(staged, 'col', split_axis=1, concat_axis=1, tiled=True)  58.8 us
    all_to_all x1, blocking collectives, shards(): lax.all_to_all(staged, 'row', split_axis=0, concat_axis=0, tiled=True)  53.1 us
    pallas_call x1, Pallas kernels, spectrum_call(): pl.pallas_call(spectrum_kernel, grid=(blocks,), in_specs=[pl.BlockSpec((2...  20.7 us
    ppermute x1, waiting for transfers between devices, from_behind_2(): return lax.ppermute(value, axis, pairs)  18 us
    another operation x2, other arithmetic  13.4 us
    reshape x1, local copies, waits for them, and re-layouts, shards(): swapped.reshape(2, sensors, per_device, sub_n, RADIX)  9.14 us
    all_to_all x1, waiting for transfers between devices, shards(): lax.all_to_all(demod, 'row', split_axis=2, concat_axis=3, tiled=True)  7.91 us
    all_to_all x1, starting transfers between devices, shards(): lax.all_to_all(demod, 'row', split_axis=2, concat_axis=3, tiled=True)  6.77 us
  transfers between devices with their start and end apart: 3, of which 2 were waited for; matrix products, arithmetic and copies ran while one was open for 7% of the time, Pallas kernels for 0%

profile of v1, /device:TPU:0, one launch (start us, length us, event | category | flops | bytes accessed | tf_op | source)
XLA Modules:
  0.0 235.9 jit_solution(18363108453958018345)
XLA Ops:
  0.7 0.9 slice.82
  1.5 1.3 collective-permute-start
  2.9 9.1 %multiply_convert_fusion = (bf16[2048,256]{0,1:T(8,128)(2,1)S(1)}, bf16[2048,256]{0,1:T(8,128)(2,1)S(1)}) fusion(s32[256]{0:T(256)S(1)} %fusion.88, f32[2048]{0:T(1024)S(1)} %subtract_multiply_fusion), kind=kLoop, calls=%fused_computation.45 | loop fusion | flops 9437184 | bytes 2106368 | tf_op jit(solution)/shard_map/convert.27
  12.0 0.8 fusion.66
  13.1 0.8 fusion.44
  13.9 0.8 fusion.46
  14.6 0.8 add_bitcast_fusion
  15.5 0.4 fusion.51
  16.0 1.8 copy.82
  17.8 6.8 %all-to-all-start = ((bf16[2,4,256,256]{3,1,0,2:T(4,128)(2,1)}), bf16[2,4,256,256]{3,1,0,2:T(4,128)(2,1)S(1)}, u32[]{:S(2)}, u32[]{:S(2)}) async-start(bf16[2,4,256,256]{3,1,0,2:T(4,128)(2,1)} %copy.82), calls=%async_computation | async-start | bytes 2097152 | tf_op jit(solution)/shard_map/all_to_all | solution.py:224
  24.6 0.7 fusion.98
  33.1 7.9 %all-to-all-done = bf16[2,4,256,256]{3,1,0,2:T(4,128)(2,1)S(1)} async-done(((bf16[2,4,256,256]{3,1,0,2:T(4,128)(2,1)}), bf16[2,4,256,256]{3,1,0,2:T(4,128)(2,1)S(1)}, u32[]{:S(2)}, u32[]{:S(2)}) %all-to-all-start) | async-done | bytes 1048608 | tf_op jit(solution)/shard_map/all_to_all | solution.py:224
  41.0 5.9 %copy.83 = bf16[2,4,16,16,256]{3,4,2,1,0:T(8,128)(2,1)} copy(bf16[2,4,16,16,256]{4,1,0,3,2:T(4,128)(2,1)S(1)} %bitcast.90) | data formatting | bytes 2097152 | tf_op jit(solution)/shard_map/all_to_all | solution.py:224
  46.9 9.1 %copy.84 = bf16[2,4,16,512,8]{3,4,2,1,0:T(8,128)(2,1)S(1)} copy(bf16[2,4,16,512,8]{2,4,3,1,0:T(8,128)(2,1)} %bitcast.82) | data formatting | bytes 2097152 | tf_op jit(solution)/shard_map/reshape | solution.py:225
  56.0 4.8 %collective-permute-start.1 = (bf16[2,4,16,8,512]{4,3,2,1,0:T(8,128)(2,1)S(1)}, bf16[2,4,16,8,512]{4,3,2,1,0:T(8,128)(2,1)S(1)}, u32[]{:S(2)}, u32[]{:S(2)}) collective-permute-start(bf16[2,4,16,8,512]{4,3,2,1,0:T(8,128)(2,1)S(1)} %bitcast.84), channel_id=1, source_target_pairs={{0,127},{1,0},{2,1},{3,2},{4,3},{5,4},{6,5},{7,6},{8,7},{9,8},{10,... | collective-permute-start | bytes 3145736 | tf_op jit(solution)/shard_map/ppermute | solution.py:23
  61.2 4.3 %sine_convert_fusion = (bf16[512,512]{1,0:T(8,128)(2,1)S(1)}, bf16[512,512]{1,0:T(8,128)(2,1)S(1)}) fusion(), kind=kLoop, calls=%fused_computation.89 | loop fusion | flops 4194304 | bytes 1048576 | tf_op jit(solution)/shard_map/convert.1
  65.7 18.0 %collective-permute-done.1 = bf16[2,4,16,8,512]{4,3,2,1,0:T(8,128)(2,1)S(1)} collective-permute-done((bf16[2,4,16,8,512]{4,3,2,1,0:T(8,128)(2,1)S(1)}, bf16[2,4,16,8,512]{4,3,2,1,0:T(8,128)(2,1)S(1)}, u32[]{:S(2)}, u32[]{:S(2)}) %collective-permute-start.1) | collective-permute-done | bytes 1048608 | tf_op jit(solution)/shard_map/ppermute | solution.py:23
  83.7 2.3 fusion.35
  86.0 0.7 fusion.60
  86.7 0.8 fusion.59
  87.5 0.3 pad_maximum_fusion.2
  87.8 0.3 pad_maximum_fusion.1
  88.1 2.3 pad_maximum_fusion.prod_ref
  90.4 20.7 %shard_map.77 = (bf16[2,4,4,16,4096]{4,3,2,1,0:T(8,128)(2,1)}, bf16[128,16,512]{2,1,0:T(8,128)(2,1)S(1)}) custom-call(bf16[2,16,128,512]{3,2,1,0:T(8,128)(2,1)} %pad_maximum_fusion.prod_ref, bf16[512,1024]{1,0:T(8,128)(2,1)S(1)} %pad_maximum_fusion.4.cos_ref.sin_ref, bf16[512,1024]{1,0:T(8,128)(2,1)S(1)} %pad_maximum_fusion.4.cos_ref.sin_ref, ...), custom_call_target="tpu_custom_call" | custom-call | flops 7516192768 | bytes 11534336 | tf_op jit(solution)/shard_map/pallas_call | solution.py:158
  111.1 3.0 %convolution_convert_fusion = bf16[256,16,512]{2,0,1:T(8,128)(2,1)S(1)} fusion(bf16[128,16,512]{2,1,0:T(8,128)(2,1)S(1)} %get-tuple-element.5, s32[128]{0:T(128)S(1)} %multiply_add_fusion), kind=kOutput, calls=%fused_computation.31 | convolution fusion | flops 539000832 | bytes 6291968 | tf_op jit(solution)/shard_map/ot,tkq->okq/dot_general | solution.py:257
  114.1 2.4 %copy.94 = bf16[256,16,512]{2,1,0:T(8,128)(2,1)S(1)} copy(bf16[256,16,512]{2,0,1:T(8,128)(2,1)S(1)} %convolution_convert_fusion) | data formatting | bytes 8388608 | tf_op jit(solution)/shard_map/convert_element_type | solution.py:258
  116.5 0.6 copy.95
  117.1 58.8 %all_to_all.25 = bf16[16,8,32,512]{3,2,0,1:T(8,128)(2,1)S(1)} all-to-all(bf16[16,8,32,512]{3,2,0,1:T(8,128)(2,1)S(1)} %copy.95), channel_id=1, replica_groups=mesh['row'=16,'col'=8] {'col'}, dimensions={1} | all-to-all | bytes 8388608 | tf_op jit(solution)/shard_map/all_to_all | solution.py:261
  175.9 0.6 copy.96
  176.5 53.1 %all_to_all.26 = bf16[16,8,32,512]{3,2,1,0:T(8,128)(2,1)S(1)} all-to-all(bf16[16,8,32,512]{3,2,1,0:T(8,128)(2,1)S(1)} %copy.96), channel_id=1, replica_groups=mesh['row'=16,'col'=8] {'row'}, dimensions={0} | all-to-all | bytes 8388608 | tf_op jit(solution)/shard_map/all_to_all | solution.py:262
  229.5 4.7 %fusion.10 = bf16[128,32,128]{2,0,1:T(8,128)(2,1)S(1)} fusion(bf16[16,8,32,512]{3,2,1,0:T(8,128)(2,1)S(1)} %all_to_all.26, bf16[1,512,128]{2,1,0:T(8,128)(2,1)S(1)} %copy-done), kind=kOutput, calls=%fused_computation.53 | convolution fusion | flops 537395200 | bytes 5373952 | tf_op jit(solution)/shard_map/tkq,qf->tkf/dot_general | solution.py:264
  234.3 1.7 copy.98
  (26 shorter events, 1.3 us)
Async XLA Ops:
  0.6 228.9 %copy-start = (bf16[1,512,128]{2,1,0:T(8,128)(2,1)S(1)}, bf16[1,512,128]{2,1,0:T(8,128)(2,1)}, u32[]{:S(2)}) copy-start(bf16[1,512,128]{2,1,0:T(8,128)(2,1)} %param.9) | copy-start | bytes 393220
  0.6 11.3 %copy-start.2 = (bf16[4,256,512]{2,1,0:T(8,128)(2,1)S(1)}, bf16[4,256,512]{2,1,0:T(8,128)(2,1)}, u32[]{:S(2)}) copy-start(bf16[4,256,512]{2,1,0:T(8,128)(2,1)} %param.6) | copy-start | bytes 3145732
  1.5 11.6 %collective-permute-start = (bf16[4,3,512]{2,1,0:T(4,128)(2,1)S(1)}, bf16[4,3,512]{2,1,0:T(4,128)(2,1)S(1)}, u32[]{:S(2)}, u32[]{:S(2)}) collective-permute-start(bf16[4,3,512]{2,1,0:T(4,128)(2,1)S(1)} %slice.82), channel_id=1, source_target_pairs={{8,0},{16,8},{24,16},{32,24},{40,32},{48,40},{56,48},{64,56},{72,6... | collective-permute-start | bytes 36872 | tf_op jit(solution)/shard_map/ppermute | solution.py:17
  16.0 8.6 %copy-start.3 = (s32[2,2]{1,0:T(2,128)S(1)}, s32[2,2]{1,0:T(2,128)}, u32[]{:S(2)}) copy-start(s32[2,2]{1,0:T(2,128)} %param.7) | copy-start | bytes 52
  16.0 14.3 %copy-start.4 = (s32[128,1]{0,1:T(1,128)S(1)}, s32[128,1]{0,1:T(1,128)}, u32[]{:S(2)}) copy-start(s32[128,1]{0,1:T(1,128)} %param.8) | copy-start | bytes 1540
  17.8 23.2 %all-to-all-start = ((bf16[2,4,256,256]{3,1,0,2:T(4,128)(2,1)}), bf16[2,4,256,256]{3,1,0,2:T(4,128)(2,1)S(1)}, u32[]{:S(2)}, u32[]{:S(2)}) async-start(bf16[2,4,256,256]{3,1,0,2:T(4,128)(2,1)} %copy.82), calls=%async_computation | async-start | bytes 2097152 | tf_op jit(solution)/shard_map/all_to_all | solution.py:224
  56.0 27.7 %collective-permute-start.1 = (bf16[2,4,16,8,512]{4,3,2,1,0:T(8,128)(2,1)S(1)}, bf16[2,4,16,8,512]{4,3,2,1,0:T(8,128)(2,1)S(1)}, u32[]{:S(2)}, u32[]{:S(2)}) collective-permute-start(bf16[2,4,16,8,512]{4,3,2,1,0:T(8,128)(2,1)S(1)} %bitcast.84), channel_id=1, source_target_pairs={{0,127},{1,0},{2,1},{3,2},{4,3},{5,4},{6,5},{7,6},{8,7},{9,8},{10,... | collective-permute-start | bytes 3145736 | tf_op jit(solution)/shard_map/ppermute | solution.py:23
  88.1 2.3 copy-start.1

commit v2 on v0

--- a/solution.py
+++ b/solution.py
@@ -24,15 +24,21 @@
 
 
 def channel_coefficients(n_total, channel_ids):
+    coarse_n = 64
     position = jnp.arange(n_total, dtype=jnp.int32)
-    turns = position[:, None] * channel_ids[None, :] % n_total
-    phase_angle = 2.0 * math.pi / n_total * turns.astype(jnp.float32)
-    window = 0.5 - 0.5 * jnp.cos(2.0 * math.pi / n_total * position.astype(jnp.float32))
+    high = jnp.arange(n_total // coarse_n, dtype=jnp.int32) * coarse_n
+    low = jnp.arange(coarse_n, dtype=jnp.int32)
+    step = 2.0 * math.pi / n_total
+    high_angle = step * (high[:, None] * channel_ids[None, :] % n_total).astype(jnp.float32)
+    low_angle = step * (low[:, None] * channel_ids[None, :] % n_total).astype(jnp.float32)
+    high_cos, high_sin = jnp.cos(high_angle)[:, None], jnp.sin(high_angle)[:, None]
+    low_cos, low_sin = jnp.cos(low_angle)[None], jnp.sin(low_angle)[None]
+    cos_part = (high_cos * low_cos - high_sin * low_sin).reshape(n_total, -1)
+    sin_part = (high_sin * low_cos + high_cos * low_sin).reshape(n_total, -1)
+    window = 0.5 - 0.5 * jnp.cos(step * position.astype(jnp.float32))
     gain_factor = math.sqrt(8.0 / (3.0 * n_total))
     weighted = gain_factor * window[:, None]
-    both = jnp.concatenate(
-        [weighted * jnp.cos(phase_angle), weighted * jnp.sin(phase_angle)], axis=1
-    )
+    both = jnp.concatenate([weighted * cos_part, weighted * sin_part], axis=1)
     return both.astype(jnp.bfloat16)
 
 
@@ -124,10 +130,8 @@
     imag_high, imag_low = split(twist_imag)
 
     def mix(table, high, low):
-        return (
-            jnp.dot(mix_ref[table], high, preferred_element_type=f32)
-            + jnp.dot(mix_ref[table], low, preferred_element_type=f32)
-            + jnp.dot(mix_ref[table + 1], high, preferred_element_type=f32)
+        return jnp.dot(mix_ref[table], high, preferred_element_type=f32) + jnp.dot(
+            mix_ref[table], low, preferred_element_type=f32
         )
 
     out_real = mix(0, real_high, real_low) + mix(2, imag_high, imag_low)
@@ -179,7 +183,7 @@
         ],
         compiler_params=pltpu.CompilerParams(vmem_limit_bytes=48 * 1024 * 1024),
         cost_estimate=pl.CostEstimate(
-            flops=blocks * (8 * rows * sub_n * sub_n + 24 * rows * rows * sub_n),
+            flops=blocks * (8 * rows * sub_n * sub_n + 16 * rows * rows * sub_n),
             transcendentals=blocks * rows * sub_n,
             bytes_accessed=blocks * rows * sub_n * 2 * 5 + 4 * sub_n * sub_n,
         ),

time: 184 us -> 183 us (level)
  local copies, waits for them, and re-layouts: 22.6 us -> 27.3 us
  other arithmetic: 21.6 us -> 17.9 us
  Pallas kernels: 20.7 us -> 18.7 us
    another operation x2, other arithmetic: 13.4 us -> 6.48 us
    sub x0 -> x1, local copies, waits for them, and re-layouts: none -> 2.89 us  [channel_coefficients(): cos_part = (high_cos * low_cos - high_sin * low_sin).reshape(n_total, -1)]
    add x0 -> x1, other arithmetic: none -> 2.64 us  [channel_coefficients(): sin_part = (high_sin * low_cos + high_cos * low_sin).reshape(n_total, -1)]
    pallas_call x1, Pallas kernels: 20.7 us -> 18.7 us  [spectrum_call(): pl.pallas_call(spectrum_kernel, grid=(blocks,), in_specs=[pl.BlockSpec((2...]
    add x0 -> x1, local copies, waits for them, and re-layouts: none -> 1.92 us  [channel_coefficients(): sin_part = (high_sin * low_cos + high_cos * low_sin).reshape(n_total, -1)]
where the time goes in v2:
time: 183 us
  blocking collectives  60.7 us (33%)
  local copies, waits for them, and re-layouts  27.3 us (15%)
  waiting for transfers between devices  25.8 us (14%)
  Pallas kernels  18.7 us (10%)
  other arithmetic  17.9 us (10%)
  starting transfers between devices  12.8 us (7%)
  matrix products  10.9 us (6%)
  between operations  8.65 us (5%)
    all_to_all x1, blocking collectives, shards(): lax.all_to_all(outgoing, ('row', 'col'), split_axis=0, concat_axis=0, til...  60.7 us
    pallas_call x1, Pallas kernels, spectrum_call(): pl.pallas_call(spectrum_kernel, grid=(blocks,), in_specs=[pl.BlockSpec((2...  18.7 us
    ppermute x1, waiting for transfers between devices, from_behind_2(): return lax.ppermute(value, axis, pairs)  18 us
    reshape x1, local copies, waits for them, and re-layouts, shards(): swapped.reshape(2, sensors, per_device, sub_n, RADIX)  9.14 us
    all_to_all x1, waiting for transfers between devices, shards(): lax.all_to_all(demod, 'row', split_axis=2, concat_axis=3, tiled=True)  7.78 us
    all_to_all x1, starting transfers between devices, shards(): lax.all_to_all(demod, 'row', split_axis=2, concat_axis=3, tiled=True)  6.76 us
    another operation x2, other arithmetic  6.48 us
    all_to_all x1, local copies, waits for them, and re-layouts, shards(): lax.all_to_all(demod, 'row', split_axis=2, concat_axis=3, tiled=True)  5.9 us
  transfers between devices with their start and end apart: 3, of which 2 were waited for; matrix products, arithmetic and copies ran while one was open for 9% of the time, Pallas kernels for 0%

profile of v2, /device:TPU:0, one launch (start us, length us, event | category | flops | bytes accessed | tf_op | source)
XLA Modules:
  0.0 182.7 jit_solution(1571459212670317688)
XLA Ops:
  0.6 0.8 slice.82
  1.4 1.3 collective-permute-start
  2.8 0.3 fusion.83
  3.3 2.6 %multiply_add_fusion = (f32[32,64,256]{2,1,0:T(8,128)}, f32[32,64,256]{2,1,0:T(8,128)}) fusion(f32[64,256]{1,0:T(8,128)S(1)} %get-tuple-element.47, f32[32,256]{1,0:T(8,128)S(1)} %get-tuple-element.41, f32[64,256]{1,0:T(8,128)S(1)} %get-tuple-element.46, f32[32,256]{1,0:T(8,128)S(1)} %get-tuple-element.40), kind=kLoop, calls=%fused_computation.39 | loop fusion | flops 3145728 | bytes 4390912 | tf_op jit(solution)/shard_map/add | solution.py:37
  6.0 1.9 %copy.64 = f32[2048,256]{0,1:T(8,128)S(1)} copy(f32[2048,256]{1,0:T(8,128)} %bitcast.86) | data formatting | bytes 4194304 | tf_op jit(solution)/shard_map/add | solution.py:37
  7.9 2.9 %copy.63 = f32[2048,256]{0,1:T(8,128)} copy(f32[2048,256]{1,0:T(8,128)} %bitcast.85) | data formatting | bytes 4194304 | tf_op jit(solution)/shard_map/sub | solution.py:36
  10.8 2.2 %multiply_convert_fusion = (bf16[2048,256]{0,1:T(8,128)(2,1)S(1)}, bf16[2048,256]{0,1:T(8,128)(2,1)S(1)}) fusion(f32[2048,256]{0,1:T(8,128)S(1)} %copy.64, f32[2048]{0:T(1024)S(1)} %subtract_multiply_fusion, f32[2048,256]{0,1:T(8,128)} %copy.63), kind=kLoop, calls=%fused_computation.38 | loop fusion | flops 2097152 | bytes 6299648 | tf_op jit(solution)/shard_map/convert.27
  13.0 0.7 fusion.59
  14.1 0.8 fusion.37
  14.9 0.8 fusion.39
  15.6 0.8 add_bitcast_fusion
  16.5 0.4 fusion.44
  17.0 1.8 copy.65
  18.8 6.8 %all-to-all-start = ((bf16[2,4,256,256]{3,1,0,2:T(4,128)(2,1)}), bf16[2,4,256,256]{3,1,0,2:T(4,128)(2,1)S(1)}, u32[]{:S(2)}, u32[]{:S(2)}) async-start(bf16[2,4,256,256]{3,1,0,2:T(4,128)(2,1)} %copy.65), calls=%async_computation | async-start | bytes 2097152 | tf_op jit(solution)/shard_map/all_to_all | solution.py:228
  25.5 0.7 fusion.104
  34.2 7.8 %all-to-all-done = bf16[2,4,256,256]{3,1,0,2:T(4,128)(2,1)S(1)} async-done(((bf16[2,4,256,256]{3,1,0,2:T(4,128)(2,1)}), bf16[2,4,256,256]{3,1,0,2:T(4,128)(2,1)S(1)}, u32[]{:S(2)}, u32[]{:S(2)}) %all-to-all-start) | async-done | bytes 1048608 | tf_op jit(solution)/shard_map/all_to_all | solution.py:228
  42.0 5.9 %copy.66 = bf16[2,4,16,16,256]{3,4,2,1,0:T(8,128)(2,1)} copy(bf16[2,4,16,16,256]{4,1,0,3,2:T(4,128)(2,1)S(1)} %bitcast.89) | data formatting | bytes 2097152 | tf_op jit(solution)/shard_map/all_to_all | solution.py:228
  47.9 9.1 %copy.67 = bf16[2,4,16,512,8]{3,4,2,1,0:T(8,128)(2,1)S(1)} copy(bf16[2,4,16,512,8]{2,4,3,1,0:T(8,128)(2,1)} %bitcast.79) | data formatting | bytes 2097152 | tf_op jit(solution)/shard_map/reshape | solution.py:229
  57.0 4.8 %collective-permute-start.1 = (bf16[2,4,16,8,512]{4,3,2,1,0:T(8,128)(2,1)S(1)}, bf16[2,4,16,8,512]{4,3,2,1,0:T(8,128)(2,1)S(1)}, u32[]{:S(2)}, u32[]{:S(2)}) collective-permute-start(bf16[2,4,16,8,512]{4,3,2,1,0:T(8,128)(2,1)S(1)} %bitcast.81), channel_id=1, source_target_pairs={{0,127},{1,0},{2,1},{3,2},{4,3},{5,4},{6,5},{7,6},{8,7},{9,8},{10,... | collective-permute-start | bytes 3145736 | tf_op jit(solution)/shard_map/ppermute | solution.py:23
  62.2 4.3 %sine_convert_fusion = (bf16[512,512]{1,0:T(8,128)(2,1)S(1)}, bf16[512,512]{1,0:T(8,128)(2,1)S(1)}) fusion(), kind=kLoop, calls=%fused_computation.81 | loop fusion | flops 4194304 | bytes 1048576 | tf_op jit(solution)/shard_map/convert.1
  66.7 18.0 %collective-permute-done.1 = bf16[2,4,16,8,512]{4,3,2,1,0:T(8,128)(2,1)S(1)} collective-permute-done((bf16[2,4,16,8,512]{4,3,2,1,0:T(8,128)(2,1)S(1)}, bf16[2,4,16,8,512]{4,3,2,1,0:T(8,128)(2,1)S(1)}, u32[]{:S(2)}, u32[]{:S(2)}) %collective-permute-start.1) | collective-permute-done | bytes 1048608 | tf_op jit(solution)/shard_map/ppermute | solution.py:23
  84.7 2.3 %fusion.28 = (f32[2,4,16,8,512]{4,3,2,1,0:T(8,128)S(1)}, f32[2,4,16,8,512]{4,3,2,1,0:T(8,128)S(1)}, f32[2,4,16,8,512]{4,3,2,1,0:T(8,128)S(1)}, f32[2,4,16,8,512]{4,3,2,1,0:T(8,128)S(1)}) fusion(s32[]{:T(128)S(6)} %select_n.131, bf16[2,4,16,8,512]{4,3,2,1,0:T(8,128)(2,1)S(1)} %bitcast.82, bf16[2,4,16,8,512]{4,3,2,1,0:T(8,128)(2,1)S(1)} %collective-permute-done.1, ...), kind=kLoop, calls=%fused_computation.68 | loop fusion | flops 4194304 | bytes 10485776 | tf_op jit(solution)/shard_map/convert_element_type | solution.py:241
  87.0 0.7 fusion.53
  87.7 0.8 fusion.52
  88.6 0.3 pad_maximum_fusion.2
  89.1 2.3 %pad_maximum_fusion.prod_ref = bf16[2,16,128,512]{3,2,1,0:T(8,128)(2,1)} fusion(bf16[1,16,128,512]{3,2,1,0:T(8,128)(2,1)S(1)} %bitcast.87, bf16[1,16,128,512]{3,2,1,0:T(8,128)(2,1)S(1)} %bitcast.88), kind=kLoop, calls=%fused_computation | loop fusion | flops 2097152 | bytes 8388608 | tf_op jit(solution)/shard_map/stack | solution.py:244
  91.5 18.7 %shard_map.77 = (bf16[2,4,4,16,4096]{4,3,2,1,0:T(8,128)(2,1)}, bf16[128,16,512]{2,1,0:T(8,128)(2,1)S(1)}) custom-call(bf16[2,16,128,512]{3,2,1,0:T(8,128)(2,1)} %pad_maximum_fusion.prod_ref, bf16[512,1024]{1,0:T(8,128)(2,1)S(1)} %pad_maximum_fusion.4.cos_ref.sin_ref, bf16[512,1024]{1,0:T(8,128)(2,1)S(1)} %pad_maximum_fusion.4.cos_ref.sin_ref, ...), custom_call_target="tpu_custom_call" | custom-call | flops 6442450944 | bytes 11534336 | tf_op jit(solution)/shard_map/pallas_call | solution.py:162
  110.1 3.0 %convolution_convert_fusion = bf16[256,16,512]{2,0,1:T(8,128)(2,1)S(1)} fusion(bf16[128,16,512]{2,1,0:T(8,128)(2,1)S(1)} %get-tuple-element.5, s32[128]{0:T(128)S(1)} %multiply_add_fusion.1), kind=kOutput, calls=%fused_computation.27 | convolution fusion | flops 539000832 | bytes 6291968 | tf_op jit(solution)/shard_map/ot,tkq->okq/dot_general | solution.py:261
  113.2 2.4 %copy.77 = bf16[256,16,512]{2,1,0:T(8,128)(2,1)S(1)} copy(bf16[256,16,512]{2,0,1:T(8,128)(2,1)S(1)} %convolution_convert_fusion) | data formatting | bytes 8388608 | tf_op jit(solution)/shard_map/convert_element_type | solution.py:262
  115.6 60.7 %all_to_all.20 = bf16[128,32,512]{2,1,0:T(8,128)(2,1)S(1)} all-to-all(bf16[128,32,512]{2,1,0:T(8,128)(2,1)S(1)} %bitcast.80), channel_id=1, replica_groups=mesh['row'=16,'col'=8] {'row','col'}, dimensions={0} | all-to-all | bytes 8388608 | tf_op jit(solution)/shard_map/all_to_all | solution.py:263
  176.3 4.7 %fusion.3 = bf16[128,32,128]{2,0,1:T(8,128)(2,1)S(1)} fusion(bf16[128,32,512]{2,1,0:T(8,128)(2,1)S(1)} %all_to_all.20, bf16[1,512,128]{2,1,0:T(8,128)(2,1)S(1)} %copy-done), kind=kOutput, calls=%fused_computation.45 | convolution fusion | flops 537395200 | bytes 5373952 | tf_op jit(solution)/shard_map/tkq,qf->tkf/dot_general | solution.py:264
  181.0 1.7 copy.79
  (29 shorter events, 1.8 us)
Async XLA Ops:
  0.6 175.6 %copy-start = (bf16[1,512,128]{2,1,0:T(8,128)(2,1)S(1)}, bf16[1,512,128]{2,1,0:T(8,128)(2,1)}, u32[]{:S(2)}) copy-start(bf16[1,512,128]{2,1,0:T(8,128)(2,1)} %param.9) | copy-start | bytes 393220
  1.4 12.6 %collective-permute-start = (bf16[4,3,512]{2,1,0:T(4,128)(2,1)S(1)}, bf16[4,3,512]{2,1,0:T(4,128)(2,1)S(1)}, u32[]{:S(2)}, u32[]{:S(2)}) collective-permute-start(bf16[4,3,512]{2,1,0:T(4,128)(2,1)S(1)} %slice.82), channel_id=1, source_target_pairs={{8,0},{16,8},{24,16},{32,24},{40,32},{48,40},{56,48},{64,56},{72,6... | collective-permute-start | bytes 36872 | tf_op jit(solution)/shard_map/ppermute | solution.py:17
  10.8 2.2 %copy-start.2 = (bf16[4,256,512]{2,1,0:T(8,128)(2,1)S(1)}, bf16[4,256,512]{2,1,0:T(8,128)(2,1)}, u32[]{:S(2)}) copy-start(bf16[4,256,512]{2,1,0:T(8,128)(2,1)} %param.6) | copy-start | bytes 3145732
  17.0 8.6 %copy-start.3 = (s32[2,2]{1,0:T(2,128)S(1)}, s32[2,2]{1,0:T(2,128)}, u32[]{:S(2)}) copy-start(s32[2,2]{1,0:T(2,128)} %param.7) | copy-start | bytes 52
  17.0 14.4 %copy-start.4 = (s32[128,1]{0,1:T(1,128)S(1)}, s32[128,1]{0,1:T(1,128)}, u32[]{:S(2)}) copy-start(s32[128,1]{0,1:T(1,128)} %param.8) | copy-start | bytes 1540
  18.8 23.2 %all-to-all-start = ((bf16[2,4,256,256]{3,1,0,2:T(4,128)(2,1)}), bf16[2,4,256,256]{3,1,0,2:T(4,128)(2,1)S(1)}, u32[]{:S(2)}, u32[]{:S(2)}) async-start(bf16[2,4,256,256]{3,1,0,2:T(4,128)(2,1)} %copy.65), calls=%async_computation | async-start | bytes 2097152 | tf_op jit(solution)/shard_map/all_to_all | solution.py:228
  57.0 27.7 %collective-permute-start.1 = (bf16[2,4,16,8,512]{4,3,2,1,0:T(8,128)(2,1)S(1)}, bf16[2,4,16,8,512]{4,3,2,1,0:T(8,128)(2,1)S(1)}, u32[]{:S(2)}, u32[]{:S(2)}) collective-permute-start(bf16[2,4,16,8,512]{4,3,2,1,0:T(8,128)(2,1)S(1)} %bitcast.81), channel_id=1, source_target_pairs={{0,127},{1,0},{2,1},{3,2},{4,3},{5,4},{6,5},{7,6},{8,7},{9,8},{10,... | collective-permute-start | bytes 3145736 | tf_op jit(solution)/shard_map/ppermute | solution.py:23
  89.1 2.3 %copy-start.1 = (bf16[4,128,128]{2,1,0:T(8,128)(2,1)S(1)}, bf16[4,128,128]{2,1,0:T(8,128)(2,1)}, u32[]{:S(2)}) copy-start(bf16[4,128,128]{2,1,0:T(8,128)(2,1)} %constant.177.mix_ref) | copy-start | bytes 393220

commit v3 on v2

--- a/solution.py
+++ b/solution.py
@@ -24,21 +24,21 @@
 
 
 def channel_coefficients(n_total, channel_ids):
-    coarse_n = 64
+    lanes = 128
     position = jnp.arange(n_total, dtype=jnp.int32)
-    high = jnp.arange(n_total // coarse_n, dtype=jnp.int32) * coarse_n
-    low = jnp.arange(coarse_n, dtype=jnp.int32)
+    high = jnp.arange(n_total // lanes, dtype=jnp.int32) * lanes
+    low = jnp.arange(lanes, dtype=jnp.int32)
     step = 2.0 * math.pi / n_total
-    high_angle = step * (high[:, None] * channel_ids[None, :] % n_total).astype(jnp.float32)
-    low_angle = step * (low[:, None] * channel_ids[None, :] % n_total).astype(jnp.float32)
-    high_cos, high_sin = jnp.cos(high_angle)[:, None], jnp.sin(high_angle)[:, None]
-    low_cos, low_sin = jnp.cos(low_angle)[None], jnp.sin(low_angle)[None]
-    cos_part = (high_cos * low_cos - high_sin * low_sin).reshape(n_total, -1)
-    sin_part = (high_sin * low_cos + high_cos * low_sin).reshape(n_total, -1)
+    high_angle = step * (channel_ids[:, None] * high[None, :] % n_total).astype(jnp.float32)
+    low_angle = step * (channel_ids[:, None] * low[None, :] % n_total).astype(jnp.float32)
+    high_cos, high_sin = jnp.cos(high_angle)[:, :, None], jnp.sin(high_angle)[:, :, None]
+    low_cos, low_sin = jnp.cos(low_angle)[:, None], jnp.sin(low_angle)[:, None]
+    cos_part = (high_cos * low_cos - high_sin * low_sin).reshape(-1, n_total)
+    sin_part = (high_sin * low_cos + high_cos * low_sin).reshape(-1, n_total)
     window = 0.5 - 0.5 * jnp.cos(step * position.astype(jnp.float32))
     gain_factor = math.sqrt(8.0 / (3.0 * n_total))
-    weighted = gain_factor * window[:, None]
-    both = jnp.concatenate([weighted * cos_part, weighted * sin_part], axis=1)
+    weighted = gain_factor * window[None, :]
+    both = jnp.concatenate([weighted * cos_part, weighted * sin_part], axis=0)
     return both.astype(jnp.bfloat16)
 
 
@@ -105,49 +105,60 @@
     return jnp.stack(mixers)
 
 
-def spectrum_kernel(prod_ref, cos_ref, sin_ref, twc_ref, tws_ref, mix_ref, spec_ref, tile_ref):
-    f32 = jnp.float32
-    prod_real = prod_ref[0, 0]
-    prod_imag = prod_ref[1, 0]
-    sub_cos = cos_ref[...]
-    sub_sin = sin_ref[...]
-    first_real = jnp.dot(prod_real, sub_cos, preferred_element_type=f32) + jnp.dot(
-        prod_imag, sub_sin, preferred_element_type=f32
-    )
-    first_imag = jnp.dot(prod_imag, sub_cos, preferred_element_type=f32) - jnp.dot(
-        prod_real, sub_sin, preferred_element_type=f32
-    )
-    twist_cos = twc_ref[...]
-    twist_sin = tws_ref[...]
-    twist_real = first_real * twist_cos + first_imag * twist_sin
-    twist_imag = first_imag * twist_cos - first_real * twist_sin
-
-    def split(value):
-        high = value.astype(jnp.bfloat16)
-        return high, (value - high.astype(f32)).astype(jnp.bfloat16)
-
-    real_high, real_low = split(twist_real)
-    imag_high, imag_low = split(twist_imag)
-
-    def mix(table, high, low):
-        return jnp.dot(mix_ref[table], high, preferred_element_type=f32) + jnp.dot(
-            mix_ref[table], low, preferred_element_type=f32
+def spectrum_kernel(
+    dest_ref, prod_ref, cos_ref, sin_ref, twc_ref, tws_ref, mix_ref, zero_ref, spec_ref, out_ref,
+    feat_scratch,
+):
+    del dest_ref, zero_ref
+    rows_per = out_ref.shape[1]
+    sub_n = out_ref.shape[2]
+
+    @pl.when(pl.program_id(1) == 0)
+    def _():
+        f32 = jnp.float32
+        prod_real = prod_ref[0, 0]
+        prod_imag = prod_ref[1, 0]
+        sub_cos = cos_ref[...]
+        sub_sin = sin_ref[...]
+        first_real = jnp.dot(prod_real, sub_cos, preferred_element_type=f32) + jnp.dot(
+            prod_imag, sub_sin, preferred_element_type=f32
         )
-
-    out_real = mix(0, real_high, real_low) + mix(2, imag_high, imag_low)
-    out_imag = mix(0, imag_high, imag_low) - mix(2, real_high, real_low)
-    feature = jnp.log1p(out_real * out_real + out_imag * out_imag)
-    rows_per = tile_ref.shape[1]
-    sub_n = tile_ref.shape[2]
-    for d in range(tile_ref.shape[0]):
-        rows = slice(d * rows_per, (d + 1) * rows_per)
-        lanes = slice(d * sub_n, (d + 1) * sub_n)
-        spec_ref[0, 0, 0, :, lanes] = out_real[rows].astype(spec_ref.dtype)
-        spec_ref[1, 0, 0, :, lanes] = out_imag[rows].astype(spec_ref.dtype)
-        tile_ref[d] = feature[rows].astype(tile_ref.dtype)
-
-
-def spectrum_call(products, table_sub, hops_total):
+        first_imag = jnp.dot(prod_imag, sub_cos, preferred_element_type=f32) - jnp.dot(
+            prod_real, sub_sin, preferred_element_type=f32
+        )
+        twist_cos = twc_ref[...]
+        twist_sin = tws_ref[...]
+        twist_real = first_real * twist_cos + first_imag * twist_sin
+        twist_imag = first_imag * twist_cos - first_real * twist_sin
+
+        def split(value):
+            high = value.astype(jnp.bfloat16)
+            return high, (value - high.astype(f32)).astype(jnp.bfloat16)
+
+        real_high, real_low = split(twist_real)
+        imag_high, imag_low = split(twist_imag)
+
+        def mix(table, high, low):
+            return jnp.dot(mix_ref[table], high, preferred_element_type=f32) + jnp.dot(
+                mix_ref[table], low, preferred_element_type=f32
+            )
+
+        out_real = mix(0, real_high, real_low) + mix(2, imag_high, imag_low)
+        out_imag = mix(0, imag_high, imag_low) - mix(2, real_high, real_low)
+        feat_scratch[...] = jnp.log1p(out_real * out_real + out_imag * out_imag).astype(
+            feat_scratch.dtype
+        )
+        for d in range(RADIX):
+            rows = slice(d * rows_per, (d + 1) * rows_per)
+            lanes = slice(d * sub_n, (d + 1) * sub_n)
+            spec_ref[0, 0, 0, :, lanes] = out_real[rows].astype(spec_ref.dtype)
+            spec_ref[1, 0, 0, :, lanes] = out_imag[rows].astype(spec_ref.dtype)
+
+    start = pl.multiple_of(pl.program_id(1) * rows_per, rows_per)
+    out_ref[0] = feat_scratch[pl.ds(start, rows_per), :]
+
+
+def spectrum_call(products, table_sub, hops_total, dest, slots):
     _, sensors, combos, rows, sub_n = products.shape
     per_device = rows // RADIX
     blocks = sensors * combos
@@ -159,36 +170,47 @@
     twist_cos = jnp.tile(norm_factor * jnp.cos(twist_angle), (per_device, 1))
     twist_sin = jnp.tile(norm_factor * jnp.sin(twist_angle), (per_device, 1))
     mixers = section_mixers(RADIX, per_device)
-    spectrum, tiles = pl.pallas_call(
-        spectrum_kernel,
-        grid=(blocks,),
+    zeros = jnp.zeros((slots, per_device, sub_n), jnp.bfloat16)
+    grid_spec = pltpu.PrefetchScalarGridSpec(
+        num_scalar_prefetch=1,
+        grid=(blocks, RADIX),
         in_specs=[
-            pl.BlockSpec((2, 1, rows, sub_n), lambda i: (0, i, 0, 0)),
-            pl.BlockSpec((sub_n, sub_n), lambda i: (0, 0)),
-            pl.BlockSpec((sub_n, sub_n), lambda i: (0, 1)),
-            pl.BlockSpec((rows, sub_n), lambda i: (0, 0)),
-            pl.BlockSpec((rows, sub_n), lambda i: (0, 0)),
-            pl.BlockSpec((4, rows, rows), lambda i: (0, 0, 0)),
+            pl.BlockSpec((2, 1, rows, sub_n), lambda i, d, dest: (0, i, 0, 0)),
+            pl.BlockSpec((sub_n, sub_n), lambda i, d, dest: (0, 0)),
+            pl.BlockSpec((sub_n, sub_n), lambda i, d, dest: (0, 1)),
+            pl.BlockSpec((rows, sub_n), lambda i, d, dest: (0, 0)),
+            pl.BlockSpec((rows, sub_n), lambda i, d, dest: (0, 0)),
+            pl.BlockSpec((4, rows, rows), lambda i, d, dest: (0, 0, 0)),
+            pl.BlockSpec(memory_space=pl.ANY),
         ],
         out_specs=[
             pl.BlockSpec(
                 (2, 1, 1, per_device, RADIX * sub_n),
-                lambda i: (0, i // combos, i % combos, 0, 0),
+                lambda i, d, dest: (0, i // combos, i % combos, 0, 0),
             ),
-            pl.BlockSpec((RADIX, per_device, sub_n), lambda i: (i, 0, 0)),
+            pl.BlockSpec((1, per_device, sub_n), lambda i, d, dest: (dest[i * RADIX + d], 0, 0)),
         ],
+        scratch_shapes=[pltpu.VMEM((rows, sub_n), jnp.bfloat16)],
+    )
+    spectrum, outgoing = pl.pallas_call(
+        spectrum_kernel,
+        grid_spec=grid_spec,
         out_shape=[
             jax.ShapeDtypeStruct((2, sensors, combos, per_device, RADIX * sub_n), jnp.bfloat16),
-            jax.ShapeDtypeStruct((blocks * RADIX, per_device, sub_n), jnp.bfloat16),
+            jax.ShapeDtypeStruct((slots, per_device, sub_n), jnp.bfloat16),
         ],
-        compiler_params=pltpu.CompilerParams(vmem_limit_bytes=48 * 1024 * 1024),
+        input_output_aliases={7: 1},
+        compiler_params=pltpu.CompilerParams(
+            vmem_limit_bytes=48 * 1024 * 1024,
+            dimension_semantics=("arbitrary", "arbitrary"),
+        ),
         cost_estimate=pl.CostEstimate(
             flops=blocks * (8 * rows * sub_n * sub_n + 16 * rows * rows * sub_n),
             transcendentals=blocks * rows * sub_n,
             bytes_accessed=blocks * rows * sub_n * 2 * 5 + 4 * sub_n * sub_n,
         ),
-    )(flat, table_sub, table_sub, twist_cos, twist_sin, mixers)
-    return spectrum, tiles
+    )(dest, flat, table_sub, table_sub, twist_cos, twist_sin, mixers, zeros)
+    return spectrum, outgoing
 
 
 def shards(frames, orders, owners, templates):
@@ -215,9 +237,9 @@
     summed = jnp.zeros((sensors, 2 * local_channels, hop_dev), jnp.float32)
     for quarter in range(4):
         summed = summed + jnp.einsum(
-            "shf,fk->skh",
+            "shf,kf->skh",
             padded[:, quarter : quarter + hop_dev],
-            coefficients[quarter * frame_len : (quarter + 1) * frame_len],
+            coefficients[:, quarter * frame_len : (quarter + 1) * frame_len],
             preferred_element_type=jnp.float32,
         )
     hop_ids = row_at * hop_dev + jnp.arange(hop_dev, dtype=jnp.int32)
@@ -225,8 +247,12 @@
         summed[:, :local_channels], summed[:, local_channels:], channel_ids, hop_ids
     )
     demod = jnp.stack([real_part, imag_part]).astype(jnp.bfloat16)
-    swapped = lax.all_to_all(demod, "row", split_axis=2, concat_axis=3, tiled=True)
-    ordered = swapped.reshape(2, sensors, per_device, sub_n, RADIX).transpose(0, 1, 2, 4, 3)
+    demod = demod.reshape(2, sensors, rows_count, per_device, hop_dev).transpose(2, 0, 1, 3, 4)
+    swapped = lax.all_to_all(demod, "row", split_axis=0, concat_axis=0, tiled=True)
+    ordered = swapped.reshape(
+        rows_count, 2, sensors, per_device, hop_dev // RADIX, RADIX
+    ).transpose(1, 2, 3, 5, 0, 4)
+    ordered = ordered.reshape(2, sensors, per_device, RADIX, sub_n)
     above = from_behind_2(ordered, ("row", "col"), -1)
     extended = jnp.concatenate([ordered, above], axis=2)
     own_real = ordered[0].astype(jnp.float32)
@@ -244,10 +270,6 @@
     products = jnp.stack([jnp.stack(prod_real, axis=1), jnp.stack(prod_imag, axis=1)]).astype(
         jnp.bfloat16
     )
-    table_sub = sub_coefficients(sub_n)
-    spectrum, tiles = spectrum_call(
-        products.reshape(2, sensors, combos, per_device * RADIX, sub_n), table_sub, hops_n
-    )
     tiles_dev = sensors * combos * RADIX
     capacity = max(2, 2 * tiles_dev // devices_n)
     owner_ids = owners[:, 0]
@@ -256,13 +278,18 @@
     before = jnp.cumsum(one_hot, axis=0) - one_hot
     slot_ids = jnp.sum(before * one_hot, axis=1)
     places = owner_ids * capacity + slot_ids
-    slot_range = jnp.arange(devices_n * capacity, dtype=jnp.int32)
-    placing = (places[None, :] == slot_range[:, None]).astype(jnp.bfloat16)
-    outgoing = jnp.einsum("ot,tkq->okq", placing, tiles, preferred_element_type=jnp.float32)
-    outgoing = outgoing.astype(jnp.bfloat16).reshape(devices_n, capacity * per_device, sub_n)
+    table_sub = sub_coefficients(sub_n)
+    spectrum, outgoing = spectrum_call(
+        products.reshape(2, sensors, combos, per_device * RADIX, sub_n),
+        table_sub,
+        hops_n,
+        places,
+        devices_n * capacity,
+    )
+    outgoing = outgoing.reshape(devices_n, capacity * per_device, sub_n)
     arrived = lax.all_to_all(outgoing, ("row", "col"), split_axis=0, concat_axis=0, tiled=True)
-    found = jnp.einsum(
-        "tkq,qf->tkf", arrived, templates[0], preferred_element_type=jnp.float32
+    found = jnp.dot(
+        arrived.reshape(-1, sub_n), templates[0], preferred_element_type=jnp.float32
     ).astype(jnp.bfloat16)
     found = found.reshape(devices_n, capacity, per_device, feat_n)
     return (spectrum, found[None])

time: 183 us -> 203 us (1.11)
  Pallas kernels: 18.7 us -> 42.3 us
  waiting for transfers between devices: 25.8 us -> 10.9 us
  local copies, waits for them, and re-layouts: 27.3 us -> 38.5 us
  matrix products: 10.9 us -> 5.34 us
  other arithmetic: 17.9 us -> 22.5 us
    pallas_call x1, Pallas kernels: 18.7 us -> 42.3 us  [spectrum_call(): pl.pallas_call(spectrum_kernel, grid_spec=grid_spec, out_shape=[jax.Shape...]
    ppermute x1, waiting for transfers between devices: 18 us -> 7.94 us  [from_behind_2(): return lax.ppermute(value, axis, pairs)]
    reshape x1 -> x2, local copies, waits for them, and re-layouts: 9.14 us -> 18.9 us  [the longest x1 12.2 us: shards(): swapped.reshape(rows_count, 2, sensors, per_device, hop_dev // RADIX, RADIX)]
    convert_element_type x0 -> x1, other arithmetic: none -> 6.56 us  [shards(): own_imag = ordered[1].astype(jnp.float32)]
    convert_element_type x1 -> x2, local copies, waits for them, and re-layouts: 2.4 us -> 7.94 us  [the longest x1 4.39 us: shards(): own_real = ordered[0].astype(jnp.float32)]
    dot_general x6 -> x5, matrix products: 10.9 us -> 5.34 us  [the longest x4 3.11 us: shards(): jnp.einsum('shf,kf->skh', padded[:, quarter:quarter + hop_dev], coefficie...]
    all_to_all x1, waiting for transfers between devices: 7.78 us -> 2.91 us  [shards(): lax.all_to_all(demod, 'row', split_axis=0, concat_axis=0, tiled=True)]
    add x3 -> x1, other arithmetic: 4.16 us -> 1.25 us  [channel_coefficients(): sin_part = (high_sin * low_cos + high_cos * low_sin).reshape(-1, n_total)]
  transfers between devices with their start and end apart: 3 -> 3, of which waited for: 2 -> 2; matrix products, arithmetic and copies ran while one was open for 9% -> 13% of each run, Pallas kernels for 0% -> 0%
where the time goes in v3:
time: 203 us; the launch traced here: 201 us
  blocking collectives  60 us (30%)
  Pallas kernels  42.3 us (21%)
  local copies, waits for them, and re-layouts  38.5 us (19%)
  other arithmetic  22.5 us (11%)
  starting transfers between devices  13.2 us (7%)
  waiting for transfers between devices  10.9 us (5%)
  between operations  8.72 us (4%)
  matrix products  5.34 us (3%)
    all_to_all x1, blocking collectives, shards(): lax.all_to_all(outgoing, ('row', 'col'), split_axis=0, concat_axis=0, til...  60 us
    pallas_call x1, Pallas kernels, spectrum_call(): pl.pallas_call(spectrum_kernel, grid_spec=grid_spec, out_shape=[jax.Shape...  42.3 us
    reshape x1, local copies, waits for them, and re-layouts, shards(): swapped.reshape(rows_count, 2, sensors, per_device, hop_dev // RADIX, RADIX)  12.2 us
    ppermute x1, waiting for transfers between devices, from_behind_2(): return lax.ppermute(value, axis, pairs)  7.94 us
    another operation x4, other arithmetic  7.72 us
    reshape x1, local copies, waits for them, and re-layouts, shards(): ordered = ordered.reshape(2, sensors, per_device, RADIX, sub_n)  6.77 us
    all_to_all x1, starting transfers between devices, shards(): lax.all_to_all(demod, 'row', split_axis=0, concat_axis=0, tiled=True)  6.76 us
    convert_element_type x1, other arithmetic, shards(): own_imag = ordered[1].astype(jnp.float32)  6.56 us
  transfers between devices with their start and end apart: 3, of which 2 were waited for; matrix products, arithmetic and copies ran while one was open for 13% of the time, Pallas kernels for 0%

profile of v3, /device:TPU:0, one launch (start us, length us, event | category | flops | bytes accessed | tf_op | source)
XLA Modules:
  0.0 201.4 jit_solution(6291935547524459127)
XLA Ops:
  0.6 0.8 slice.84
  1.4 1.3 collective-permute-start
  2.8 0.6 fusion.38
  3.8 1.2 multiply_add_fusion
  5.1 1.3 fusion
  6.4 0.7 fusion.21
  7.5 0.8 fusion.9
  8.3 0.8 fusion.11
  9.0 0.8 add_bitcast_fusion
  9.9 0.4 subtract_convert_fusion.5
  10.3 1.1 copy_bitcast_fusion
  11.4 6.8 %all-to-all-start = ((bf16[16,2,4,16,256]{4,3,2,1,0:T(8,128)(2,1)}), bf16[16,2,4,16,256]{4,3,2,1,0:T(8,128)(2,1)S(1)}, u32[]{:S(2)}, u32[]{:S(2)}) async-start(bf16[16,2,4,16,256]{4,3,2,1,0:T(8,128)(2,1)} %copy_bitcast_fusion), calls=%async_computation | async-start | bytes 2097152 | tf_op jit(solution)/shard_map/all_to_all | solution.py:251
  18.2 0.7 fusion.63
  27.3 4.3 %sine_convert_fusion = (bf16[512,512]{1,0:T(8,128)(2,1)S(1)}, bf16[512,512]{1,0:T(8,128)(2,1)S(1)}) fusion(), kind=kLoop, calls=%fused_computation.42 | loop fusion | flops 4194304 | bytes 1048576 | tf_op jit(solution)/shard_map/convert.3
  31.7 2.9 %all-to-all-done = bf16[16,2,4,16,256]{4,3,2,1,0:T(8,128)(2,1)S(1)} async-done(((bf16[16,2,4,16,256]{4,3,2,1,0:T(8,128)(2,1)}), bf16[16,2,4,16,256]{4,3,2,1,0:T(8,128)(2,1)S(1)}, u32[]{:S(2)}, u32[]{:S(2)}) %all-to-all-start) | async-done | bytes 1048608 | tf_op jit(solution)/shard_map/all_to_all | solution.py:251
  34.6 5.8 %copy.53 = bf16[16,2,4,16,256]{3,4,2,1,0:T(8,128)(2,1)} copy(bf16[16,2,4,16,256]{4,3,2,1,0:T(8,128)(2,1)S(1)} %all-to-all-done) | data formatting | bytes 2097152 | tf_op jit(solution)/shard_map/all_to_all | solution.py:251
  40.5 12.2 %copy.54 = bf16[16,2,4,16,32,8]{4,0,5,3,2,1:T(8,128)(2,1)} copy(bf16[16,2,4,16,32,8]{3,5,4,2,1,0:T(8,128)(2,1)} %bitcast.107) | data formatting | bytes 2097152 | tf_op jit(solution)/shard_map/reshape | solution.py:252
  52.6 6.8 %reshape.625 = bf16[2,4,16,8,512]{4,3,2,1,0:T(8,128)(2,1)} reshape(bf16[2,4,16,8,16,32]{5,4,3,2,1,0:T(8,128)(2,1)} %bitcast.105) | data formatting | bytes 2097152 | tf_op jit(solution)/shard_map/reshape | solution.py:255
  59.4 5.2 %collective-permute-start.1 = (bf16[2,4,16,8,512]{4,3,2,1,0:T(8,128)(2,1)}, bf16[2,4,16,8,512]{4,3,2,1,0:T(8,128)(2,1)}, u32[]{:S(2)}, u32[]{:S(2)}) collective-permute-start(bf16[2,4,16,8,512]{4,3,2,1,0:T(8,128)(2,1)} %reshape.625), channel_id=1, source_target_pairs={{0,127},{1,0},{2,1},{3,2},{4,3},{5,4},{6,5},{7,6},{8,7},{9,8},{10,... | collective-permute-start | bytes 3145736 | tf_op jit(solution)/shard_map/ppermute | solution.py:23
  64.7 6.6 %slice_convert_fusion = (f32[1,4,16,8,16,32]{5,4,3,2,1,0:T(8,128)}, f32[1,4,16,8,16,32]{5,4,3,2,1,0:T(8,128)}) fusion(bf16[2,4,16,8,16,32]{5,4,3,2,1,0:T(8,128)(2,1)} %bitcast.106), kind=kLoop, calls=%fused_computation.12 | loop fusion | flops 524288 | bytes 3145728 | tf_op jit(solution)/shard_map/convert_element_type | solution.py:259
  71.2 3.5 %reshape.629 = f32[4,1,16,8,512]{4,3,2,0,1:T(8,128)S(1)} reshape(f32[1,4,16,8,16,32]{5,4,3,2,1,0:T(8,128)} %get-tuple-element.14) | data formatting | bytes 2097152 | tf_op jit(solution)/shard_map/convert_element_type | solution.py:259
  74.8 4.4 %reshape.628 = f32[4,1,16,8,512]{4,3,2,0,1:T(8,128)} reshape(f32[1,4,16,8,16,32]{5,4,3,2,1,0:T(8,128)} %get-tuple-element.15) | data formatting | bytes 2097152 | tf_op jit(solution)/shard_map/convert_element_type | solution.py:258
  79.2 1.3 constant_dynamic-update-slice_fusion.3
  80.5 7.9 %collective-permute-done.1 = bf16[2,4,16,8,512]{4,3,2,1,0:T(8,128)(2,1)} collective-permute-done((bf16[2,4,16,8,512]{4,3,2,1,0:T(8,128)(2,1)}, bf16[2,4,16,8,512]{4,3,2,1,0:T(8,128)(2,1)}, u32[]{:S(2)}, u32[]{:S(2)}) %collective-permute-start.1) | collective-permute-done | bytes 1048608 | tf_op jit(solution)/shard_map/ppermute | solution.py:23
  88.4 1.3 constant_dynamic-update-slice_fusion.2
  89.8 1.2 dynamic-slice_convert_fusion.3
  91.0 1.7 add_convert_fusion.3
  93.7 2.3 %pad_maximum_fusion.prod_ref = bf16[2,16,128,512]{3,2,1,0:T(8,128)(2,1)} fusion(bf16[1,16,128,512]{3,2,1,0:T(8,128)(2,1)S(1)} %bitcast.111, bf16[1,16,128,512]{3,2,1,0:T(8,128)(2,1)S(1)} %bitcast.112), kind=kLoop, calls=%fused_computation.1 | loop fusion | flops 2097152 | bytes 8388608 | tf_op jit(solution)/shard_map/stack | solution.py:270
  96.0 0.5 broadcast_in_dim.2.zero_ref
  96.9 42.3 %shard_map.77 = (bf16[2,4,4,16,4096]{4,3,2,1,0:T(8,128)(2,1)}, bf16[256,16,512]{2,1,0:T(8,128)(2,1)S(1)}) custom-call(s32[128]{0:T(128)S(1)} %multiply_add_fusion.1.dest_ref, bf16[2,16,128,512]{3,2,1,0:T(8,128)(2,1)} %pad_maximum_fusion.prod_ref, bf16[512,1024]{1,0:T(8,128)(2,1)S(1)} %pad_maximum_fusion.4.cos_ref.sin_ref, ...), custom_call_target="tpu_custom_call", output_to_operand_aliasing={{1}: (7, {})} | custom-call | flops 6442450944 | bytes 11534336 | tf_op jit(solution)/shard_map/pallas_call | solution.py:195
  139.2 60.0 %all_to_all.10 = bf16[128,32,512]{2,1,0:T(8,128)(2,1)S(1)} all-to-all(bf16[128,32,512]{2,1,0:T(8,128)(2,1)S(1)} %bitcast.104), channel_id=1, replica_groups=mesh['row'=16,'col'=8] {'row','col'}, dimensions={0} | all-to-all | bytes 8388608 | tf_op jit(solution)/shard_map/all_to_all | solution.py:290
  199.2 2.2 %convolution_convert_fusion = bf16[4096,128]{1,0:T(8,128)(2,1)} fusion(bf16[4096,512]{1,0:T(8,128)(2,1)S(1)} %bitcast.108, bf16[1,512,128]{2,1,0:T(8,128)(2,1)S(1)} %copy-done), kind=kOutput, calls=%fused_computation | convolution fusion | flops 537395200 | bytes 5373952 | tf_op jit(solution)/shard_map/dot_general | solution.py:291
  (35 shorter events, 2.9 us)
Async XLA Ops:
  0.6 198.6 %copy-start = (bf16[1,512,128]{2,1,0:T(8,128)(2,1)S(1)}, bf16[1,512,128]{2,1,0:T(8,128)(2,1)}, u32[]{:S(2)}) copy-start(bf16[1,512,128]{2,1,0:T(8,128)(2,1)} %param.9) | copy-start | bytes 393220
  1.4 6.0 %collective-permute-start = (bf16[4,3,512]{2,1,0:T(4,128)(2,1)S(1)}, bf16[4,3,512]{2,1,0:T(4,128)(2,1)S(1)}, u32[]{:S(2)}, u32[]{:S(2)}) collective-permute-start(bf16[4,3,512]{2,1,0:T(4,128)(2,1)S(1)} %slice.84), channel_id=1, source_target_pairs={{8,0},{16,8},{24,16},{32,24},{40,32},{48,40},{56,48},{64,56},{72,6... | collective-permute-start | bytes 36872 | tf_op jit(solution)/shard_map/ppermute | solution.py:17
  5.1 1.3 copy-start.2
  10.3 7.9 %copy-start.4 = (s32[2,2]{1,0:T(2,128)S(1)}, s32[2,2]{1,0:T(2,128)}, u32[]{:S(2)}) copy-start(s32[2,2]{1,0:T(2,128)} %param.7) | copy-start | bytes 52
  10.3 13.7 %copy-start.5 = (s32[128,1]{0,1:T(1,128)S(1)}, s32[128,1]{0,1:T(1,128)}, u32[]{:S(2)}) copy-start(s32[128,1]{0,1:T(1,128)} %param.8) | copy-start | bytes 1540
  11.4 23.2 %all-to-all-start = ((bf16[16,2,4,16,256]{4,3,2,1,0:T(8,128)(2,1)}), bf16[16,2,4,16,256]{4,3,2,1,0:T(8,128)(2,1)S(1)}, u32[]{:S(2)}, u32[]{:S(2)}) async-start(bf16[16,2,4,16,256]{4,3,2,1,0:T(8,128)(2,1)} %copy_bitcast_fusion), calls=%async_computation | async-start | bytes 2097152 | tf_op jit(solution)/shard_map/all_to_all | solution.py:251
  59.4 29.0 %collective-permute-start.1 = (bf16[2,4,16,8,512]{4,3,2,1,0:T(8,128)(2,1)}, bf16[2,4,16,8,512]{4,3,2,1,0:T(8,128)(2,1)}, u32[]{:S(2)}, u32[]{:S(2)}) collective-permute-start(bf16[2,4,16,8,512]{4,3,2,1,0:T(8,128)(2,1)} %reshape.625), channel_id=1, source_target_pairs={{0,127},{1,0},{2,1},{3,2},{4,3},{5,4},{6,5},{7,6},{8,7},{9,8},{10,... | collective-permute-start | bytes 3145736 | tf_op jit(solution)/shard_map/ppermute | solution.py:23
  89.8 1.2 copy-start.3
  96.0 0.9 copy-start.1

commit v4 on v2

--- a/solution.py
+++ b/solution.py
@@ -24,21 +24,21 @@
 
 
 def channel_coefficients(n_total, channel_ids):
-    coarse_n = 64
+    lanes = 128
     position = jnp.arange(n_total, dtype=jnp.int32)
-    high = jnp.arange(n_total // coarse_n, dtype=jnp.int32) * coarse_n
-    low = jnp.arange(coarse_n, dtype=jnp.int32)
+    high = jnp.arange(n_total // lanes, dtype=jnp.int32) * lanes
+    low = jnp.arange(lanes, dtype=jnp.int32)
     step = 2.0 * math.pi / n_total
-    high_angle = step * (high[:, None] * channel_ids[None, :] % n_total).astype(jnp.float32)
-    low_angle = step * (low[:, None] * channel_ids[None, :] % n_total).astype(jnp.float32)
-    high_cos, high_sin = jnp.cos(high_angle)[:, None], jnp.sin(high_angle)[:, None]
-    low_cos, low_sin = jnp.cos(low_angle)[None], jnp.sin(low_angle)[None]
-    cos_part = (high_cos * low_cos - high_sin * low_sin).reshape(n_total, -1)
-    sin_part = (high_sin * low_cos + high_cos * low_sin).reshape(n_total, -1)
+    high_angle = step * (channel_ids[:, None] * high[None, :] % n_total).astype(jnp.float32)
+    low_angle = step * (channel_ids[:, None] * low[None, :] % n_total).astype(jnp.float32)
+    high_cos, high_sin = jnp.cos(high_angle)[:, :, None], jnp.sin(high_angle)[:, :, None]
+    low_cos, low_sin = jnp.cos(low_angle)[:, None], jnp.sin(low_angle)[:, None]
+    cos_part = (high_cos * low_cos - high_sin * low_sin).reshape(-1, n_total)
+    sin_part = (high_sin * low_cos + high_cos * low_sin).reshape(-1, n_total)
     window = 0.5 - 0.5 * jnp.cos(step * position.astype(jnp.float32))
     gain_factor = math.sqrt(8.0 / (3.0 * n_total))
-    weighted = gain_factor * window[:, None]
-    both = jnp.concatenate([weighted * cos_part, weighted * sin_part], axis=1)
+    weighted = gain_factor * window[None, :]
+    both = jnp.concatenate([weighted * cos_part, weighted * sin_part], axis=0)
     return both.astype(jnp.bfloat16)
 
 
@@ -105,8 +105,15 @@
     return jnp.stack(mixers)
 
 
-def spectrum_kernel(prod_ref, cos_ref, sin_ref, twc_ref, tws_ref, mix_ref, spec_ref, tile_ref):
+def spectrum_kernel(
+    dest_ref, prod_ref, cos_ref, sin_ref, twc_ref, tws_ref, mix_ref, zero_ref, spec_ref, out_ref,
+    feat_scratch, sems,
+):
+    del zero_ref
     f32 = jnp.float32
+    block = pl.program_id(0)
+    rows_per = feat_scratch.shape[1]
+    sub_n = feat_scratch.shape[2]
     prod_real = prod_ref[0, 0]
     prod_imag = prod_ref[1, 0]
     sub_cos = cos_ref[...]
@@ -136,18 +143,35 @@
 
     out_real = mix(0, real_high, real_low) + mix(2, imag_high, imag_low)
     out_imag = mix(0, imag_high, imag_low) - mix(2, real_high, real_low)
-    feature = jnp.log1p(out_real * out_real + out_imag * out_imag)
-    rows_per = tile_ref.shape[1]
-    sub_n = tile_ref.shape[2]
-    for d in range(tile_ref.shape[0]):
+    feature = jnp.log1p(out_real * out_real + out_imag * out_imag).astype(feat_scratch.dtype)
+    for d in range(RADIX):
         rows = slice(d * rows_per, (d + 1) * rows_per)
         lanes = slice(d * sub_n, (d + 1) * sub_n)
         spec_ref[0, 0, 0, :, lanes] = out_real[rows].astype(spec_ref.dtype)
         spec_ref[1, 0, 0, :, lanes] = out_imag[rows].astype(spec_ref.dtype)
-        tile_ref[d] = feature[rows].astype(tile_ref.dtype)
-
-
-def spectrum_call(products, table_sub, hops_total):
+
+    def tile_copy(step, d):
+        return pltpu.make_async_copy(
+            feat_scratch.at[d], out_ref.at[dest_ref[step * RADIX + d]], sems.at[d]
+        )
+
+    @pl.when(block > 0)
+    def _():
+        for d in range(RADIX):
+            tile_copy(block - 1, d).wait()
+
+    for d in range(RADIX):
+        feat_scratch[d] = feature[d * rows_per : (d + 1) * rows_per]
+    for d in range(RADIX):
+        tile_copy(block, d).start()
+
+    @pl.when(block == pl.num_programs(0) - 1)
+    def _():
+        for d in range(RADIX):
+            tile_copy(block, d).wait()
+
+
+def spectrum_call(products, table_sub, hops_total, dest, slots):
     _, sensors, combos, rows, sub_n = products.shape
     per_device = rows // RADIX
     blocks = sensors * combos
@@ -159,36 +183,50 @@
     twist_cos = jnp.tile(norm_factor * jnp.cos(twist_angle), (per_device, 1))
     twist_sin = jnp.tile(norm_factor * jnp.sin(twist_angle), (per_device, 1))
     mixers = section_mixers(RADIX, per_device)
-    spectrum, tiles = pl.pallas_call(
-        spectrum_kernel,
+    zeros = jnp.zeros((slots, per_device, sub_n), jnp.bfloat16)
+    grid_spec = pltpu.PrefetchScalarGridSpec(
+        num_scalar_prefetch=1,
         grid=(blocks,),
         in_specs=[
-            pl.BlockSpec((2, 1, rows, sub_n), lambda i: (0, i, 0, 0)),
-            pl.BlockSpec((sub_n, sub_n), lambda i: (0, 0)),
-            pl.BlockSpec((sub_n, sub_n), lambda i: (0, 1)),
-            pl.BlockSpec((rows, sub_n), lambda i: (0, 0)),
-            pl.BlockSpec((rows, sub_n), lambda i: (0, 0)),
-            pl.BlockSpec((4, rows, rows), lambda i: (0, 0, 0)),
+            pl.BlockSpec((2, 1, rows, sub_n), lambda i, dest: (0, i, 0, 0)),
+            pl.BlockSpec((sub_n, sub_n), lambda i, dest: (0, 0)),
+            pl.BlockSpec((sub_n, sub_n), lambda i, dest: (0, 1)),
+            pl.BlockSpec((rows, sub_n), lambda i, dest: (0, 0)),
+            pl.BlockSpec((rows, sub_n), lambda i, dest: (0, 0)),
+            pl.BlockSpec((4, rows, rows), lambda i, dest: (0, 0, 0)),
+            pl.BlockSpec(memory_space=pl.ANY),
         ],
         out_specs=[
             pl.BlockSpec(
                 (2, 1, 1, per_device, RADIX * sub_n),
-                lambda i: (0, i // combos, i % combos, 0, 0),
+                lambda i, dest: (0, i // combos, i % combos, 0, 0),
             ),
-            pl.BlockSpec((RADIX, per_device, sub_n), lambda i: (i, 0, 0)),
+            pl.BlockSpec(memory_space=pl.ANY),
         ],
+        scratch_shapes=[
+            pltpu.VMEM((RADIX, per_device, sub_n), jnp.bfloat16),
+            pltpu.SemaphoreType.DMA((RADIX,)),
+        ],
+    )
+    spectrum, outgoing = pl.pallas_call(
+        spectrum_kernel,
+        grid_spec=grid_spec,
         out_shape=[
             jax.ShapeDtypeStruct((2, sensors, combos, per_device, RADIX * sub_n), jnp.bfloat16),
-            jax.ShapeDtypeStruct((blocks * RADIX, per_device, sub_n), jnp.bfloat16),
+            jax.ShapeDtypeStruct((slots, per_device, sub_n), jnp.bfloat16),
         ],
-        compiler_params=pltpu.CompilerParams(vmem_limit_bytes=48 * 1024 * 1024),
+        input_output_aliases={7: 1},
+        compiler_params=pltpu.CompilerParams(
+            vmem_limit_bytes=48 * 1024 * 1024,
+            dimension_semantics=("arbitrary",),
+        ),
         cost_estimate=pl.CostEstimate(
             flops=blocks * (8 * rows * sub_n * sub_n + 16 * rows * rows * sub_n),
             transcendentals=blocks * rows * sub_n,
             bytes_accessed=blocks * rows * sub_n * 2 * 5 + 4 * sub_n * sub_n,
         ),
-    )(flat, table_sub, table_sub, twist_cos, twist_sin, mixers)
-    return spectrum, tiles
+    )(dest, flat, table_sub, table_sub, twist_cos, twist_sin, mixers, zeros)
+    return spectrum, outgoing
 
 
 def shards(frames, orders, owners, templates):
@@ -215,9 +253,9 @@
     summed = jnp.zeros((sensors, 2 * local_channels, hop_dev), jnp.float32)
     for quarter in range(4):
         summed = summed + jnp.einsum(
-            "shf,fk->skh",
+            "shf,kf->skh",
             padded[:, quarter : quarter + hop_dev],
-            coefficients[quarter * frame_len : (quarter + 1) * frame_len],
+            coefficients[:, quarter * frame_len : (quarter + 1) * frame_len],
             preferred_element_type=jnp.float32,
         )
     hop_ids = row_at * hop_dev + jnp.arange(hop_dev, dtype=jnp.int32)
@@ -244,10 +282,6 @@
     products = jnp.stack([jnp.stack(prod_real, axis=1), jnp.stack(prod_imag, axis=1)]).astype(
         jnp.bfloat16
     )
-    table_sub = sub_coefficients(sub_n)
-    spectrum, tiles = spectrum_call(
-        products.reshape(2, sensors, combos, per_device * RADIX, sub_n), table_sub, hops_n
-    )
     tiles_dev = sensors * combos * RADIX
     capacity = max(2, 2 * tiles_dev // devices_n)
     owner_ids = owners[:, 0]
@@ -256,13 +290,18 @@
     before = jnp.cumsum(one_hot, axis=0) - one_hot
     slot_ids = jnp.sum(before * one_hot, axis=1)
     places = owner_ids * capacity + slot_ids
-    slot_range = jnp.arange(devices_n * capacity, dtype=jnp.int32)
-    placing = (places[None, :] == slot_range[:, None]).astype(jnp.bfloat16)
-    outgoing = jnp.einsum("ot,tkq->okq", placing, tiles, preferred_element_type=jnp.float32)
-    outgoing = outgoing.astype(jnp.bfloat16).reshape(devices_n, capacity * per_device, sub_n)
+    table_sub = sub_coefficients(sub_n)
+    spectrum, outgoing = spectrum_call(
+        products.reshape(2, sensors, combos, per_device * RADIX, sub_n),
+        table_sub,
+        hops_n,
+        places,
+        devices_n * capacity,
+    )
+    outgoing = outgoing.reshape(devices_n, capacity * per_device, sub_n)
     arrived = lax.all_to_all(outgoing, ("row", "col"), split_axis=0, concat_axis=0, tiled=True)
-    found = jnp.einsum(
-        "tkq,qf->tkf", arrived, templates[0], preferred_element_type=jnp.float32
+    found = jnp.dot(
+        arrived.reshape(-1, sub_n), templates[0], preferred_element_type=jnp.float32
     ).astype(jnp.bfloat16)
     found = found.reshape(devices_n, capacity, per_device, feat_n)
     return (spectrum, found[None])

time: 183 us -> 172 us (0.940)
  local copies, waits for them, and re-layouts: 27.3 us -> 19.6 us
  matrix products: 10.9 us -> 5.31 us
  Pallas kernels: 18.7 us -> 23 us
  other arithmetic: 17.9 us -> 15.9 us
    dot_general x6 -> x5, matrix products: 10.9 us -> 5.31 us  [the longest x4 3.08 us: shards(): jnp.einsum('shf,kf->skh', padded[:, quarter:quarter + hop_dev], coefficie...]
    pallas_call x1, Pallas kernels: 18.7 us -> 23 us  [spectrum_call(): pl.pallas_call(spectrum_kernel, grid_spec=grid_spec, out_shape=[jax.Shape...]
    sub x1 -> x0, local copies, waits for them, and re-layouts: 2.89 us -> none  [channel_coefficients(): cos_part = (high_cos * low_cos - high_sin * low_sin).reshape(n_total, -1)]
    convert_element_type x1 -> x0, local copies, waits for them, and re-layouts: 2.4 us -> none  [shards(): outgoing.astype(jnp.bfloat16)]
    add x1 -> x0, local copies, waits for them, and re-layouts: 1.92 us -> none  [channel_coefficients(): sin_part = (high_sin * low_cos + high_cos * low_sin).reshape(n_total, -1)]
  transfers between devices with their start and end apart: 3 -> 3, of which waited for: 2 -> 2; matrix products, arithmetic and copies ran while one was open for 9% -> 6% of each run, Pallas kernels for 0% -> 0%
where the time goes in v4:
time: 172 us
  blocking collectives  60.7 us (35%)
  waiting for transfers between devices  25.8 us (15%)
  Pallas kernels  23 us (13%)
  local copies, waits for them, and re-layouts  19.6 us (11%)
  other arithmetic  15.9 us (9%)
  starting transfers between devices  12.8 us (7%)
  between operations  8.66 us (5%)
  matrix products  5.31 us (3%)
    all_to_all x1, blocking collectives, shards(): lax.all_to_all(outgoing, ('row', 'col'), split_axis=0, concat_axis=0, til...  60.7 us
    pallas_call x1, Pallas kernels, spectrum_call(): pl.pallas_call(spectrum_kernel, grid_spec=grid_spec, out_shape=[jax.Shape...  23 us
    ppermute x1, waiting for transfers between devices, from_behind_2(): return lax.ppermute(value, axis, pairs)  18 us
    reshape x1, local copies, waits for them, and re-layouts, shards(): swapped.reshape(2, sensors, per_device, sub_n, RADIX)  9.14 us
    all_to_all x1, waiting for transfers between devices, shards(): lax.all_to_all(demod, 'row', split_axis=2, concat_axis=3, tiled=True)  7.77 us
    all_to_all x1, starting transfers between devices, shards(): lax.all_to_all(demod, 'row', split_axis=2, concat_axis=3, tiled=True)  6.78 us
    all_to_all x1, local copies, waits for them, and re-layouts, shards(): lax.all_to_all(demod, 'row', split_axis=2, concat_axis=3, tiled=True)  5.9 us
    another operation x2, other arithmetic  5.61 us
  transfers between devices with their start and end apart: 3, of which 2 were waited for; matrix products, arithmetic and copies ran while one was open for 6% of the time, Pallas kernels for 0%

profile of v4, /device:TPU:0, one launch (start us, length us, event | category | flops | bytes accessed | tf_op | source)
XLA Modules:
  0.0 171.7 jit_solution(10860949127656241139)
XLA Ops:
  0.6 0.8 slice.82
  1.4 1.3 collective-permute-start
  2.9 0.6 fusion.72
  3.8 0.3 convert_subtract_fusion.1
  4.1 1.2 multiply_add_fusion
  5.3 1.3 fusion
  6.7 0.7 fusion.55
  7.5 0.8 fusion.35
  8.3 0.8 fusion.33
  9.0 0.8 add_bitcast_fusion
  9.9 0.4 fusion.40
  10.4 1.8 %copy.46 = bf16[2,4,256,256]{3,1,0,2:T(4,128)(2,1)} copy(bf16[2,4,256,256]{3,2,1,0:T(8,128)(2,1)S(1)} %pad_maximum_fusion.3) | data formatting | bytes 2097152 | tf_op jit(solution)/shard_map/stack | solution.py:265
  12.2 6.8 %all-to-all-start = ((bf16[2,4,256,256]{3,1,0,2:T(4,128)(2,1)}), bf16[2,4,256,256]{3,1,0,2:T(4,128)(2,1)S(1)}, u32[]{:S(2)}, u32[]{:S(2)}) async-start(bf16[2,4,256,256]{3,1,0,2:T(4,128)(2,1)} %copy.46), calls=%async_computation | async-start | bytes 2097152 | tf_op jit(solution)/shard_map/all_to_all | solution.py:266
  19.0 0.7 fusion.97
  27.6 7.8 %all-to-all-done = bf16[2,4,256,256]{3,1,0,2:T(4,128)(2,1)S(1)} async-done(((bf16[2,4,256,256]{3,1,0,2:T(4,128)(2,1)}), bf16[2,4,256,256]{3,1,0,2:T(4,128)(2,1)S(1)}, u32[]{:S(2)}, u32[]{:S(2)}) %all-to-all-start) | async-done | bytes 1048608 | tf_op jit(solution)/shard_map/all_to_all | solution.py:266
  35.4 5.9 %copy.47 = bf16[2,4,16,16,256]{3,4,2,1,0:T(8,128)(2,1)} copy(bf16[2,4,16,16,256]{4,1,0,3,2:T(4,128)(2,1)S(1)} %bitcast.96) | data formatting | bytes 2097152 | tf_op jit(solution)/shard_map/all_to_all | solution.py:266
  41.3 9.1 %copy.48 = bf16[2,4,16,512,8]{3,4,2,1,0:T(8,128)(2,1)S(1)} copy(bf16[2,4,16,512,8]{2,4,3,1,0:T(8,128)(2,1)} %bitcast.86) | data formatting | bytes 2097152 | tf_op jit(solution)/shard_map/reshape | solution.py:267
  50.5 4.8 %collective-permute-start.1 = (bf16[2,4,16,8,512]{4,3,2,1,0:T(8,128)(2,1)S(1)}, bf16[2,4,16,8,512]{4,3,2,1,0:T(8,128)(2,1)S(1)}, u32[]{:S(2)}, u32[]{:S(2)}) collective-permute-start(bf16[2,4,16,8,512]{4,3,2,1,0:T(8,128)(2,1)S(1)} %bitcast.88), channel_id=1, source_target_pairs={{0,127},{1,0},{2,1},{3,2},{4,3},{5,4},{6,5},{7,6},{8,7},{9,8},{10,... | collective-permute-start | bytes 3145736 | tf_op jit(solution)/shard_map/ppermute | solution.py:23
  55.4 0.2 select_reduce_fusion
  55.6 4.3 %sine_convert_fusion = (bf16[512,512]{1,0:T(8,128)(2,1)S(1)}, bf16[512,512]{1,0:T(8,128)(2,1)S(1)}) fusion(), kind=kLoop, calls=%fused_computation.79 | loop fusion | flops 4194304 | bytes 1048576 | tf_op jit(solution)/shard_map/convert.1
  60.1 18.0 %collective-permute-done.1 = bf16[2,4,16,8,512]{4,3,2,1,0:T(8,128)(2,1)S(1)} collective-permute-done((bf16[2,4,16,8,512]{4,3,2,1,0:T(8,128)(2,1)S(1)}, bf16[2,4,16,8,512]{4,3,2,1,0:T(8,128)(2,1)S(1)}, u32[]{:S(2)}, u32[]{:S(2)}) %collective-permute-start.1) | collective-permute-done | bytes 1048608 | tf_op jit(solution)/shard_map/ppermute | solution.py:23
  78.1 2.3 %fusion.24 = (f32[2,4,16,8,512]{4,3,2,1,0:T(8,128)S(1)}, f32[2,4,16,8,512]{4,3,2,1,0:T(8,128)S(1)}, f32[2,4,16,8,512]{4,3,2,1,0:T(8,128)S(1)}, f32[2,4,16,8,512]{4,3,2,1,0:T(8,128)S(1)}) fusion(s32[]{:T(128)S(6)} %select_n.129, bf16[2,4,16,8,512]{4,3,2,1,0:T(8,128)(2,1)S(1)} %bitcast.89, bf16[2,4,16,8,512]{4,3,2,1,0:T(8,128)(2,1)S(1)} %collective-permute-done.1, ...), kind=kLoop, calls=%fused_computation.66 | loop fusion | flops 4194304 | bytes 10485776 | tf_op jit(solution)/shard_map/convert_element_type | solution.py:279
  80.4 0.8 fusion.49
  81.2 0.8 fusion.48
  82.1 0.3 pad_maximum_fusion.1
  82.3 0.3 pad_maximum_fusion.2
  82.6 2.3 %pad_maximum_fusion.prod_ref = bf16[2,16,128,512]{3,2,1,0:T(8,128)(2,1)} fusion(bf16[1,16,128,512]{3,2,1,0:T(8,128)(2,1)S(1)} %bitcast.95, bf16[1,16,128,512]{3,2,1,0:T(8,128)(2,1)S(1)} %bitcast.94), kind=kLoop, calls=%fused_computation.1 | loop fusion | flops 2097152 | bytes 8388608 | tf_op jit(solution)/shard_map/stack | solution.py:282
  84.9 0.5 broadcast_in_dim.2.zero_ref
  85.5 0.4 copy-done.1
  85.8 23.0 %shard_map.77 = (bf16[2,4,4,16,4096]{4,3,2,1,0:T(8,128)(2,1)}, bf16[256,16,512]{2,1,0:T(8,128)(2,1)S(1)}) custom-call(s32[128]{0:T(128)S(1)} %multiply_add_fusion.1.dest_ref, bf16[2,16,128,512]{3,2,1,0:T(8,128)(2,1)} %pad_maximum_fusion.prod_ref, bf16[512,1024]{1,0:T(8,128)(2,1)S(1)} %pad_maximum_fusion.4.cos_ref.sin_ref, ...), custom_call_target="tpu_custom_call", output_to_operand_aliasing={{1}: (7, {})} | custom-call | flops 6442450944 | bytes 11534336 | tf_op jit(solution)/shard_map/pallas_call | solution.py:211
  108.8 60.7 %all_to_all.20 = bf16[128,32,512]{2,1,0:T(8,128)(2,1)S(1)} all-to-all(bf16[128,32,512]{2,1,0:T(8,128)(2,1)S(1)} %bitcast.85), channel_id=1, replica_groups=mesh['row'=16,'col'=8] {'row','col'}, dimensions={0} | all-to-all | bytes 8388608 | tf_op jit(solution)/shard_map/all_to_all | solution.py:302
  169.5 2.2 %convolution_convert_fusion = bf16[4096,128]{1,0:T(8,128)(2,1)} fusion(bf16[4096,512]{1,0:T(8,128)(2,1)S(1)} %bitcast.87, bf16[1,512,128]{2,1,0:T(8,128)(2,1)S(1)} %copy-done), kind=kOutput, calls=%fused_computation | convolution fusion | flops 537395200 | bytes 5373952 | tf_op jit(solution)/shard_map/dot_general | solution.py:303
  (27 shorter events, 1.3 us)
Async XLA Ops:
  0.6 168.9 %copy-start = (bf16[1,512,128]{2,1,0:T(8,128)(2,1)S(1)}, bf16[1,512,128]{2,1,0:T(8,128)(2,1)}, u32[]{:S(2)}) copy-start(bf16[1,512,128]{2,1,0:T(8,128)(2,1)} %param.9) | copy-start | bytes 393220
  1.4 6.0 %collective-permute-start = (bf16[4,3,512]{2,1,0:T(4,128)(2,1)S(1)}, bf16[4,3,512]{2,1,0:T(4,128)(2,1)S(1)}, u32[]{:S(2)}, u32[]{:S(2)}) collective-permute-start(bf16[4,3,512]{2,1,0:T(4,128)(2,1)S(1)} %slice.82), channel_id=1, source_target_pairs={{8,0},{16,8},{24,16},{32,24},{40,32},{48,40},{56,48},{64,56},{72,6... | collective-permute-start | bytes 36872 | tf_op jit(solution)/shard_map/ppermute | solution.py:17
  5.3 1.3 copy-start.2
  10.4 8.6 %copy-start.3 = (s32[2,2]{1,0:T(2,128)S(1)}, s32[2,2]{1,0:T(2,128)}, u32[]{:S(2)}) copy-start(s32[2,2]{1,0:T(2,128)} %param.7) | copy-start | bytes 52
  10.4 14.4 %copy-start.4 = (s32[128,1]{0,1:T(1,128)S(1)}, s32[128,1]{0,1:T(1,128)}, u32[]{:S(2)}) copy-start(s32[128,1]{0,1:T(1,128)} %param.8) | copy-start | bytes 1540
  12.2 23.2 %all-to-all-start = ((bf16[2,4,256,256]{3,1,0,2:T(4,128)(2,1)}), bf16[2,4,256,256]{3,1,0,2:T(4,128)(2,1)S(1)}, u32[]{:S(2)}, u32[]{:S(2)}) async-start(bf16[2,4,256,256]{3,1,0,2:T(4,128)(2,1)} %copy.46), calls=%async_computation | async-start | bytes 2097152 | tf_op jit(solution)/shard_map/all_to_all | solution.py:266
  50.5 27.7 %collective-permute-start.1 = (bf16[2,4,16,8,512]{4,3,2,1,0:T(8,128)(2,1)S(1)}, bf16[2,4,16,8,512]{4,3,2,1,0:T(8,128)(2,1)S(1)}, u32[]{:S(2)}, u32[]{:S(2)}) collective-permute-start(bf16[2,4,16,8,512]{4,3,2,1,0:T(8,128)(2,1)S(1)} %bitcast.88), channel_id=1, source_target_pairs={{0,127},{1,0},{2,1},{3,2},{4,3},{5,4},{6,5},{7,6},{8,7},{9,8},{10,... | collective-permute-start | bytes 3145736 | tf_op jit(solution)/shard_map/ppermute | solution.py:23
  84.9 0.9 copy-start.1

commit v5 on v4

--- a/solution.py
+++ b/solution.py
@@ -105,11 +105,8 @@
     return jnp.stack(mixers)
 
 
-def spectrum_kernel(
-    dest_ref, prod_ref, cos_ref, sin_ref, twc_ref, tws_ref, mix_ref, zero_ref, spec_ref, out_ref,
-    feat_scratch, sems,
-):
-    del zero_ref
+def spectrum_kernel(dest_ref, prod_ref, cos_ref, sin_ref, twc_ref, tws_ref, mix_ref, *refs):
+    spec_ref, out_ref, feat_scratch, sems = refs[-4:]
     f32 = jnp.float32
     block = pl.program_id(0)
     rows_per = feat_scratch.shape[1]
@@ -171,10 +168,10 @@
             tile_copy(block, d).wait()
 
 
-def spectrum_call(products, table_sub, hops_total, dest, slots):
-    _, sensors, combos, rows, sub_n = products.shape
+def spectrum_call(products, table_sub, hops_total, dest, outgoing, spectrum, first_block, sensors):
+    _, _, combos, rows, sub_n = products.shape
     per_device = rows // RADIX
-    blocks = sensors * combos
+    blocks = products.shape[1] * combos
     flat = products.reshape(2, blocks, rows, sub_n)
     index_b = jnp.arange(RADIX, dtype=jnp.int32)[:, None]
     index_p = jnp.arange(sub_n, dtype=jnp.int32)[None, :]
@@ -183,23 +180,30 @@
     twist_cos = jnp.tile(norm_factor * jnp.cos(twist_angle), (per_device, 1))
     twist_sin = jnp.tile(norm_factor * jnp.sin(twist_angle), (per_device, 1))
     mixers = section_mixers(RADIX, per_device)
-    zeros = jnp.zeros((slots, per_device, sub_n), jnp.bfloat16)
+    operands = [dest, flat, table_sub, table_sub, twist_cos, twist_sin, mixers, outgoing]
+    in_specs = [
+        pl.BlockSpec((2, 1, rows, sub_n), lambda i, dest: (0, i, 0, 0)),
+        pl.BlockSpec((sub_n, sub_n), lambda i, dest: (0, 0)),
+        pl.BlockSpec((sub_n, sub_n), lambda i, dest: (0, 1)),
+        pl.BlockSpec((rows, sub_n), lambda i, dest: (0, 0)),
+        pl.BlockSpec((rows, sub_n), lambda i, dest: (0, 0)),
+        pl.BlockSpec((4, rows, rows), lambda i, dest: (0, 0, 0)),
+        pl.BlockSpec(memory_space=pl.ANY),
+    ]
+    aliases = {7: 1}
+    if spectrum is not None:
+        operands.append(spectrum)
+        in_specs.append(pl.BlockSpec(memory_space=pl.ANY))
+        aliases[8] = 0
+    spec_shape = (2, sensors, combos, per_device, RADIX * sub_n)
     grid_spec = pltpu.PrefetchScalarGridSpec(
         num_scalar_prefetch=1,
         grid=(blocks,),
-        in_specs=[
-            pl.BlockSpec((2, 1, rows, sub_n), lambda i, dest: (0, i, 0, 0)),
-            pl.BlockSpec((sub_n, sub_n), lambda i, dest: (0, 0)),
-            pl.BlockSpec((sub_n, sub_n), lambda i, dest: (0, 1)),
-            pl.BlockSpec((rows, sub_n), lambda i, dest: (0, 0)),
-            pl.BlockSpec((rows, sub_n), lambda i, dest: (0, 0)),
-            pl.BlockSpec((4, rows, rows), lambda i, dest: (0, 0, 0)),
-            pl.BlockSpec(memory_space=pl.ANY),
-        ],
+        in_specs=in_specs,
         out_specs=[
             pl.BlockSpec(
                 (2, 1, 1, per_device, RADIX * sub_n),
-                lambda i, dest: (0, i // combos, i % combos, 0, 0),
+                lambda i, dest: (0, (i + first_block) // combos, (i + first_block) % combos, 0, 0),
             ),
             pl.BlockSpec(memory_space=pl.ANY),
         ],
@@ -208,14 +212,14 @@
             pltpu.SemaphoreType.DMA((RADIX,)),
         ],
     )
-    spectrum, outgoing = pl.pallas_call(
+    return pl.pallas_call(
         spectrum_kernel,
         grid_spec=grid_spec,
         out_shape=[
-            jax.ShapeDtypeStruct((2, sensors, combos, per_device, RADIX * sub_n), jnp.bfloat16),
-            jax.ShapeDtypeStruct((slots, per_device, sub_n), jnp.bfloat16),
+            jax.ShapeDtypeStruct(spec_shape, jnp.bfloat16),
+            jax.ShapeDtypeStruct(outgoing.shape, jnp.bfloat16),
         ],
-        input_output_aliases={7: 1},
+        input_output_aliases=aliases,
         compiler_params=pltpu.CompilerParams(
             vmem_limit_bytes=48 * 1024 * 1024,
             dimension_semantics=("arbitrary",),
@@ -225,8 +229,7 @@
             transcendentals=blocks * rows * sub_n,
             bytes_accessed=blocks * rows * sub_n * 2 * 5 + 4 * sub_n * sub_n,
         ),
-    )(dest, flat, table_sub, table_sub, twist_cos, twist_sin, mixers, zeros)
-    return spectrum, outgoing
+    )(*operands)
 
 
 def shards(frames, orders, owners, templates):
@@ -246,42 +249,48 @@
     row_at = lax.axis_index("row")
     col_at = lax.axis_index("col")
     tail_frames = from_behind(frames[:, :3], "row", -1)
-    padded = jnp.concatenate([frames, tail_frames], axis=1)
+    padded_all = jnp.concatenate([frames, tail_frames], axis=1)
     column = jnp.arange(local_channels, dtype=jnp.int32)
     channel_ids = (column // per_device * cols_count + col_at) * per_device + column % per_device
     coefficients = channel_coefficients(channels_n, channel_ids)
-    summed = jnp.zeros((sensors, 2 * local_channels, hop_dev), jnp.float32)
-    for quarter in range(4):
-        summed = summed + jnp.einsum(
-            "shf,kf->skh",
-            padded[:, quarter : quarter + hop_dev],
-            coefficients[:, quarter * frame_len : (quarter + 1) * frame_len],
-            preferred_element_type=jnp.float32,
-        )
-    hop_ids = row_at * hop_dev + jnp.arange(hop_dev, dtype=jnp.int32)
-    real_part, imag_part = quarter_turn(
-        summed[:, :local_channels], summed[:, local_channels:], channel_ids, hop_ids
-    )
-    demod = jnp.stack([real_part, imag_part]).astype(jnp.bfloat16)
-    swapped = lax.all_to_all(demod, "row", split_axis=2, concat_axis=3, tiled=True)
-    ordered = swapped.reshape(2, sensors, per_device, sub_n, RADIX).transpose(0, 1, 2, 4, 3)
-    above = from_behind_2(ordered, ("row", "col"), -1)
-    extended = jnp.concatenate([ordered, above], axis=2)
-    own_real = ordered[0].astype(jnp.float32)
-    own_imag = ordered[1].astype(jnp.float32)
-    prod_real = []
-    prod_imag = []
-    for wheel in range(orders.shape[0]):
-        for order_at in range(orders.shape[1]):
-            partner = lax.dynamic_slice_in_dim(
-                extended, orders[wheel, order_at], per_device, axis=2
+
+    def front(padded):
+        sensors = padded.shape[0]
+        summed = jnp.zeros((sensors, 2 * local_channels, hop_dev), jnp.float32)
+        for quarter in range(4):
+            summed = summed + jnp.einsum(
+                "shf,kf->skh",
+                padded[:, quarter : quarter + hop_dev],
+                coefficients[:, quarter * frame_len : (quarter + 1) * frame_len],
+                preferred_element_type=jnp.float32,
             )
-            partner = partner.astype(jnp.float32)
-            prod_real.append(own_real * partner[0] + own_imag * partner[1])
-            prod_imag.append(own_imag * partner[0] - own_real * partner[1])
-    products = jnp.stack([jnp.stack(prod_real, axis=1), jnp.stack(prod_imag, axis=1)]).astype(
-        jnp.bfloat16
-    )
+        hop_ids = row_at * hop_dev + jnp.arange(hop_dev, dtype=jnp.int32)
+        real_part, imag_part = quarter_turn(
+            summed[:, :local_channels], summed[:, local_channels:], channel_ids, hop_ids
+        )
+        demod = jnp.stack([real_part, imag_part]).astype(jnp.bfloat16)
+        swapped = lax.all_to_all(demod, "row", split_axis=2, concat_axis=3, tiled=True)
+        ordered = swapped.reshape(2, sensors, per_device, sub_n, RADIX).transpose(0, 1, 2, 4, 3)
+        above = from_behind_2(ordered, ("row", "col"), -1)
+        extended = jnp.concatenate([ordered, above], axis=2)
+        own_real = ordered[0].astype(jnp.float32)
+        own_imag = ordered[1].astype(jnp.float32)
+        prod_real = []
+        prod_imag = []
+        for wheel in range(orders.shape[0]):
+            for order_at in range(orders.shape[1]):
+                partner = lax.dynamic_slice_in_dim(
+                    extended, orders[wheel, order_at], per_device, axis=2
+                )
+                partner = partner.astype(jnp.float32)
+                prod_real.append(own_real * partner[0] + own_imag * partner[1])
+                prod_imag.append(own_imag * partner[0] - own_real * partner[1])
+        products = jnp.stack([jnp.stack(prod_real, axis=1), jnp.stack(prod_imag, axis=1)]).astype(
+            jnp.bfloat16
+        )
+
+        return products.reshape(2, sensors, combos, per_device * RADIX, sub_n)
+
     tiles_dev = sensors * combos * RADIX
     capacity = max(2, 2 * tiles_dev // devices_n)
     owner_ids = owners[:, 0]
@@ -291,13 +300,23 @@
     slot_ids = jnp.sum(before * one_hot, axis=1)
     places = owner_ids * capacity + slot_ids
     table_sub = sub_coefficients(sub_n)
-    spectrum, outgoing = spectrum_call(
-        products.reshape(2, sensors, combos, per_device * RADIX, sub_n),
-        table_sub,
-        hops_n,
-        places,
-        devices_n * capacity,
-    )
+    halves = 2
+    part = sensors // halves
+    tiles_part = tiles_dev // halves
+    outgoing = jnp.zeros((devices_n * capacity, per_device, sub_n), jnp.bfloat16)
+    spectrum = None
+    for half in range(halves):
+        products = front(padded_all[half * part : (half + 1) * part])
+        spectrum, outgoing = spectrum_call(
+            products,
+            table_sub,
+            hops_n,
+            places[half * tiles_part : (half + 1) * tiles_part],
+            outgoing,
+            spectrum,
+            half * part * combos,
+            sensors,
+        )
     outgoing = outgoing.reshape(devices_n, capacity * per_device, sub_n)
     arrived = lax.all_to_all(outgoing, ("row", "col"), split_axis=0, concat_axis=0, tiled=True)
     found = jnp.dot(

time: 172 us -> 181 us (1.052)
  starting transfers between devices: 12.8 us -> 20.3 us
  local copies, waits for them, and re-layouts: 19.6 us -> 25.8 us
  waiting for transfers between devices: 25.8 us -> 19.6 us
  matrix products: 5.31 us -> 9.18 us
    ppermute x1 -> x2, waiting for transfers between devices: 18 us -> 10.5 us  [from_behind_2(): return lax.ppermute(value, axis, pairs)]
    dot_general x4 -> x8, matrix products: 3.08 us -> 6.96 us  [front(): jnp.einsum('shf,kf->skh', padded[:, quarter:quarter + hop_dev], coefficie...]
    ppermute x1 -> x2, starting transfers between devices: 4.78 us -> 8.64 us  [from_behind_2(): return lax.ppermute(value, axis, pairs)]
    all_to_all x1 -> x2, starting transfers between devices: 6.78 us -> 10.4 us  [front(): lax.all_to_all(demod, 'row', split_axis=2, concat_axis=3, tiled=True)]
    unnamed x11 -> x21, local copies, waits for them, and re-layouts: 0.48 us -> 2.61 us
    broadcast_in_dim x1, local copies, waits for them, and re-layouts: 0.52 us -> 2.49 us  [shards(): jnp.zeros((devices_n * capacity, per_device, sub_n), jnp.bfloat16)]
    all_to_all x1 -> x2, waiting for transfers between devices: 7.77 us -> 9.17 us  [front(): lax.all_to_all(demod, 'row', split_axis=2, concat_axis=3, tiled=True)]
    another operation x7 -> x11, other arithmetic: 8.94 us -> 7.65 us
  transfers between devices with their start and end apart: 3 -> 5, of which waited for: 2 -> 2; matrix products, arithmetic and copies ran while one was open for 6% -> 20% of each run, Pallas kernels for 0% -> 0%
where the time goes in v5:
time: 181 us; the launch traced here: 180 us
  blocking collectives  59.3 us (33%)
  local copies, waits for them, and re-layouts  25.8 us (14%)
  Pallas kernels  22.1 us (12%)
  starting transfers between devices  20.3 us (11%)
  waiting for transfers between devices  19.6 us (11%)
  other arithmetic  15.5 us (9%)
  matrix products  9.18 us (5%)
  between operations  8.62 us (5%)
    all_to_all x1, blocking collectives, shards(): lax.all_to_all(outgoing, ('row', 'col'), split_axis=0, concat_axis=0, til...  59.3 us
    pallas_call x2, Pallas kernels, spectrum_call(): pl.pallas_call(spectrum_kernel, grid_spec=grid_spec, out_shape=[jax.Shape...  22.1 us
    ppermute x2, waiting for transfers between devices, from_behind_2(): return lax.ppermute(value, axis, pairs)  10.5 us
    all_to_all x2, starting transfers between devices, front(): lax.all_to_all(demod, 'row', split_axis=2, concat_axis=3, tiled=True)  10.4 us
    reshape x2, local copies, waits for them, and re-layouts, front(): swapped.reshape(2, sensors, per_device, sub_n, RADIX)  9.88 us
    all_to_all x2, waiting for transfers between devices, front(): lax.all_to_all(demod, 'row', split_axis=2, concat_axis=3, tiled=True)  9.17 us
    ppermute x2, starting transfers between devices, from_behind_2(): return lax.ppermute(value, axis, pairs)  8.64 us
    dot_general x8, matrix products, front(): jnp.einsum('shf,kf->skh', padded[:, quarter:quarter + hop_dev], coefficie...  6.96 us
  transfers between devices with their start and end apart: 5, of which 2 were waited for; matrix products, arithmetic and copies ran while one was open for 20% of the time, Pallas kernels for 0%

profile of v5, /device:TPU:0, one launch (start us, length us, event | category | flops | bytes accessed | tf_op | source)
XLA Modules:
  0.0 180.4 jit_solution(10284478048574976560)
XLA Ops:
  0.6 0.8 slice.169
  1.4 1.3 collective-permute-start
  2.8 5.0 %sine_convert_fusion = (bf16[512,512]{1,0:T(8,128)(2,1)}, bf16[512,512]{1,0:T(8,128)(2,1)}) fusion(), kind=kLoop, calls=%fused_computation.82 | loop fusion | flops 4194304 | bytes 1048576 | tf_op jit(solution)/shard_map/convert.25
  7.8 1.3 constant_dynamic-update-slice_fusion.1
  9.1 0.6 fusion.114
  10.1 1.2 multiply_subtract_fusion
  11.3 1.3 fusion.1
  12.6 0.9 fusion.72
  13.5 0.5 copy-done.2
  14.0 1.4 fusion.75
  15.5 1.4 fusion.77
  17.8 1.6 fusion.66
  20.4 0.7 copy-done.3
  23.1 1.3 copy.96
  24.4 6.8 %all-to-all-start.1 = ((bf16[2,2,256,256]{3,1,0,2:T(2,128)(2,1)}), bf16[2,2,256,256]{3,1,0,2:T(2,128)(2,1)S(1)}, u32[]{:S(2)}, u32[]{:S(2)}) async-start(bf16[2,2,256,256]{3,1,0,2:T(2,128)(2,1)} %copy.96), calls=%async_computation.1 | async-start | bytes 1048576 | tf_op jit(solution)/shard_map/all_to_all | solution.py:272
  31.5 1.3 copy.85
  32.9 9.2 %all-to-all-done.1 = bf16[2,2,256,256]{3,1,0,2:T(2,128)(2,1)S(1)} async-done(((bf16[2,2,256,256]{3,1,0,2:T(2,128)(2,1)}), bf16[2,2,256,256]{3,1,0,2:T(2,128)(2,1)S(1)}, u32[]{:S(2)}, u32[]{:S(2)}) %all-to-all-start.1) | async-done | bytes 524320 | tf_op jit(solution)/shard_map/all_to_all | solution.py:272
  42.0 3.6 %all-to-all-start = ((bf16[2,2,256,256]{3,1,0,2:T(2,128)(2,1)}), bf16[2,2,256,256]{3,1,0,2:T(2,128)(2,1)S(1)}, u32[]{:S(2)}, u32[]{:S(2)}) async-start(bf16[2,2,256,256]{3,1,0,2:T(2,128)(2,1)} %copy.85), calls=%async_computation | async-start | bytes 1048576 | tf_op jit(solution)/shard_map/all_to_all | solution.py:272
  45.6 3.2 %copy.97 = bf16[2,2,16,16,256]{3,4,2,1,0:T(8,128)(2,1)} copy(bf16[2,2,16,16,256]{4,1,0,3,2:T(2,128)(2,1)S(1)} %bitcast.152) | data formatting | bytes 1048576 | tf_op jit(solution)/shard_map/all_to_all | solution.py:272
  48.8 4.9 %copy.98 = bf16[2,2,16,512,8]{3,4,2,1,0:T(8,128)(2,1)S(1)} copy(bf16[2,2,16,512,8]{2,4,3,1,0:T(8,128)(2,1)} %bitcast.135) | data formatting | bytes 1048576 | tf_op jit(solution)/shard_map/reshape | solution.py:273
  53.8 8.3 %collective-permute-start.2 = (bf16[2,2,16,8,512]{4,3,2,1,0:T(8,128)(2,1)S(1)}, bf16[2,2,16,8,512]{4,3,2,1,0:T(8,128)(2,1)S(1)}, u32[]{:S(2)}, u32[]{:S(2)}) collective-permute-start(bf16[2,2,16,8,512]{4,3,2,1,0:T(8,128)(2,1)S(1)} %bitcast.137), channel_id=1, source_target_pairs={{0,127},{1,0},{2,1},{3,2},{4,3},{5,4},{6,5},{7,6},{8,7},{9,8},{10,... | collective-permute-start | bytes 1572872 | tf_op jit(solution)/shard_map/ppermute | solution.py:23
  62.0 0.7 fusion.141
  70.4 3.2 %copy.86 = bf16[2,2,16,16,256]{3,4,2,1,0:T(8,128)(2,1)} copy(bf16[2,2,16,16,256]{4,1,0,3,2:T(2,128)(2,1)S(1)} %bitcast.151) | data formatting | bytes 1048576 | tf_op jit(solution)/shard_map/all_to_all | solution.py:272
  73.6 4.9 %copy.87 = bf16[2,2,16,512,8]{3,4,2,1,0:T(8,128)(2,1)S(1)} copy(bf16[2,2,16,512,8]{2,4,3,1,0:T(8,128)(2,1)} %bitcast.136) | data formatting | bytes 1048576 | tf_op jit(solution)/shard_map/reshape | solution.py:273
  78.9 1.3 fusion.47
  81.3 10.5 %collective-permute-done.1 = bf16[2,2,16,8,512]{4,3,2,1,0:T(8,128)(2,1)S(1)} collective-permute-done((bf16[2,2,16,8,512]{4,3,2,1,0:T(8,128)(2,1)S(1)}, bf16[2,2,16,8,512]{4,3,2,1,0:T(8,128)(2,1)S(1)}, u32[]{:S(2)}, u32[]{:S(2)}) %collective-permute-start.1) | collective-permute-done | bytes 524320 | tf_op jit(solution)/shard_map/ppermute | solution.py:23
  91.8 1.2 fusion.55
  94.2 2.5 %broadcast_in_dim.2.refs_0_ = bf16[256,16,512]{2,1,0:T(8,128)(2,1)} broadcast(bf16[]{:T(256)} %constant.172.clone.1), dimensions={} | broadcast | bytes 4194306 | tf_op jit(solution)/shard_map/broadcast_in_dim | solution.py:306
  96.7 11.0 %shard_map.95 = (bf16[2,4,4,16,4096]{4,3,2,1,0:T(8,128)(2,1)}, bf16[256,16,512]{2,1,0:T(8,128)(2,1)}) custom-call(s32[64]{0:T(128)S(1)} %get-tuple-element.62.dest_ref, bf16[2,8,128,512]{3,2,1,0:T(8,128)(2,1)S(1)} %pad_maximum_fusion.1.prod_ref, bf16[512,1024]{1,0:T(8,128)(2,1)S(1)} %pad_maximum_fusion.4.cos_ref.sin_ref, ...), custom_call_target="tpu_custom_call", output_to_operand_aliasing={{1}: (7, {})} | custom-call | flops 3221225472 | bytes 6291456 | tf_op jit(solution)/shard_map/pallas_call | solution.py:215
  107.7 11.1 %shard_map.96 = (bf16[2,4,4,16,4096]{4,3,2,1,0:T(8,128)(2,1)}, bf16[256,16,512]{2,1,0:T(8,128)(2,1)}) custom-call(s32[64]{0:T(128)S(1)} %get-tuple-element.63.dest_ref, bf16[2,8,128,512]{3,2,1,0:T(8,128)(2,1)S(1)} %pad_maximum_fusion.prod_ref, bf16[512,1024]{1,0:T(8,128)(2,1)S(1)} %pad_maximum_fusion.4.cos_ref.sin_ref, ...), custom_call_target="tpu_custom_call", output_to_operand_aliasing={{1}: (7, {}), {0}: (8, {})} | custom-call | flops 3221225472 | bytes 6291456 | tf_op jit(solution)/shard_map/pallas_call | solution.py:215
  118.8 59.3 %all_to_all.35 = bf16[128,32,512]{2,1,0:T(8,128)(2,1)S(1)} all-to-all(bf16[128,32,512]{2,1,0:T(8,128)(2,1)} %bitcast.133), channel_id=1, replica_groups=mesh['row'=16,'col'=8] {'row','col'}, dimensions={0} | all-to-all | bytes 8388608 | tf_op jit(solution)/shard_map/all_to_all | solution.py:321
  178.1 2.2 %convolution_convert_fusion = bf16[4096,128]{1,0:T(8,128)(2,1)} fusion(bf16[4096,512]{1,0:T(8,128)(2,1)S(1)} %bitcast.134, bf16[1,512,128]{2,1,0:T(8,128)(2,1)S(1)} %copy-done), kind=kOutput, calls=%fused_computation | convolution fusion | flops 537395200 | bytes 5373952 | tf_op jit(solution)/shard_map/dot_general | solution.py:322
  (58 shorter events, 7.2 us)
Async XLA Ops:
  0.6 177.5 %copy-start = (bf16[1,512,128]{2,1,0:T(8,128)(2,1)S(1)}, bf16[1,512,128]{2,1,0:T(8,128)(2,1)}, u32[]{:S(2)}) copy-start(bf16[1,512,128]{2,1,0:T(8,128)(2,1)} %param.11) | copy-start | bytes 393220
  1.4 16.3 %collective-permute-start = (bf16[4,3,512]{2,1,0:T(4,128)(2,1)S(1)}, bf16[4,3,512]{2,1,0:T(4,128)(2,1)S(1)}, u32[]{:S(2)}, u32[]{:S(2)}) collective-permute-start(bf16[4,3,512]{2,1,0:T(4,128)(2,1)S(1)} %slice.169), channel_id=1, source_target_pairs={{8,0},{16,8},{24,16},{32,24},{40,32},{48,40},{56,48},{64,56},{72,6... | collective-permute-start | bytes 36872 | tf_op jit(solution)/shard_map/ppermute | solution.py:17
  12.6 1.4 copy-start.2
  15.5 1.5 copy-start.9
  17.2 2.2 %copy-start.7 = (bf16[512,512,1]{1,0,2:T(8,128)(2,1)S(1)}, bf16[512,512,1]{1,0,2:T(8,128)(2,1)}, u32[]{:S(2)}) copy-start(bf16[512,512,1]{1,0,2:T(8,128)(2,1)} %fusion.72) | copy-start | bytes 1572868
  17.8 2.1 %copy-start.4 = (f32[512,2,256]{2,0,1:T(8,128)S(1)}, f32[512,2,256]{2,0,1:T(8,128)}, u32[]{:S(2)}) copy-start(f32[512,2,256]{2,0,1:T(8,128)} %fusion.75) | copy-start | bytes 3145732
  19.9 1.2 copy-start.3
  23.0 8.3 %copy-start.5 = (bf16[512,512]{1,0:T(8,128)(2,1)S(1)}, bf16[512,512]{1,0:T(8,128)(2,1)}, u32[]{:S(2)}) copy-start(bf16[512,512]{1,0:T(8,128)(2,1)} %get-tuple-element.66) | copy-start | bytes 1572868
  23.0 8.3 %copy-start.6 = (bf16[512,512]{1,0:T(8,128)(2,1)S(1)}, bf16[512,512]{1,0:T(8,128)(2,1)}, u32[]{:S(2)}) copy-start(bf16[512,512]{1,0:T(8,128)(2,1)} %get-tuple-element.67) | copy-start | bytes 1572868
  24.4 17.6 %all-to-all-start.1 = ((bf16[2,2,256,256]{3,1,0,2:T(2,128)(2,1)}), bf16[2,2,256,256]{3,1,0,2:T(2,128)(2,1)S(1)}, u32[]{:S(2)}, u32[]{:S(2)}) async-start(bf16[2,2,256,256]{3,1,0,2:T(2,128)(2,1)} %copy.96), calls=%async_computation.1 | async-start | bytes 1048576 | tf_op jit(solution)/shard_map/all_to_all | solution.py:272
  42.0 28.4 %all-to-all-start = ((bf16[2,2,256,256]{3,1,0,2:T(2,128)(2,1)}), bf16[2,2,256,256]{3,1,0,2:T(2,128)(2,1)S(1)}, u32[]{:S(2)}, u32[]{:S(2)}) async-start(bf16[2,2,256,256]{3,1,0,2:T(2,128)(2,1)} %copy.85), calls=%async_computation | async-start | bytes 1048576 | tf_op jit(solution)/shard_map/all_to_all | solution.py:272
  48.8 13.2 %copy-start.8 = (s32[2,2]{1,0:T(2,128)S(1)}, s32[2,2]{1,0:T(2,128)}, u32[]{:S(2)}) copy-start(s32[2,2]{1,0:T(2,128)} %param.9) | copy-start | bytes 52
  53.8 25.1 %collective-permute-start.2 = (bf16[2,2,16,8,512]{4,3,2,1,0:T(8,128)(2,1)S(1)}, bf16[2,2,16,8,512]{4,3,2,1,0:T(8,128)(2,1)S(1)}, u32[]{:S(2)}, u32[]{:S(2)}) collective-permute-start(bf16[2,2,16,8,512]{4,3,2,1,0:T(8,128)(2,1)S(1)} %bitcast.137), channel_id=1, source_target_pairs={{0,127},{1,0},{2,1},{3,2},{4,3},{5,4},{6,5},{7,6},{8,7},{9,8},{10,... | collective-permute-start | bytes 1572872 | tf_op jit(solution)/shard_map/ppermute | solution.py:23
  78.5 13.3 %collective-permute-start.1 = (bf16[2,2,16,8,512]{4,3,2,1,0:T(8,128)(2,1)S(1)}, bf16[2,2,16,8,512]{4,3,2,1,0:T(8,128)(2,1)S(1)}, u32[]{:S(2)}, u32[]{:S(2)}) collective-permute-start(bf16[2,2,16,8,512]{4,3,2,1,0:T(8,128)(2,1)S(1)} %bitcast.141), channel_id=1, source_target_pairs={{0,127},{1,0},{2,1},{3,2},{4,3},{5,4},{6,5},{7,6},{8,7},{9,8},{10,... | collective-permute-start | bytes 1572872 | tf_op jit(solution)/shard_map/ppermute | solution.py:23
  94.2 2.5 %copy-start.1 = (bf16[4,128,128]{2,1,0:T(8,128)(2,1)S(1)}, bf16[4,128,128]{2,1,0:T(8,128)(2,1)}, u32[]{:S(2)}) copy-start(bf16[4,128,128]{2,1,0:T(8,128)(2,1)} %constant.188.mix_ref) | copy-start | bytes 393220

commit v6 on v4

--- a/solution.py
+++ b/solution.py
@@ -92,17 +92,18 @@
 def section_mixers(radix_count, rows_per):
     index_b = np.arange(radix_count)
     angle = 2.0 * np.pi / radix_count * ((index_b[:, None] * index_b[None, :]) % radix_count)
-    mixers = []
+    size = radix_count * rows_per
+    tables = []
     for table in (np.cos(angle).astype(np.float32), np.sin(angle).astype(np.float32)):
-        full = np.zeros((radix_count * rows_per, rows_per * radix_count), np.float32)
+        full = np.zeros((size, size), np.float32)
         for d in range(radix_count):
             for b in range(radix_count):
                 for k in range(rows_per):
                     full[d * rows_per + k, k * radix_count + b] = table[b, d]
-        high = jnp.asarray(full).astype(jnp.bfloat16)
-        low = (jnp.asarray(full) - high.astype(jnp.float32)).astype(jnp.bfloat16)
-        mixers += [high, low]
-    return jnp.stack(mixers)
+        tables.append(full)
+    cos_full, sin_full = tables
+    both = np.block([[cos_full, sin_full], [-sin_full, cos_full]])
+    return jnp.asarray(both).astype(jnp.bfloat16)[None]
 
 
 def spectrum_kernel(
@@ -114,35 +115,25 @@
     block = pl.program_id(0)
     rows_per = feat_scratch.shape[1]
     sub_n = feat_scratch.shape[2]
-    prod_real = prod_ref[0, 0]
-    prod_imag = prod_ref[1, 0]
-    sub_cos = cos_ref[...]
-    sub_sin = sin_ref[...]
-    first_real = jnp.dot(prod_real, sub_cos, preferred_element_type=f32) + jnp.dot(
-        prod_imag, sub_sin, preferred_element_type=f32
-    )
-    first_imag = jnp.dot(prod_imag, sub_cos, preferred_element_type=f32) - jnp.dot(
-        prod_real, sub_sin, preferred_element_type=f32
-    )
+    rows_all = prod_ref.shape[2]
+    both = jnp.concatenate([prod_ref[0, 0], prod_ref[1, 0]], axis=0)
+    by_cos = jnp.dot(both, cos_ref[...], preferred_element_type=f32)
+    by_sin = jnp.dot(both, sin_ref[...], preferred_element_type=f32)
+    first_real = by_cos[:rows_all] + by_sin[rows_all:]
+    first_imag = by_cos[rows_all:] - by_sin[:rows_all]
     twist_cos = twc_ref[...]
     twist_sin = tws_ref[...]
     twist_real = first_real * twist_cos + first_imag * twist_sin
     twist_imag = first_imag * twist_cos - first_real * twist_sin
 
-    def split(value):
-        high = value.astype(jnp.bfloat16)
-        return high, (value - high.astype(f32)).astype(jnp.bfloat16)
-
-    real_high, real_low = split(twist_real)
-    imag_high, imag_low = split(twist_imag)
-
-    def mix(table, high, low):
-        return jnp.dot(mix_ref[table], high, preferred_element_type=f32) + jnp.dot(
-            mix_ref[table], low, preferred_element_type=f32
-        )
-
-    out_real = mix(0, real_high, real_low) + mix(2, imag_high, imag_low)
-    out_imag = mix(0, imag_high, imag_low) - mix(2, real_high, real_low)
+    twist = jnp.concatenate([twist_real, twist_imag], axis=0)
+    high = twist.astype(jnp.bfloat16)
+    low = (twist - high.astype(f32)).astype(jnp.bfloat16)
+    mixed = jnp.dot(mix_ref[0], high, preferred_element_type=f32) + jnp.dot(
+        mix_ref[0], low, preferred_element_type=f32
+    )
+    out_real = mixed[:rows_all]
+    out_imag = mixed[rows_all:]
     feature = jnp.log1p(out_real * out_real + out_imag * out_imag).astype(feat_scratch.dtype)
     for d in range(RADIX):
         rows = slice(d * rows_per, (d + 1) * rows_per)
@@ -193,7 +184,7 @@
             pl.BlockSpec((sub_n, sub_n), lambda i, dest: (0, 1)),
             pl.BlockSpec((rows, sub_n), lambda i, dest: (0, 0)),
             pl.BlockSpec((rows, sub_n), lambda i, dest: (0, 0)),
-            pl.BlockSpec((4, rows, rows), lambda i, dest: (0, 0, 0)),
+            pl.BlockSpec((1, 2 * rows, 2 * rows), lambda i, dest: (0, 0, 0)),
             pl.BlockSpec(memory_space=pl.ANY),
         ],
         out_specs=[

time: 172 us -> 170 us (0.988)
  Pallas kernels: 23 us -> 20.8 us
    pallas_call x1, Pallas kernels: 23 us -> 20.8 us  [spectrum_call(): pl.pallas_call(spectrum_kernel, grid_spec=grid_spec, out_shape=[jax.Shape...]
where the time goes in v6:
time: 170 us
  blocking collectives  60.7 us (36%)
  waiting for transfers between devices  25.8 us (15%)
  Pallas kernels  20.8 us (12%)
  local copies, waits for them, and re-layouts  19.6 us (12%)
  other arithmetic  16 us (9%)
  starting transfers between devices  12.8 us (8%)
  between operations  8.66 us (5%)
  matrix products  5.31 us (3%)
    all_to_all x1, blocking collectives, shards(): lax.all_to_all(outgoing, ('row', 'col'), split_axis=0, concat_axis=0, til...  60.7 us
    pallas_call x1, Pallas kernels, spectrum_call(): pl.pallas_call(spectrum_kernel, grid_spec=grid_spec, out_shape=[jax.Shape...  20.8 us
    ppermute x1, waiting for transfers between devices, from_behind_2(): return lax.ppermute(value, axis, pairs)  18 us
    reshape x1, local copies, waits for them, and re-layouts, shards(): swapped.reshape(2, sensors, per_device, sub_n, RADIX)  9.14 us
    all_to_all x1, waiting for transfers between devices, shards(): lax.all_to_all(demod, 'row', split_axis=2, concat_axis=3, tiled=True)  7.77 us
    all_to_all x1, starting transfers between devices, shards(): lax.all_to_all(demod, 'row', split_axis=2, concat_axis=3, tiled=True)  6.78 us
    all_to_all x1, local copies, waits for them, and re-layouts, shards(): lax.all_to_all(demod, 'row', split_axis=2, concat_axis=3, tiled=True)  5.9 us
    another operation x2, other arithmetic  5.61 us
  transfers between devices with their start and end apart: 3, of which 2 were waited for; matrix products, arithmetic and copies ran while one was open for 6% of the time, Pallas kernels for 0%

profile of v6, /device:TPU:0, one launch (start us, length us, event | category | flops | bytes accessed | tf_op | source)
XLA Modules:
  0.0 169.6 jit_solution(15501526218425217219)
XLA Ops:
  0.6 0.8 slice.82
  1.4 1.3 collective-permute-start
  2.9 0.6 fusion.72
  3.8 0.3 convert_subtract_fusion.1
  4.1 1.2 multiply_add_fusion
  5.3 1.3 fusion
  6.7 0.7 fusion.55
  7.5 0.8 fusion.35
  8.3 0.8 fusion.33
  9.0 0.8 add_bitcast_fusion
  9.9 0.4 fusion.40
  10.4 1.8 %copy.45 = bf16[2,4,256,256]{3,1,0,2:T(4,128)(2,1)} copy(bf16[2,4,256,256]{3,2,1,0:T(8,128)(2,1)S(1)} %pad_maximum_fusion.3) | data formatting | bytes 2097152 | tf_op jit(solution)/shard_map/stack | solution.py:256
  12.2 6.8 %all-to-all-start = ((bf16[2,4,256,256]{3,1,0,2:T(4,128)(2,1)}), bf16[2,4,256,256]{3,1,0,2:T(4,128)(2,1)S(1)}, u32[]{:S(2)}, u32[]{:S(2)}) async-start(bf16[2,4,256,256]{3,1,0,2:T(4,128)(2,1)} %copy.45), calls=%async_computation | async-start | bytes 2097152 | tf_op jit(solution)/shard_map/all_to_all | solution.py:257
  19.0 0.7 fusion.97
  27.6 7.8 %all-to-all-done = bf16[2,4,256,256]{3,1,0,2:T(4,128)(2,1)S(1)} async-done(((bf16[2,4,256,256]{3,1,0,2:T(4,128)(2,1)}), bf16[2,4,256,256]{3,1,0,2:T(4,128)(2,1)S(1)}, u32[]{:S(2)}, u32[]{:S(2)}) %all-to-all-start) | async-done | bytes 1048608 | tf_op jit(solution)/shard_map/all_to_all | solution.py:257
  35.4 5.9 %copy.46 = bf16[2,4,16,16,256]{3,4,2,1,0:T(8,128)(2,1)} copy(bf16[2,4,16,16,256]{4,1,0,3,2:T(4,128)(2,1)S(1)} %bitcast.96) | data formatting | bytes 2097152 | tf_op jit(solution)/shard_map/all_to_all | solution.py:257
  41.3 9.1 %copy.47 = bf16[2,4,16,512,8]{3,4,2,1,0:T(8,128)(2,1)S(1)} copy(bf16[2,4,16,512,8]{2,4,3,1,0:T(8,128)(2,1)} %bitcast.86) | data formatting | bytes 2097152 | tf_op jit(solution)/shard_map/reshape | solution.py:258
  50.5 4.8 %collective-permute-start.1 = (bf16[2,4,16,8,512]{4,3,2,1,0:T(8,128)(2,1)S(1)}, bf16[2,4,16,8,512]{4,3,2,1,0:T(8,128)(2,1)S(1)}, u32[]{:S(2)}, u32[]{:S(2)}) collective-permute-start(bf16[2,4,16,8,512]{4,3,2,1,0:T(8,128)(2,1)S(1)} %bitcast.88), channel_id=1, source_target_pairs={{0,127},{1,0},{2,1},{3,2},{4,3},{5,4},{6,5},{7,6},{8,7},{9,8},{10,... | collective-permute-start | bytes 3145736 | tf_op jit(solution)/shard_map/ppermute | solution.py:23
  55.4 0.2 select_reduce_fusion
  55.6 4.3 %sine_convert_fusion = (bf16[512,512]{1,0:T(8,128)(2,1)S(1)}, bf16[512,512]{1,0:T(8,128)(2,1)S(1)}) fusion(), kind=kLoop, calls=%fused_computation.79 | loop fusion | flops 4194304 | bytes 1048576 | tf_op jit(solution)/shard_map/convert.1
  60.1 18.0 %collective-permute-done.1 = bf16[2,4,16,8,512]{4,3,2,1,0:T(8,128)(2,1)S(1)} collective-permute-done((bf16[2,4,16,8,512]{4,3,2,1,0:T(8,128)(2,1)S(1)}, bf16[2,4,16,8,512]{4,3,2,1,0:T(8,128)(2,1)S(1)}, u32[]{:S(2)}, u32[]{:S(2)}) %collective-permute-start.1) | collective-permute-done | bytes 1048608 | tf_op jit(solution)/shard_map/ppermute | solution.py:23
  78.1 2.4 %fusion.24 = (f32[2,4,16,8,512]{4,3,2,1,0:T(8,128)S(1)}, f32[2,4,16,8,512]{4,3,2,1,0:T(8,128)S(1)}, f32[2,4,16,8,512]{4,3,2,1,0:T(8,128)S(1)}, f32[2,4,16,8,512]{4,3,2,1,0:T(8,128)S(1)}) fusion(s32[]{:T(128)S(6)} %select_n.129, bf16[2,4,16,8,512]{4,3,2,1,0:T(8,128)(2,1)S(1)} %bitcast.89, bf16[2,4,16,8,512]{4,3,2,1,0:T(8,128)(2,1)S(1)} %collective-permute-done.1, ...), kind=kLoop, calls=%fused_computation.66 | loop fusion | flops 4194304 | bytes 10485776 | tf_op jit(solution)/shard_map/convert_element_type | solution.py:270
  80.5 0.8 fusion.49
  81.3 0.8 fusion.48
  82.1 0.3 pad_maximum_fusion.1
  82.4 0.3 pad_maximum_fusion.2
  82.6 2.3 %pad_maximum_fusion.prod_ref = bf16[2,16,128,512]{3,2,1,0:T(8,128)(2,1)} fusion(bf16[1,16,128,512]{3,2,1,0:T(8,128)(2,1)S(1)} %bitcast.95, bf16[1,16,128,512]{3,2,1,0:T(8,128)(2,1)S(1)} %bitcast.94), kind=kLoop, calls=%fused_computation.1 | loop fusion | flops 2097152 | bytes 8388608 | tf_op jit(solution)/shard_map/stack | solution.py:273
  85.0 0.5 broadcast_in_dim.5.zero_ref
  85.5 0.4 copy-done.1
  85.9 20.8 %shard_map.68 = (bf16[2,4,4,16,4096]{4,3,2,1,0:T(8,128)(2,1)}, bf16[256,16,512]{2,1,0:T(8,128)(2,1)S(1)}) custom-call(s32[128]{0:T(128)S(1)} %multiply_add_fusion.1.dest_ref, bf16[2,16,128,512]{3,2,1,0:T(8,128)(2,1)} %pad_maximum_fusion.prod_ref, bf16[512,1024]{1,0:T(8,128)(2,1)S(1)} %pad_maximum_fusion.4.cos_ref.sin_ref, ...), custom_call_target="tpu_custom_call", output_to_operand_aliasing={{1}: (7, {})} | custom-call | flops 6442450944 | bytes 11534336 | tf_op jit(solution)/shard_map/pallas_call | solution.py:202
  106.6 60.7 %all_to_all.20 = bf16[128,32,512]{2,1,0:T(8,128)(2,1)S(1)} all-to-all(bf16[128,32,512]{2,1,0:T(8,128)(2,1)S(1)} %bitcast.85), channel_id=1, replica_groups=mesh['row'=16,'col'=8] {'row','col'}, dimensions={0} | all-to-all | bytes 8388608 | tf_op jit(solution)/shard_map/all_to_all | solution.py:293
  167.3 2.2 %convolution_convert_fusion = bf16[4096,128]{1,0:T(8,128)(2,1)} fusion(bf16[4096,512]{1,0:T(8,128)(2,1)S(1)} %bitcast.87, bf16[1,512,128]{2,1,0:T(8,128)(2,1)S(1)} %copy-done), kind=kOutput, calls=%fused_computation | convolution fusion | flops 537395200 | bytes 5373952 | tf_op jit(solution)/shard_map/dot_general | solution.py:294
  (27 shorter events, 1.3 us)
Async XLA Ops:
  0.6 166.7 %copy-start = (bf16[1,512,128]{2,1,0:T(8,128)(2,1)S(1)}, bf16[1,512,128]{2,1,0:T(8,128)(2,1)}, u32[]{:S(2)}) copy-start(bf16[1,512,128]{2,1,0:T(8,128)(2,1)} %param.8) | copy-start | bytes 393220
  1.4 6.0 %collective-permute-start = (bf16[4,3,512]{2,1,0:T(4,128)(2,1)S(1)}, bf16[4,3,512]{2,1,0:T(4,128)(2,1)S(1)}, u32[]{:S(2)}, u32[]{:S(2)}) collective-permute-start(bf16[4,3,512]{2,1,0:T(4,128)(2,1)S(1)} %slice.82), channel_id=1, source_target_pairs={{8,0},{16,8},{24,16},{32,24},{40,32},{48,40},{56,48},{64,56},{72,6... | collective-permute-start | bytes 36872 | tf_op jit(solution)/shard_map/ppermute | solution.py:17
  5.3 1.3 copy-start.2
  10.4 8.6 %copy-start.3 = (s32[2,2]{1,0:T(2,128)S(1)}, s32[2,2]{1,0:T(2,128)}, u32[]{:S(2)}) copy-start(s32[2,2]{1,0:T(2,128)} %param.6) | copy-start | bytes 52
  10.4 14.4 %copy-start.4 = (s32[128,1]{0,1:T(1,128)S(1)}, s32[128,1]{0,1:T(1,128)}, u32[]{:S(2)}) copy-start(s32[128,1]{0,1:T(1,128)} %param.7) | copy-start | bytes 1540
  12.2 23.2 %all-to-all-start = ((bf16[2,4,256,256]{3,1,0,2:T(4,128)(2,1)}), bf16[2,4,256,256]{3,1,0,2:T(4,128)(2,1)S(1)}, u32[]{:S(2)}, u32[]{:S(2)}) async-start(bf16[2,4,256,256]{3,1,0,2:T(4,128)(2,1)} %copy.45), calls=%async_computation | async-start | bytes 2097152 | tf_op jit(solution)/shard_map/all_to_all | solution.py:257
  50.5 27.7 %collective-permute-start.1 = (bf16[2,4,16,8,512]{4,3,2,1,0:T(8,128)(2,1)S(1)}, bf16[2,4,16,8,512]{4,3,2,1,0:T(8,128)(2,1)S(1)}, u32[]{:S(2)}, u32[]{:S(2)}) collective-permute-start(bf16[2,4,16,8,512]{4,3,2,1,0:T(8,128)(2,1)S(1)} %bitcast.88), channel_id=1, source_target_pairs={{0,127},{1,0},{2,1},{3,2},{4,3},{5,4},{6,5},{7,6},{8,7},{9,8},{10,... | collective-permute-start | bytes 3145736 | tf_op jit(solution)/shard_map/ppermute | solution.py:23
  85.0 0.9 copy-start.1

commit v7 on v6

--- a/solution.py
+++ b/solution.py
@@ -255,24 +255,32 @@
     )
     demod = jnp.stack([real_part, imag_part]).astype(jnp.bfloat16)
     swapped = lax.all_to_all(demod, "row", split_axis=2, concat_axis=3, tiled=True)
-    ordered = swapped.reshape(2, sensors, per_device, sub_n, RADIX).transpose(0, 1, 2, 4, 3)
-    above = from_behind_2(ordered, ("row", "col"), -1)
-    extended = jnp.concatenate([ordered, above], axis=2)
-    own_real = ordered[0].astype(jnp.float32)
-    own_imag = ordered[1].astype(jnp.float32)
-    prod_real = []
-    prod_imag = []
-    for wheel in range(orders.shape[0]):
-        for order_at in range(orders.shape[1]):
-            partner = lax.dynamic_slice_in_dim(
-                extended, orders[wheel, order_at], per_device, axis=2
+    halves = 2
+    part = sensors // halves
+    pieces = []
+    for half in range(halves):
+        ordered = swapped[:, half * part : (half + 1) * part]
+        ordered = ordered.reshape(2, part, per_device, sub_n, RADIX).transpose(0, 1, 2, 4, 3)
+        above = from_behind_2(ordered, ("row", "col"), -1)
+        extended = jnp.concatenate([ordered, above], axis=2)
+        own_real = ordered[0].astype(jnp.float32)
+        own_imag = ordered[1].astype(jnp.float32)
+        prod_real = []
+        prod_imag = []
+        for wheel in range(orders.shape[0]):
+            for order_at in range(orders.shape[1]):
+                partner = lax.dynamic_slice_in_dim(
+                    extended, orders[wheel, order_at], per_device, axis=2
+                )
+                partner = partner.astype(jnp.float32)
+                prod_real.append(own_real * partner[0] + own_imag * partner[1])
+                prod_imag.append(own_imag * partner[0] - own_real * partner[1])
+        pieces.append(
+            jnp.stack([jnp.stack(prod_real, axis=1), jnp.stack(prod_imag, axis=1)]).astype(
+                jnp.bfloat16
             )
-            partner = partner.astype(jnp.float32)
-            prod_real.append(own_real * partner[0] + own_imag * partner[1])
-            prod_imag.append(own_imag * partner[0] - own_real * partner[1])
-    products = jnp.stack([jnp.stack(prod_real, axis=1), jnp.stack(prod_imag, axis=1)]).astype(
-        jnp.bfloat16
-    )
+        )
+    products = jnp.concatenate(pieces, axis=1)
     tiles_dev = sensors * combos * RADIX
     capacity = max(2, 2 * tiles_dev // devices_n)
     owner_ids = owners[:, 0]

time: 170 us -> 162 us (0.953)
  waiting for transfers between devices: 25.8 us -> 16.1 us
  local copies, waits for them, and re-layouts: 19.6 us -> 21.7 us
  blocking collectives: 60.7 us -> 58.8 us
    slice x0 -> x3, local copies, waits for them, and re-layouts: none -> 6.17 us  [shards(): ordered = swapped[:, half * part:(half + 1) * part]]
    ppermute x1 -> x2, waiting for transfers between devices: 18 us -> 12.9 us  [from_behind_2(): return lax.ppermute(value, axis, pairs)]
    all_to_all x1 -> x2, local copies, waits for them, and re-layouts: 5.9 us -> 1.11 us  [shards(): lax.all_to_all(demod, 'row', split_axis=2, concat_axis=3, tiled=True)]
    all_to_all x1, waiting for transfers between devices: 7.77 us -> 3.22 us  [shards(): lax.all_to_all(demod, 'row', split_axis=2, concat_axis=3, tiled=True)]
    concatenate x0 -> x1, other arithmetic: none -> 2.19 us  [shards(): products = jnp.concatenate(pieces, axis=1)]
    all_to_all x1, blocking collectives: 60.7 us -> 58.8 us  [shards(): lax.all_to_all(outgoing, ('row', 'col'), split_axis=0, concat_axis=0, til...]
    another operation x1 -> x4, other arithmetic: 2.33 us -> 0.53 us  [shards(): jnp.stack([jnp.stack(prod_real, axis=1), jnp.stack(prod_imag, axis=1)])]
    convert_element_type x1 -> x2, other arithmetic: 2.35 us -> 3.53 us  [shards(): partner = partner.astype(jnp.float32)]
  transfers between devices with their start and end apart: 3 -> 4, of which waited for: 2 -> 3; matrix products, arithmetic and copies ran while one was open for 6% -> 13% of each run, Pallas kernels for 0% -> 0%
where the time goes in v7:
time: 162 us
  blocking collectives  58.8 us (36%)
  local copies, waits for them, and re-layouts  21.7 us (13%)
  Pallas kernels  20.8 us (13%)
  other arithmetic  16.9 us (10%)
  waiting for transfers between devices  16.1 us (10%)
  starting transfers between devices  13.5 us (8%)
  between operations  8.56 us (5%)
  matrix products  5.31 us (3%)
    all_to_all x1, blocking collectives, shards(): lax.all_to_all(outgoing, ('row', 'col'), split_axis=0, concat_axis=0, til...  58.8 us
    pallas_call x1, Pallas kernels, spectrum_call(): pl.pallas_call(spectrum_kernel, grid_spec=grid_spec, out_shape=[jax.Shape...  20.8 us
    ppermute x2, waiting for transfers between devices, from_behind_2(): return lax.ppermute(value, axis, pairs)  12.9 us
    reshape x2, local copies, waits for them, and re-layouts, shards(): ordered.reshape(2, part, per_device, sub_n, RADIX).transpose(0, 1, 2, 4, 3)  9.87 us
    all_to_all x1, starting transfers between devices, shards(): lax.all_to_all(demod, 'row', split_axis=2, concat_axis=3, tiled=True)  6.78 us
    slice x3, local copies, waits for them, and re-layouts, shards(): ordered = swapped[:, half * part:(half + 1) * part]  6.17 us
    another operation x2, other arithmetic  5.61 us
    ppermute x2, starting transfers between devices, from_behind_2(): return lax.ppermute(value, axis, pairs)  5.47 us
  transfers between devices with their start and end apart: 4, of which 3 were waited for; matrix products, arithmetic and copies ran while one was open for 13% of the time, Pallas kernels for 0%

profile of v7, /device:TPU:0, one launch (start us, length us, event | category | flops | bytes accessed | tf_op | source)
XLA Modules:
  0.0 161.6 jit_solution(7423923913576229794)
XLA Ops:
  0.6 0.8 slice.130
  1.4 1.3 collective-permute-start
  2.9 0.6 fusion.104
  4.1 1.2 multiply_add_fusion
  5.3 1.3 fusion
  6.7 0.7 fusion.71
  7.5 0.8 fusion.11
  8.3 0.8 fusion.9
  9.0 0.8 add_bitcast_fusion
  10.4 1.8 %copy.78 = bf16[2,4,256,256]{3,1,0,2:T(4,128)(2,1)} copy(bf16[2,4,256,256]{3,2,1,0:T(8,128)(2,1)S(1)} %pad_maximum_fusion) | data formatting | bytes 2097152 | tf_op jit(solution)/shard_map/stack | solution.py:256
  12.2 6.8 %all-to-all-start = ((bf16[2,4,256,256]{3,1,0,2:T(4,128)(2,1)}), bf16[2,4,256,256]{3,1,0,2:T(4,128)(2,1)S(1)}, u32[]{:S(2)}, u32[]{:S(2)}) async-start(bf16[2,4,256,256]{3,1,0,2:T(4,128)(2,1)} %copy.78), calls=%async_computation | async-start | bytes 2097152 | tf_op jit(solution)/shard_map/all_to_all | solution.py:257
  19.0 0.7 fusion.130
  27.7 4.3 %sine_convert_fusion = (bf16[512,512]{1,0:T(8,128)(2,1)S(1)}, bf16[512,512]{1,0:T(8,128)(2,1)S(1)}) fusion(), kind=kLoop, calls=%fused_computation.82 | loop fusion | flops 4194304 | bytes 1048576 | tf_op jit(solution)/shard_map/convert.1
  32.2 3.2 %all-to-all-done = bf16[2,4,256,256]{3,1,0,2:T(4,128)(2,1)S(1)} async-done(((bf16[2,4,256,256]{3,1,0,2:T(4,128)(2,1)}), bf16[2,4,256,256]{3,1,0,2:T(4,128)(2,1)S(1)}, u32[]{:S(2)}, u32[]{:S(2)}) %all-to-all-start) | async-done | bytes 1048608 | tf_op jit(solution)/shard_map/all_to_all | solution.py:257
  35.4 0.6 copy.105
  36.0 0.5 all_to_all.19
  36.6 3.0 %copy.80 = bf16[2,2,16,4096]{2,3,1,0:T(8,128)(2,1)} copy(bf16[2,2,16,4096]{3,2,1,0:T(8,128)(2,1)S(1)} %get-tuple-element.28) | data formatting | bytes 1048576 | tf_op jit(solution)/shard_map/slice | solution.py:262
  39.7 4.9 %copy.81 = bf16[2,2,16,512,8]{3,4,2,1,0:T(8,128)(2,1)S(1)} copy(bf16[2,2,16,512,8]{2,4,3,1,0:T(8,128)(2,1)} %bitcast.131) | data formatting | bytes 1048576 | tf_op jit(solution)/shard_map/reshape | solution.py:263
  44.6 4.9 %collective-permute-start.1 = (bf16[2,2,16,8,512]{4,3,2,1,0:T(8,128)(2,1)S(1)}, bf16[2,2,16,8,512]{4,3,2,1,0:T(8,128)(2,1)}, u32[]{:S(2)}, u32[]{:S(2)}) collective-permute-start(bf16[2,2,16,8,512]{4,3,2,1,0:T(8,128)(2,1)S(1)} %bitcast.137), channel_id=1, source_target_pairs={{0,127},{1,0},{2,1},{3,2},{4,3},{5,4},{6,5},{7,6},{8,7},{9,8},{10,... | collective-permute-start | bytes 1572872 | tf_op jit(solution)/shard_map/ppermute | solution.py:23
  49.7 3.0 %copy.90 = bf16[2,2,16,4096]{2,3,1,0:T(8,128)(2,1)} copy(bf16[2,2,16,4096]{3,2,1,0:T(8,128)(2,1)S(1)} %get-tuple-element.29) | data formatting | bytes 1048576 | tf_op jit(solution)/shard_map/slice | solution.py:262
  52.7 4.9 %copy.91 = bf16[2,2,16,512,8]{3,4,2,1,0:T(8,128)(2,1)S(1)} copy(bf16[2,2,16,512,8]{2,4,3,1,0:T(8,128)(2,1)} %bitcast.132) | data formatting | bytes 1048576 | tf_op jit(solution)/shard_map/reshape | solution.py:263
  57.7 0.5 collective-permute-start.2
  58.2 3.3 %collective-permute-done.1 = bf16[2,2,16,8,512]{4,3,2,1,0:T(8,128)(2,1)} collective-permute-done((bf16[2,2,16,8,512]{4,3,2,1,0:T(8,128)(2,1)S(1)}, bf16[2,2,16,8,512]{4,3,2,1,0:T(8,128)(2,1)}, u32[]{:S(2)}, u32[]{:S(2)}) %collective-permute-start.1) | collective-permute-done | bytes 524320 | tf_op jit(solution)/shard_map/ppermute | solution.py:23
  61.5 2.3 %fusion.61 = (f32[2,2,16,8,512]{4,3,2,1,0:T(8,128)S(1)}, f32[2,2,16,8,512]{4,3,2,1,0:T(8,128)S(1)}, f32[2,2,16,8,512]{4,3,2,1,0:T(8,128)S(1)}, f32[2,2,16,8,512]{4,3,2,1,0:T(8,128)S(1)}) fusion(s32[]{:T(128)S(6)} %select_n.133, bf16[2,2,16,8,512]{4,3,2,1,0:T(8,128)(2,1)S(1)} %bitcast.138, bf16[2,2,16,8,512]{4,3,2,1,0:T(8,128)(2,1)} %collective-permute-done.1, ...), kind=kLoop, calls=%fused_computation.134 | loop fusion | flops 2097152 | bytes 5242896 | tf_op jit(solution)/shard_map/convert_element_type | solution.py:275
  64.6 9.6 %collective-permute-done.2 = bf16[2,2,16,8,512]{4,3,2,1,0:T(8,128)(2,1)S(1)} collective-permute-done((bf16[2,2,16,8,512]{4,3,2,1,0:T(8,128)(2,1)S(1)}, bf16[2,2,16,8,512]{4,3,2,1,0:T(8,128)(2,1)S(1)}, u32[]{:S(2)}, u32[]{:S(2)}) %collective-permute-start.2) | collective-permute-done | bytes 524320 | tf_op jit(solution)/shard_map/ppermute | solution.py:23
  74.2 1.3 fusion.53
  75.8 0.4 fusion.86
  76.8 2.2 %maximum_maximum_fusion = bf16[2,4,4,16,8,512]{5,4,3,2,1,0:T(8,128)(2,1)} fusion(bf16[1,2,4,16,8,512]{5,4,3,2,1,0:T(8,128)(2,1)S(1)} %maximum_bitcast_fusion.3, bf16[1,2,4,16,8,512]{5,4,3,2,1,0:T(8,128)(2,1)S(1)} %maximum_bitcast_fusion.2, bf16[1,2,4,16,8,512]{5,4,3,2,1,0:T(8,128)(2,1)S(1)} %maximum_bitcast_fusion.1, ...), kind=kLoop, calls=%fused_computation.1 | loop fusion | flops 6291456 | bytes 8388608 | tf_op jit(solution)/shard_map/concatenate | solution.py:283
  79.0 0.5 broadcast_in_dim.5.zero_ref
  79.9 20.8 %shard_map.68 = (bf16[2,4,4,16,4096]{4,3,2,1,0:T(8,128)(2,1)}, bf16[256,16,512]{2,1,0:T(8,128)(2,1)S(1)}) custom-call(s32[128]{0:T(128)S(1)} %multiply_add_fusion.1.dest_ref, bf16[2,16,128,512]{3,2,1,0:T(8,128)(2,1)} %bitcast.143, bf16[512,1024]{1,0:T(8,128)(2,1)S(1)} %pad_maximum_fusion.1.cos_ref.sin_ref, ...), custom_call_target="tpu_custom_call", output_to_operand_aliasing={{1}: (7, {})} | custom-call | flops 6442450944 | bytes 11534336 | tf_op jit(solution)/shard_map/pallas_call | solution.py:202
  100.7 58.8 %all_to_all.23 = bf16[128,32,512]{2,1,0:T(8,128)(2,1)S(1)} all-to-all(bf16[128,32,512]{2,1,0:T(8,128)(2,1)S(1)} %bitcast.129), channel_id=1, replica_groups=mesh['row'=16,'col'=8] {'row','col'}, dimensions={0} | all-to-all | bytes 8388608 | tf_op jit(solution)/shard_map/all_to_all | solution.py:301
  159.4 2.2 %convolution_convert_fusion = bf16[4096,128]{1,0:T(8,128)(2,1)} fusion(bf16[4096,512]{1,0:T(8,128)(2,1)S(1)} %bitcast.130, bf16[1,512,128]{2,1,0:T(8,128)(2,1)S(1)} %copy-done), kind=kOutput, calls=%fused_computation | convolution fusion | flops 537395200 | bytes 5373952 | tf_op jit(solution)/shard_map/dot_general | solution.py:302
  (39 shorter events, 4.2 us)
Async XLA Ops:
  0.6 158.8 %copy-start = (bf16[1,512,128]{2,1,0:T(8,128)(2,1)S(1)}, bf16[1,512,128]{2,1,0:T(8,128)(2,1)}, u32[]{:S(2)}) copy-start(bf16[1,512,128]{2,1,0:T(8,128)(2,1)} %param.8) | copy-start | bytes 393220
  1.4 6.0 %collective-permute-start = (bf16[4,3,512]{2,1,0:T(4,128)(2,1)S(1)}, bf16[4,3,512]{2,1,0:T(4,128)(2,1)S(1)}, u32[]{:S(2)}, u32[]{:S(2)}) collective-permute-start(bf16[4,3,512]{2,1,0:T(4,128)(2,1)S(1)} %slice.130), channel_id=1, source_target_pairs={{8,0},{16,8},{24,16},{32,24},{40,32},{48,40},{56,48},{64,56},{72,6... | collective-permute-start | bytes 36872 | tf_op jit(solution)/shard_map/ppermute | solution.py:17
  5.3 1.3 copy-start.2
  10.4 8.6 %copy-start.3 = (s32[2,2]{1,0:T(2,128)S(1)}, s32[2,2]{1,0:T(2,128)}, u32[]{:S(2)}) copy-start(s32[2,2]{1,0:T(2,128)} %param.6) | copy-start | bytes 52
  10.4 14.3 %copy-start.4 = (s32[128,1]{0,1:T(1,128)S(1)}, s32[128,1]{0,1:T(1,128)}, u32[]{:S(2)}) copy-start(s32[128,1]{0,1:T(1,128)} %param.7) | copy-start | bytes 1540
  12.2 23.2 %all-to-all-start = ((bf16[2,4,256,256]{3,1,0,2:T(4,128)(2,1)}), bf16[2,4,256,256]{3,1,0,2:T(4,128)(2,1)S(1)}, u32[]{:S(2)}, u32[]{:S(2)}) async-start(bf16[2,4,256,256]{3,1,0,2:T(4,128)(2,1)} %copy.78), calls=%async_computation | async-start | bytes 2097152 | tf_op jit(solution)/shard_map/all_to_all | solution.py:257
  44.6 16.9 %collective-permute-start.1 = (bf16[2,2,16,8,512]{4,3,2,1,0:T(8,128)(2,1)S(1)}, bf16[2,2,16,8,512]{4,3,2,1,0:T(8,128)(2,1)}, u32[]{:S(2)}, u32[]{:S(2)}) collective-permute-start(bf16[2,2,16,8,512]{4,3,2,1,0:T(8,128)(2,1)S(1)} %bitcast.137), channel_id=1, source_target_pairs={{0,127},{1,0},{2,1},{3,2},{4,3},{5,4},{6,5},{7,6},{8,7},{9,8},{10,... | collective-permute-start | bytes 1572872 | tf_op jit(solution)/shard_map/ppermute | solution.py:23
  57.7 16.5 %collective-permute-start.2 = (bf16[2,2,16,8,512]{4,3,2,1,0:T(8,128)(2,1)S(1)}, bf16[2,2,16,8,512]{4,3,2,1,0:T(8,128)(2,1)S(1)}, u32[]{:S(2)}, u32[]{:S(2)}) collective-permute-start(bf16[2,2,16,8,512]{4,3,2,1,0:T(8,128)(2,1)S(1)} %bitcast.133), channel_id=1, source_target_pairs={{0,127},{1,0},{2,1},{3,2},{4,3},{5,4},{6,5},{7,6},{8,7},{9,8},{10,... | collective-permute-start | bytes 1572872 | tf_op jit(solution)/shard_map/ppermute | solution.py:23
  79.0 0.9 copy-start.1

commit v8 on v7

--- a/solution.py
+++ b/solution.py
@@ -255,7 +255,7 @@
     )
     demod = jnp.stack([real_part, imag_part]).astype(jnp.bfloat16)
     swapped = lax.all_to_all(demod, "row", split_axis=2, concat_axis=3, tiled=True)
-    halves = 2
+    halves = 4
     part = sensors // halves
     pieces = []
     for half in range(halves):

time: 162 us -> 168 us (1.037)
  starting transfers between devices: 13.5 us -> 16.6 us
  local copies, waits for them, and re-layouts: 21.7 us -> 24.5 us
  other arithmetic: 16.9 us -> 19.6 us
  waiting for transfers between devices: 16.1 us -> 14.3 us
    ppermute x2 -> x4, waiting for transfers between devices: 12.9 us -> 4.11 us  [from_behind_2(): return lax.ppermute(value, axis, pairs)]
    all_to_all x1, waiting for transfers between devices: 3.22 us -> 10.1 us  [shards(): lax.all_to_all(demod, 'row', split_axis=2, concat_axis=3, tiled=True)]
    ppermute x2 -> x4, starting transfers between devices: 5.47 us -> 8.5 us  [from_behind_2(): return lax.ppermute(value, axis, pairs)]
    slice x3 -> x5, local copies, waits for them, and re-layouts: 6.17 us -> 7.93 us  [shards(): ordered = swapped[:, half * part:(half + 1) * part]]
    another operation x2 -> x10, other arithmetic: 5.61 us -> 7.07 us
    convert_element_type x2 -> x4, other arithmetic: 3.53 us -> 4.93 us  [shards(): partner = partner.astype(jnp.float32)]
    reshape x2 -> x4, local copies, waits for them, and re-layouts: 9.87 us -> 10.2 us  [shards(): ordered.reshape(2, part, per_device, sub_n, RADIX).transpose(0, 1, 2, 4, 3)]
  transfers between devices with their start and end apart: 4 -> 6, of which waited for: 3 -> 2; matrix products, arithmetic and copies ran while one was open for 13% -> 19% of each run, Pallas kernels for 0% -> 0%
where the time goes in v8:
time: 168 us
  blocking collectives  58.3 us (35%)
  local copies, waits for them, and re-layouts  24.5 us (15%)
  Pallas kernels  20.8 us (12%)
  other arithmetic  19.6 us (12%)
  starting transfers between devices  16.6 us (10%)
  waiting for transfers between devices  14.3 us (9%)
  between operations  8.6 us (5%)
  matrix products  5.33 us (3%)
    all_to_all x1, blocking collectives, shards(): lax.all_to_all(outgoing, ('row', 'col'), split_axis=0, concat_axis=0, til...  58.3 us
    pallas_call x1, Pallas kernels, spectrum_call(): pl.pallas_call(spectrum_kernel, grid_spec=grid_spec, out_shape=[jax.Shape...  20.8 us
    reshape x4, local copies, waits for them, and re-layouts, shards(): ordered.reshape(2, part, per_device, sub_n, RADIX).transpose(0, 1, 2, 4, 3)  10.2 us
    all_to_all x1, waiting for transfers between devices, shards(): lax.all_to_all(demod, 'row', split_axis=2, concat_axis=3, tiled=True)  10.1 us
    ppermute x4, starting transfers between devices, from_behind_2(): return lax.ppermute(value, axis, pairs)  8.5 us
    slice x5, local copies, waits for them, and re-layouts, shards(): ordered = swapped[:, half * part:(half + 1) * part]  7.93 us
    another operation x10, other arithmetic  7.07 us
    all_to_all x1, starting transfers between devices, shards(): lax.all_to_all(demod, 'row', split_axis=2, concat_axis=3, tiled=True)  6.78 us
  transfers between devices with their start and end apart: 6, of which 2 were waited for; matrix products, arithmetic and copies ran while one was open for 19% of the time, Pallas kernels for 0%

profile of v8, /device:TPU:0, one launch (start us, length us, event | category | flops | bytes accessed | tf_op | source)
XLA Modules:
  0.0 167.9 jit_solution(15892046387917953954)
XLA Ops:
  0.6 0.8 slice.220
  1.4 1.3 collective-permute-start
  4.1 1.2 multiply_add_fusion
  5.3 1.3 fusion
  6.7 0.7 fusion.23
  7.5 0.8 fusion.11
  8.3 0.8 fusion.9
  9.1 0.8 add_bitcast_fusion
  10.4 1.8 %copy.142 = bf16[2,4,256,256]{3,1,0,2:T(4,128)(2,1)} copy(bf16[2,4,256,256]{3,2,1,0:T(8,128)(2,1)S(1)} %pad_maximum_fusion) | data formatting | bytes 2097152 | tf_op jit(solution)/shard_map/stack | solution.py:256
  12.2 6.8 %all-to-all-start = ((bf16[2,4,256,256]{3,1,0,2:T(4,128)(2,1)}), bf16[2,4,256,256]{3,1,0,2:T(4,128)(2,1)S(1)}, u32[]{:S(2)}, u32[]{:S(2)}) async-start(bf16[2,4,256,256]{3,1,0,2:T(4,128)(2,1)} %copy.142), calls=%async_computation | async-start | bytes 2097152 | tf_op jit(solution)/shard_map/all_to_all | solution.py:257
  20.8 4.3 %sine_convert_fusion = (bf16[512,512]{1,0:T(8,128)(2,1)S(1)}, bf16[512,512]{1,0:T(8,128)(2,1)S(1)}) fusion(), kind=kLoop, calls=%fused_computation.30 | loop fusion | flops 4194304 | bytes 1048576 | tf_op jit(solution)/shard_map/convert.1
  25.3 10.1 %all-to-all-done = bf16[2,4,256,256]{3,1,0,2:T(4,128)(2,1)S(1)} async-done(((bf16[2,4,256,256]{3,1,0,2:T(4,128)(2,1)}), bf16[2,4,256,256]{3,1,0,2:T(4,128)(2,1)S(1)}, u32[]{:S(2)}, u32[]{:S(2)}) %all-to-all-start) | async-done | bytes 1048608 | tf_op jit(solution)/shard_map/all_to_all | solution.py:257
  36.5 0.9 fusion.161
  37.4 1.0 copy.144
  38.4 1.7 %copy.145 = bf16[2,1,16,512,8]{3,4,2,1,0:T(8,128)(2,1)S(1)} copy(bf16[2,1,16,512,8]{2,4,3,0,1:T(8,128)(2,1)S(1)} %bitcast.79) | data formatting | bytes 524288 | tf_op jit(solution)/shard_map/reshape | solution.py:263
  40.1 4.8 %collective-permute-start.1 = (bf16[2,1,16,8,512]{4,3,2,1,0:T(8,128)(2,1)S(1)}, bf16[2,1,16,8,512]{4,3,2,1,0:T(8,128)(2,1)S(1)}, u32[]{:S(2)}, u32[]{:S(2)}) collective-permute-start(bf16[2,1,16,8,512]{4,3,2,1,0:T(8,128)(2,1)S(1)} %bitcast.89), channel_id=1, source_target_pairs={{0,127},{1,0},{2,1},{3,2},{4,3},{5,4},{6,5},{7,6},{8,7},{9,8},{10,... | collective-permute-start | bytes 786440 | tf_op jit(solution)/shard_map/ppermute | solution.py:23
  53.1 0.8 broadcast_bitcast_fusion
  53.9 2.6 %copy.150 = bf16[2,1,16,4096]{2,3,0,1:T(8,128)(2,1)} copy(bf16[2,1,16,4096]{3,2,1,0:T(8,128)(2,1)} %get-tuple-element.9) | data formatting | bytes 524288 | tf_op jit(solution)/shard_map/slice | solution.py:262
  56.6 2.8 %copy.151 = bf16[2,1,16,512,8]{3,4,2,1,0:T(8,128)(2,1)S(1)} copy(bf16[2,1,16,512,8]{2,4,3,0,1:T(8,128)(2,1)} %bitcast.80) | data formatting | bytes 524288 | tf_op jit(solution)/shard_map/reshape | solution.py:263
  59.7 1.7 %copy.148 = bf16[2,1,16,4096]{2,3,0,1:T(8,128)(2,1)} copy(bf16[2,1,16,4096]{3,2,1,0:T(8,128)(2,1)S(1)} %copy-done.4) | data formatting | bytes 524288 | tf_op jit(solution)/shard_map/slice | solution.py:262
  61.4 2.8 %copy.149 = bf16[2,1,16,512,8]{3,4,2,1,0:T(8,128)(2,1)S(1)} copy(bf16[2,1,16,512,8]{2,4,3,0,1:T(8,128)(2,1)} %bitcast.81) | data formatting | bytes 524288 | tf_op jit(solution)/shard_map/reshape | solution.py:263
  64.3 3.0 %collective-permute-start.3 = (bf16[2,1,16,8,512]{4,3,2,1,0:T(8,128)(2,1)S(1)}, bf16[2,1,16,8,512]{4,3,2,1,0:T(8,128)(2,1)}, u32[]{:S(2)}, u32[]{:S(2)}) collective-permute-start(bf16[2,1,16,8,512]{4,3,2,1,0:T(8,128)(2,1)S(1)} %bitcast.93), channel_id=1, source_target_pairs={{0,127},{1,0},{2,1},{3,2},{4,3},{5,4},{6,5},{7,6},{8,7},{9,8},{10,... | collective-permute-start | bytes 786440 | tf_op jit(solution)/shard_map/ppermute | solution.py:23
  67.3 1.7 %copy.146 = bf16[2,1,16,4096]{2,3,0,1:T(8,128)(2,1)} copy(bf16[2,1,16,4096]{3,2,1,0:T(8,128)(2,1)S(1)} %copy-done.3) | data formatting | bytes 524288 | tf_op jit(solution)/shard_map/slice | solution.py:262
  69.0 2.8 %copy.147 = bf16[2,1,16,512,8]{3,4,2,1,0:T(8,128)(2,1)S(1)} copy(bf16[2,1,16,512,8]{2,4,3,0,1:T(8,128)(2,1)} %bitcast.82) | data formatting | bytes 524288 | tf_op jit(solution)/shard_map/reshape | solution.py:263
  72.2 0.7 fusion.123
  73.3 1.8 %fusion.99 = (f32[2,1,16,8,512]{4,3,2,1,0:T(8,128)S(1)}, f32[2,1,16,8,512]{4,3,2,1,0:T(8,128)S(1)}, f32[2,1,16,8,512]{4,3,2,1,0:T(8,128)S(1)}, f32[2,1,16,8,512]{4,3,2,1,0:T(8,128)S(1)}) fusion(s32[]{:T(128)S(6)} %select_n.141, bf16[2,1,16,8,512]{4,3,2,1,0:T(8,128)(2,1)S(1)} %bitcast.98, bf16[2,1,16,8,512]{4,3,2,1,0:T(8,128)(2,1)} %collective-permute-done.4, ...), kind=kLoop, calls=%fused_computation.226 | loop fusion | flops 1048576 | bytes 2621456 | tf_op jit(solution)/shard_map/convert_element_type | solution.py:275
  75.5 1.7 %fusion.107 = (f32[2,1,16,8,512]{4,3,2,1,0:T(8,128)S(1)}, f32[2,1,16,8,512]{4,3,2,1,0:T(8,128)S(1)}, f32[2,1,16,8,512]{4,3,2,1,0:T(8,128)S(1)}, f32[2,1,16,8,512]{4,3,2,1,0:T(8,128)S(1)}) fusion(s32[]{:T(128)S(6)} %select_n.141, bf16[2,1,16,8,512]{4,3,2,1,0:T(8,128)(2,1)S(1)} %bitcast.94, bf16[2,1,16,8,512]{4,3,2,1,0:T(8,128)(2,1)} %collective-permute-done.3, ...), kind=kLoop, calls=%fused_computation.234 | loop fusion | flops 1048576 | bytes 2621456 | tf_op jit(solution)/shard_map/convert_element_type | solution.py:275
  77.6 4.1 %collective-permute-done.2 = bf16[2,1,16,8,512]{4,3,2,1,0:T(8,128)(2,1)S(1)} collective-permute-done((bf16[2,1,16,8,512]{4,3,2,1,0:T(8,128)(2,1)S(1)}, bf16[2,1,16,8,512]{4,3,2,1,0:T(8,128)(2,1)S(1)}, u32[]{:S(2)}, u32[]{:S(2)}) %collective-permute-start.2) | collective-permute-done | bytes 262176 | tf_op jit(solution)/shard_map/ppermute | solution.py:23
  83.4 2.2 %maximum_maximum_fusion = bf16[2,4,4,16,8,512]{5,4,3,2,1,0:T(8,128)(2,1)} fusion(bf16[1,1,4,16,8,512]{5,4,3,2,1,0:T(8,128)(2,1)S(1)} %maximum_bitcast_fusion.7, bf16[1,1,4,16,8,512]{5,4,3,2,1,0:T(8,128)(2,1)S(1)} %maximum_bitcast_fusion.6, bf16[1,1,4,16,8,512]{5,4,3,2,1,0:T(8,128)(2,1)S(1)} %maximum_bitcast_fusion.5, ...), kind=kLoop, calls=%fused_computation.1 | loop fusion | flops 14680064 | bytes 8388608 | tf_op jit(solution)/shard_map/concatenate | solution.py:283
  86.5 20.8 %shard_map.68 = (bf16[2,4,4,16,4096]{4,3,2,1,0:T(8,128)(2,1)}, bf16[256,16,512]{2,1,0:T(8,128)(2,1)S(1)}) custom-call(s32[128]{0:T(128)S(1)} %multiply_add_fusion.1.dest_ref, bf16[2,16,128,512]{3,2,1,0:T(8,128)(2,1)} %bitcast.101, bf16[512,1024]{1,0:T(8,128)(2,1)S(1)} %pad_maximum_fusion.1.cos_ref.sin_ref, ...), custom_call_target="tpu_custom_call", output_to_operand_aliasing={{1}: (7, {})} | custom-call | flops 6442450944 | bytes 11534336 | tf_op jit(solution)/shard_map/pallas_call | solution.py:202
  107.4 58.3 %all_to_all.23 = bf16[128,32,512]{2,1,0:T(8,128)(2,1)S(1)} all-to-all(bf16[128,32,512]{2,1,0:T(8,128)(2,1)S(1)} %bitcast.77), channel_id=1, replica_groups=mesh['row'=16,'col'=8] {'row','col'}, dimensions={0} | all-to-all | bytes 8388608 | tf_op jit(solution)/shard_map/all_to_all | solution.py:301
  165.6 2.2 %convolution_convert_fusion = bf16[4096,128]{1,0:T(8,128)(2,1)} fusion(bf16[4096,512]{1,0:T(8,128)(2,1)S(1)} %bitcast.78, bf16[1,512,128]{2,1,0:T(8,128)(2,1)S(1)} %copy-done), kind=kOutput, calls=%fused_computation | convolution fusion | flops 537395200 | bytes 5373952 | tf_op jit(solution)/shard_map/dot_general | solution.py:302
  (61 shorter events, 9.9 us)
Async XLA Ops:
  0.6 165.0 %copy-start = (bf16[1,512,128]{2,1,0:T(8,128)(2,1)S(1)}, bf16[1,512,128]{2,1,0:T(8,128)(2,1)}, u32[]{:S(2)}) copy-start(bf16[1,512,128]{2,1,0:T(8,128)(2,1)} %param.8) | copy-start | bytes 393220
  1.4 6.0 %collective-permute-start = (bf16[4,3,512]{2,1,0:T(4,128)(2,1)S(1)}, bf16[4,3,512]{2,1,0:T(4,128)(2,1)S(1)}, u32[]{:S(2)}, u32[]{:S(2)}) collective-permute-start(bf16[4,3,512]{2,1,0:T(4,128)(2,1)S(1)} %slice.220), channel_id=1, source_target_pairs={{8,0},{16,8},{24,16},{32,24},{40,32},{48,40},{56,48},{64,56},{72,6... | collective-permute-start | bytes 36872 | tf_op jit(solution)/shard_map/ppermute | solution.py:17
  5.3 1.3 copy-start.2
  10.4 8.6 %copy-start.6 = (s32[128,1]{0,1:T(1,128)S(1)}, s32[128,1]{0,1:T(1,128)}, u32[]{:S(2)}) copy-start(s32[128,1]{0,1:T(1,128)} %param.7) | copy-start | bytes 1540
  12.2 23.2 %all-to-all-start = ((bf16[2,4,256,256]{3,1,0,2:T(4,128)(2,1)}), bf16[2,4,256,256]{3,1,0,2:T(4,128)(2,1)S(1)}, u32[]{:S(2)}, u32[]{:S(2)}) async-start(bf16[2,4,256,256]{3,1,0,2:T(4,128)(2,1)} %copy.142), calls=%async_computation | async-start | bytes 2097152 | tf_op jit(solution)/shard_map/all_to_all | solution.py:257
  37.4 7.5 %copy-start.5 = (s32[2,2]{1,0:T(2,128)S(1)}, s32[2,2]{1,0:T(2,128)}, u32[]{:S(2)}) copy-start(s32[2,2]{1,0:T(2,128)} %param.6) | copy-start | bytes 52
  40.1 32.1 %collective-permute-start.1 = (bf16[2,1,16,8,512]{4,3,2,1,0:T(8,128)(2,1)S(1)}, bf16[2,1,16,8,512]{4,3,2,1,0:T(8,128)(2,1)S(1)}, u32[]{:S(2)}, u32[]{:S(2)}) collective-permute-start(bf16[2,1,16,8,512]{4,3,2,1,0:T(8,128)(2,1)S(1)} %bitcast.89), channel_id=1, source_target_pairs={{0,127},{1,0},{2,1},{3,2},{4,3},{5,4},{6,5},{7,6},{8,7},{9,8},{10,... | collective-permute-start | bytes 786440 | tf_op jit(solution)/shard_map/ppermute | solution.py:23
  53.9 5.8 %copy-start.4 = (bf16[2,1,16,4096]{3,2,1,0:T(8,128)(2,1)S(1)}, bf16[2,1,16,4096]{3,2,1,0:T(8,128)(2,1)}, u32[]{:S(2)}) copy-start(bf16[2,1,16,4096]{3,2,1,0:T(8,128)(2,1)} %get-tuple-element.10) | copy-start | bytes 786436
  59.4 13.9 %collective-permute-start.4 = (bf16[2,1,16,8,512]{4,3,2,1,0:T(8,128)(2,1)S(1)}, bf16[2,1,16,8,512]{4,3,2,1,0:T(8,128)(2,1)}, u32[]{:S(2)}, u32[]{:S(2)}) collective-permute-start(bf16[2,1,16,8,512]{4,3,2,1,0:T(8,128)(2,1)S(1)} %bitcast.97), channel_id=1, source_target_pairs={{0,127},{1,0},{2,1},{3,2},{4,3},{5,4},{6,5},{7,6},{8,7},{9,8},{10,... | collective-permute-start | bytes 786440 | tf_op jit(solution)/shard_map/ppermute | solution.py:23
  59.7 7.6 %copy-start.3 = (bf16[2,1,16,4096]{3,2,1,0:T(8,128)(2,1)S(1)}, bf16[2,1,16,4096]{3,2,1,0:T(8,128)(2,1)}, u32[]{:S(2)}) copy-start(bf16[2,1,16,4096]{3,2,1,0:T(8,128)(2,1)} %get-tuple-element.11) | copy-start | bytes 786436
  64.3 11.2 %collective-permute-start.3 = (bf16[2,1,16,8,512]{4,3,2,1,0:T(8,128)(2,1)S(1)}, bf16[2,1,16,8,512]{4,3,2,1,0:T(8,128)(2,1)}, u32[]{:S(2)}, u32[]{:S(2)}) collective-permute-start(bf16[2,1,16,8,512]{4,3,2,1,0:T(8,128)(2,1)S(1)} %bitcast.93), channel_id=1, source_target_pairs={{0,127},{1,0},{2,1},{3,2},{4,3},{5,4},{6,5},{7,6},{8,7},{9,8},{10,... | collective-permute-start | bytes 786440 | tf_op jit(solution)/shard_map/ppermute | solution.py:23
  71.9 9.8 %collective-permute-start.2 = (bf16[2,1,16,8,512]{4,3,2,1,0:T(8,128)(2,1)S(1)}, bf16[2,1,16,8,512]{4,3,2,1,0:T(8,128)(2,1)S(1)}, u32[]{:S(2)}, u32[]{:S(2)}) collective-permute-start(bf16[2,1,16,8,512]{4,3,2,1,0:T(8,128)(2,1)S(1)} %bitcast.85), channel_id=1, source_target_pairs={{0,127},{1,0},{2,1},{3,2},{4,3},{5,4},{6,5},{7,6},{8,7},{9,8},{10,... | collective-permute-start | bytes 786440 | tf_op jit(solution)/shard_map/ppermute | solution.py:23
  85.6 0.9 copy-start.1

commit v9 on v7

--- a/solution.py
+++ b/solution.py
@@ -106,11 +106,8 @@
     return jnp.asarray(both).astype(jnp.bfloat16)[None]
 
 
-def spectrum_kernel(
-    dest_ref, prod_ref, cos_ref, sin_ref, twc_ref, tws_ref, mix_ref, zero_ref, spec_ref, out_ref,
-    feat_scratch, sems,
-):
-    del zero_ref
+def spectrum_kernel(dest_ref, prod_ref, cos_ref, sin_ref, twc_ref, tws_ref, mix_ref, *refs):
+    spec_ref, out_ref, feat_scratch, sems = refs[-4:]
     f32 = jnp.float32
     block = pl.program_id(0)
     rows_per = feat_scratch.shape[1]
@@ -162,10 +159,10 @@
             tile_copy(block, d).wait()
 
 
-def spectrum_call(products, table_sub, hops_total, dest, slots):
-    _, sensors, combos, rows, sub_n = products.shape
+def spectrum_call(products, table_sub, hops_total, dest, outgoing, spectrum, first_block, sensors):
+    _, _, combos, rows, sub_n = products.shape
     per_device = rows // RADIX
-    blocks = sensors * combos
+    blocks = products.shape[1] * combos
     flat = products.reshape(2, blocks, rows, sub_n)
     index_b = jnp.arange(RADIX, dtype=jnp.int32)[:, None]
     index_p = jnp.arange(sub_n, dtype=jnp.int32)[None, :]
@@ -174,23 +171,30 @@
     twist_cos = jnp.tile(norm_factor * jnp.cos(twist_angle), (per_device, 1))
     twist_sin = jnp.tile(norm_factor * jnp.sin(twist_angle), (per_device, 1))
     mixers = section_mixers(RADIX, per_device)
-    zeros = jnp.zeros((slots, per_device, sub_n), jnp.bfloat16)
+    operands = [dest, flat, table_sub, table_sub, twist_cos, twist_sin, mixers, outgoing]
+    in_specs = [
+        pl.BlockSpec((2, 1, rows, sub_n), lambda i, dest: (0, i, 0, 0)),
+        pl.BlockSpec((sub_n, sub_n), lambda i, dest: (0, 0)),
+        pl.BlockSpec((sub_n, sub_n), lambda i, dest: (0, 1)),
+        pl.BlockSpec((rows, sub_n), lambda i, dest: (0, 0)),
+        pl.BlockSpec((rows, sub_n), lambda i, dest: (0, 0)),
+        pl.BlockSpec((1, 2 * rows, 2 * rows), lambda i, dest: (0, 0, 0)),
+        pl.BlockSpec(memory_space=pl.ANY),
+    ]
+    aliases = {7: 1}
+    if spectrum is not None:
+        operands.append(spectrum)
+        in_specs.append(pl.BlockSpec(memory_space=pl.ANY))
+        aliases[8] = 0
+    spec_shape = (2, sensors, combos, per_device, RADIX * sub_n)
     grid_spec = pltpu.PrefetchScalarGridSpec(
         num_scalar_prefetch=1,
         grid=(blocks,),
-        in_specs=[
-            pl.BlockSpec((2, 1, rows, sub_n), lambda i, dest: (0, i, 0, 0)),
-            pl.BlockSpec((sub_n, sub_n), lambda i, dest: (0, 0)),
-            pl.BlockSpec((sub_n, sub_n), lambda i, dest: (0, 1)),
-            pl.BlockSpec((rows, sub_n), lambda i, dest: (0, 0)),
-            pl.BlockSpec((rows, sub_n), lambda i, dest: (0, 0)),
-            pl.BlockSpec((1, 2 * rows, 2 * rows), lambda i, dest: (0, 0, 0)),
-            pl.BlockSpec(memory_space=pl.ANY),
-        ],
+        in_specs=in_specs,
         out_specs=[
             pl.BlockSpec(
                 (2, 1, 1, per_device, RADIX * sub_n),
-                lambda i, dest: (0, i // combos, i % combos, 0, 0),
+                lambda i, dest: (0, (i + first_block) // combos, (i + first_block) % combos, 0, 0),
             ),
             pl.BlockSpec(memory_space=pl.ANY),
         ],
@@ -199,14 +203,14 @@
             pltpu.SemaphoreType.DMA((RADIX,)),
         ],
     )
-    spectrum, outgoing = pl.pallas_call(
+    return pl.pallas_call(
         spectrum_kernel,
         grid_spec=grid_spec,
         out_shape=[
-            jax.ShapeDtypeStruct((2, sensors, combos, per_device, RADIX * sub_n), jnp.bfloat16),
-            jax.ShapeDtypeStruct((slots, per_device, sub_n), jnp.bfloat16),
+            jax.ShapeDtypeStruct(spec_shape, jnp.bfloat16),
+            jax.ShapeDtypeStruct(outgoing.shape, jnp.bfloat16),
         ],
-        input_output_aliases={7: 1},
+        input_output_aliases=aliases,
         compiler_params=pltpu.CompilerParams(
             vmem_limit_bytes=48 * 1024 * 1024,
             dimension_semantics=("arbitrary",),
@@ -216,8 +220,7 @@
             transcendentals=blocks * rows * sub_n,
             bytes_accessed=blocks * rows * sub_n * 2 * 5 + 4 * sub_n * sub_n,
         ),
-    )(dest, flat, table_sub, table_sub, twist_cos, twist_sin, mixers, zeros)
-    return spectrum, outgoing
+    )(*operands)
 
 
 def shards(frames, orders, owners, templates):
@@ -278,9 +281,8 @@
         pieces.append(
             jnp.stack([jnp.stack(prod_real, axis=1), jnp.stack(prod_imag, axis=1)]).astype(
                 jnp.bfloat16
-            )
+            ).reshape(2, part, combos, per_device * RADIX, sub_n)
         )
-    products = jnp.concatenate(pieces, axis=1)
     tiles_dev = sensors * combos * RADIX
     capacity = max(2, 2 * tiles_dev // devices_n)
     owner_ids = owners[:, 0]
@@ -290,13 +292,20 @@
     slot_ids = jnp.sum(before * one_hot, axis=1)
     places = owner_ids * capacity + slot_ids
     table_sub = sub_coefficients(sub_n)
-    spectrum, outgoing = spectrum_call(
-        products.reshape(2, sensors, combos, per_device * RADIX, sub_n),
-        table_sub,
-        hops_n,
-        places,
-        devices_n * capacity,
-    )
+    tiles_part = tiles_dev // halves
+    outgoing = jnp.zeros((devices_n * capacity, per_device, sub_n), jnp.bfloat16)
+    spectrum = None
+    for half in range(halves):
+        spectrum, outgoing = spectrum_call(
+            pieces[half],
+            table_sub,
+            hops_n,
+            places[half * tiles_part : (half + 1) * tiles_part],
+            outgoing,
+            spectrum,
+            half * part * combos,
+            sensors,
+        )
     outgoing = outgoing.reshape(devices_n, capacity * per_device, sub_n)
     arrived = lax.all_to_all(outgoing, ("row", "col"), split_axis=0, concat_axis=0, tiled=True)
     found = jnp.dot(

time: 162 us -> 161 us (level)
  other arithmetic: 16.9 us -> 15 us
    concatenate x1 -> x0, other arithmetic: 2.19 us -> none  [shards(): products = jnp.concatenate(pieces, axis=1)]
    broadcast_in_dim x1, local copies, waits for them, and re-layouts: 0.52 us -> 2.48 us  [shards(): jnp.zeros((devices_n * capacity, per_device, sub_n), jnp.bfloat16)]
    pallas_call x1 -> x2, Pallas kernels: 20.8 us -> 19.8 us  [spectrum_call(): pl.pallas_call(spectrum_kernel, grid_spec=grid_spec, out_shape=[jax.Shape...]
    another operation x2 -> x6, other arithmetic: 5.61 us -> 6.15 us
  transfers between devices with their start and end apart: 4 -> 4, of which waited for: 3 -> 3; matrix products, arithmetic and copies ran while one was open for 13% -> 14% of each run, Pallas kernels for 0% -> 0%
where the time goes in v9:
time: 161 us; the launch traced here: 160 us
  blocking collectives  59.1 us (37%)
  local copies, waits for them, and re-layouts  23.3 us (14%)
  Pallas kernels  19.8 us (12%)
  waiting for transfers between devices  15.7 us (10%)
  other arithmetic  15 us (9%)
  starting transfers between devices  13.6 us (8%)
  between operations  8.63 us (5%)
  matrix products  5.31 us (3%)
    all_to_all x1, blocking collectives, shards(): lax.all_to_all(outgoing, ('row', 'col'), split_axis=0, concat_axis=0, til...  59.1 us
    pallas_call x2, Pallas kernels, spectrum_call(): pl.pallas_call(spectrum_kernel, grid_spec=grid_spec, out_shape=[jax.Shape...  19.8 us
    ppermute x2, waiting for transfers between devices, from_behind_2(): return lax.ppermute(value, axis, pairs)  12.5 us
    reshape x2, local copies, waits for them, and re-layouts, shards(): ordered.reshape(2, part, per_device, sub_n, RADIX).transpose(0, 1, 2, 4, 3)  9.87 us
    all_to_all x1, starting transfers between devices, shards(): lax.all_to_all(demod, 'row', split_axis=2, concat_axis=3, tiled=True)  6.78 us
    slice x3, local copies, waits for them, and re-layouts, shards(): ordered = swapped[:, half * part:(half + 1) * part]  6.15 us
    another operation x2, other arithmetic  5.61 us
    ppermute x2, starting transfers between devices, from_behind_2(): return lax.ppermute(value, axis, pairs)  5.52 us
  transfers between devices with their start and end apart: 4, of which 3 were waited for; matrix products, arithmetic and copies ran while one was open for 14% of the time, Pallas kernels for 0%

profile of v9, /device:TPU:0, one launch (start us, length us, event | category | flops | bytes accessed | tf_op | source)
XLA Modules:
  0.0 160.4 jit_solution(3936892465927231870)
XLA Ops:
  0.6 0.8 slice.137
  1.4 1.3 collective-permute-start
  2.9 0.6 fusion.104
  4.1 1.2 multiply_add_fusion
  5.3 1.3 fusion
  6.7 0.7 fusion.71
  7.5 0.8 fusion.11
  8.3 0.8 fusion.9
  9.0 0.8 add_bitcast_fusion
  9.9 0.4 fusion.16
  10.4 1.8 %copy.84 = bf16[2,4,256,256]{3,1,0,2:T(4,128)(2,1)} copy(bf16[2,4,256,256]{3,2,1,0:T(8,128)(2,1)S(1)} %pad_maximum_fusion.2) | data formatting | bytes 2097152 | tf_op jit(solution)/shard_map/stack | solution.py:259
  12.2 6.8 %all-to-all-start = ((bf16[2,4,256,256]{3,1,0,2:T(4,128)(2,1)}), bf16[2,4,256,256]{3,1,0,2:T(4,128)(2,1)S(1)}, u32[]{:S(2)}, u32[]{:S(2)}) async-start(bf16[2,4,256,256]{3,1,0,2:T(4,128)(2,1)} %copy.84), calls=%async_computation | async-start | bytes 2097152 | tf_op jit(solution)/shard_map/all_to_all | solution.py:260
  19.0 0.7 fusion.130
  27.8 4.3 %sine_convert_fusion = (bf16[512,512]{1,0:T(8,128)(2,1)S(1)}, bf16[512,512]{1,0:T(8,128)(2,1)S(1)}) fusion(), kind=kLoop, calls=%fused_computation.83 | loop fusion | flops 4194304 | bytes 1048576 | tf_op jit(solution)/shard_map/convert.21
  32.2 3.2 %all-to-all-done = bf16[2,4,256,256]{3,1,0,2:T(4,128)(2,1)S(1)} async-done(((bf16[2,4,256,256]{3,1,0,2:T(4,128)(2,1)}), bf16[2,4,256,256]{3,1,0,2:T(4,128)(2,1)S(1)}, u32[]{:S(2)}, u32[]{:S(2)}) %all-to-all-start) | async-done | bytes 1048608 | tf_op jit(solution)/shard_map/all_to_all | solution.py:260
  35.4 0.6 copy.111
  36.0 0.5 all_to_all.19
  36.6 3.0 %copy.96 = bf16[2,2,16,4096]{2,3,1,0:T(8,128)(2,1)} copy(bf16[2,2,16,4096]{3,2,1,0:T(8,128)(2,1)S(1)} %get-tuple-element.32) | data formatting | bytes 1048576 | tf_op jit(solution)/shard_map/slice | solution.py:265
  39.6 4.9 %copy.97 = bf16[2,2,16,512,8]{3,4,2,1,0:T(8,128)(2,1)S(1)} copy(bf16[2,2,16,512,8]{2,4,3,1,0:T(8,128)(2,1)} %bitcast.126) | data formatting | bytes 1048576 | tf_op jit(solution)/shard_map/reshape | solution.py:266
  44.6 5.2 %collective-permute-start.2 = (bf16[2,2,16,8,512]{4,3,2,1,0:T(8,128)(2,1)S(1)}, bf16[2,2,16,8,512]{4,3,2,1,0:T(8,128)(2,1)}, u32[]{:S(2)}, u32[]{:S(2)}) collective-permute-start(bf16[2,2,16,8,512]{4,3,2,1,0:T(8,128)(2,1)S(1)} %bitcast.132), channel_id=1, source_target_pairs={{0,127},{1,0},{2,1},{3,2},{4,3},{5,4},{6,5},{7,6},{8,7},{9,8},{10,... | collective-permute-start | bytes 1572872 | tf_op jit(solution)/shard_map/ppermute | solution.py:23
  50.0 3.0 %copy.86 = bf16[2,2,16,4096]{2,3,1,0:T(8,128)(2,1)} copy(bf16[2,2,16,4096]{3,2,1,0:T(8,128)(2,1)S(1)} %get-tuple-element.33) | data formatting | bytes 1048576 | tf_op jit(solution)/shard_map/slice | solution.py:265
  53.0 4.9 %copy.87 = bf16[2,2,16,512,8]{3,4,2,1,0:T(8,128)(2,1)S(1)} copy(bf16[2,2,16,512,8]{2,4,3,1,0:T(8,128)(2,1)} %bitcast.127) | data formatting | bytes 1048576 | tf_op jit(solution)/shard_map/reshape | solution.py:266
  58.0 0.3 collective-permute-start.1
  58.3 3.5 %collective-permute-done.2 = bf16[2,2,16,8,512]{4,3,2,1,0:T(8,128)(2,1)} collective-permute-done((bf16[2,2,16,8,512]{4,3,2,1,0:T(8,128)(2,1)S(1)}, bf16[2,2,16,8,512]{4,3,2,1,0:T(8,128)(2,1)}, u32[]{:S(2)}, u32[]{:S(2)}) %collective-permute-start.2) | collective-permute-done | bytes 524320 | tf_op jit(solution)/shard_map/ppermute | solution.py:23
  61.8 2.3 %fusion.53 = (f32[2,2,16,8,512]{4,3,2,1,0:T(8,128)S(1)}, f32[2,2,16,8,512]{4,3,2,1,0:T(8,128)S(1)}, f32[2,2,16,8,512]{4,3,2,1,0:T(8,128)S(1)}, f32[2,2,16,8,512]{4,3,2,1,0:T(8,128)S(1)}) fusion(s32[]{:T(128)S(6)} %select_n.139, bf16[2,2,16,8,512]{4,3,2,1,0:T(8,128)(2,1)S(1)} %bitcast.133, bf16[2,2,16,8,512]{4,3,2,1,0:T(8,128)(2,1)} %collective-permute-done.2, ...), kind=kLoop, calls=%fused_computation.127 | loop fusion | flops 2097152 | bytes 5242896 | tf_op jit(solution)/shard_map/convert_element_type | solution.py:278
  65.3 9.0 %collective-permute-done.1 = bf16[2,2,16,8,512]{4,3,2,1,0:T(8,128)(2,1)S(1)} collective-permute-done((bf16[2,2,16,8,512]{4,3,2,1,0:T(8,128)(2,1)S(1)}, bf16[2,2,16,8,512]{4,3,2,1,0:T(8,128)(2,1)S(1)}, u32[]{:S(2)}, u32[]{:S(2)}) %collective-permute-start.1) | collective-permute-done | bytes 524320 | tf_op jit(solution)/shard_map/ppermute | solution.py:23
  74.3 1.2 fusion.61
  76.8 2.5 %broadcast_in_dim.8.refs_0_ = bf16[256,16,512]{2,1,0:T(8,128)(2,1)} broadcast(bf16[]{:T(256)} %constant.161.clone.1), dimensions={} | broadcast | bytes 4194306 | tf_op jit(solution)/shard_map/broadcast_in_dim | solution.py:296
  79.3 9.9 %shard_map.77 = (bf16[2,4,4,16,4096]{4,3,2,1,0:T(8,128)(2,1)}, bf16[256,16,512]{2,1,0:T(8,128)(2,1)}) custom-call(s32[64]{0:T(128)S(1)} %get-tuple-element.60.dest_ref, bf16[2,8,128,512]{3,2,1,0:T(8,128)(2,1)S(1)} %pad_maximum_fusion.1.prod_ref, bf16[512,1024]{1,0:T(8,128)(2,1)S(1)} %pad_maximum_fusion.5.cos_ref.sin_ref, ...), custom_call_target="tpu_custom_call", output_to_operand_aliasing={{1}: (7, {})} | custom-call | flops 3221225472 | bytes 6291456 | tf_op jit(solution)/shard_map/pallas_call | solution.py:206
  89.2 9.9 %shard_map.78 = (bf16[2,4,4,16,4096]{4,3,2,1,0:T(8,128)(2,1)}, bf16[256,16,512]{2,1,0:T(8,128)(2,1)}) custom-call(s32[64]{0:T(128)S(1)} %get-tuple-element.61.dest_ref, bf16[2,8,128,512]{3,2,1,0:T(8,128)(2,1)S(1)} %pad_maximum_fusion.prod_ref, bf16[512,1024]{1,0:T(8,128)(2,1)S(1)} %pad_maximum_fusion.5.cos_ref.sin_ref, ...), custom_call_target="tpu_custom_call", output_to_operand_aliasing={{1}: (7, {}), {0}: (8, {})} | custom-call | flops 3221225472 | bytes 6291456 | tf_op jit(solution)/shard_map/pallas_call | solution.py:206
  99.1 59.1 %all_to_all.23 = bf16[128,32,512]{2,1,0:T(8,128)(2,1)S(1)} all-to-all(bf16[128,32,512]{2,1,0:T(8,128)(2,1)} %bitcast.124), channel_id=1, replica_groups=mesh['row'=16,'col'=8] {'row','col'}, dimensions={0} | all-to-all | bytes 8388608 | tf_op jit(solution)/shard_map/all_to_all | solution.py:310
  158.2 2.2 %convolution_convert_fusion = bf16[4096,128]{1,0:T(8,128)(2,1)} fusion(bf16[4096,512]{1,0:T(8,128)(2,1)S(1)} %bitcast.125, bf16[1,512,128]{2,1,0:T(8,128)(2,1)S(1)} %copy-done), kind=kOutput, calls=%fused_computation | convolution fusion | flops 537395200 | bytes 5373952 | tf_op jit(solution)/shard_map/dot_general | solution.py:311
  (42 shorter events, 4.1 us)
Async XLA Ops:
  0.6 157.6 %copy-start = (bf16[1,512,128]{2,1,0:T(8,128)(2,1)S(1)}, bf16[1,512,128]{2,1,0:T(8,128)(2,1)}, u32[]{:S(2)}) copy-start(bf16[1,512,128]{2,1,0:T(8,128)(2,1)} %param.9) | copy-start | bytes 393220
  1.4 6.0 %collective-permute-start = (bf16[4,3,512]{2,1,0:T(4,128)(2,1)S(1)}, bf16[4,3,512]{2,1,0:T(4,128)(2,1)S(1)}, u32[]{:S(2)}, u32[]{:S(2)}) collective-permute-start(bf16[4,3,512]{2,1,0:T(4,128)(2,1)S(1)} %slice.137), channel_id=1, source_target_pairs={{8,0},{16,8},{24,16},{32,24},{40,32},{48,40},{56,48},{64,56},{72,6... | collective-permute-start | bytes 36872 | tf_op jit(solution)/shard_map/ppermute | solution.py:17
  5.3 1.3 copy-start.2
  10.4 8.6 %copy-start.3 = (s32[2,2]{1,0:T(2,128)S(1)}, s32[2,2]{1,0:T(2,128)}, u32[]{:S(2)}) copy-start(s32[2,2]{1,0:T(2,128)} %param.7) | copy-start | bytes 52
  10.4 14.3 %copy-start.4 = (s32[128,1]{0,1:T(1,128)S(1)}, s32[128,1]{0,1:T(1,128)}, u32[]{:S(2)}) copy-start(s32[128,1]{0,1:T(1,128)} %param.8) | copy-start | bytes 1540
  12.2 23.2 %all-to-all-start = ((bf16[2,4,256,256]{3,1,0,2:T(4,128)(2,1)}), bf16[2,4,256,256]{3,1,0,2:T(4,128)(2,1)S(1)}, u32[]{:S(2)}, u32[]{:S(2)}) async-start(bf16[2,4,256,256]{3,1,0,2:T(4,128)(2,1)} %copy.84), calls=%async_computation | async-start | bytes 2097152 | tf_op jit(solution)/shard_map/all_to_all | solution.py:260
  44.6 17.2 %collective-permute-start.2 = (bf16[2,2,16,8,512]{4,3,2,1,0:T(8,128)(2,1)S(1)}, bf16[2,2,16,8,512]{4,3,2,1,0:T(8,128)(2,1)}, u32[]{:S(2)}, u32[]{:S(2)}) collective-permute-start(bf16[2,2,16,8,512]{4,3,2,1,0:T(8,128)(2,1)S(1)} %bitcast.132), channel_id=1, source_target_pairs={{0,127},{1,0},{2,1},{3,2},{4,3},{5,4},{6,5},{7,6},{8,7},{9,8},{10,... | collective-permute-start | bytes 1572872 | tf_op jit(solution)/shard_map/ppermute | solution.py:23
  58.0 16.4 %collective-permute-start.1 = (bf16[2,2,16,8,512]{4,3,2,1,0:T(8,128)(2,1)S(1)}, bf16[2,2,16,8,512]{4,3,2,1,0:T(8,128)(2,1)S(1)}, u32[]{:S(2)}, u32[]{:S(2)}) collective-permute-start(bf16[2,2,16,8,512]{4,3,2,1,0:T(8,128)(2,1)S(1)} %bitcast.128), channel_id=1, source_target_pairs={{0,127},{1,0},{2,1},{3,2},{4,3},{5,4},{6,5},{7,6},{8,7},{9,8},{10,... | collective-permute-start | bytes 1572872 | tf_op jit(solution)/shard_map/ppermute | solution.py:23
  76.8 2.5 %copy-start.1 = (bf16[1,256,256]{2,1,0:T(8,128)(2,1)S(1)}, bf16[1,256,256]{2,1,0:T(8,128)(2,1)}, u32[]{:S(2)}) copy-start(bf16[1,256,256]{2,1,0:T(8,128)(2,1)} %constant.165.mix_ref) | copy-start | bytes 393220

commit v10 on v9

--- a/solution.py
+++ b/solution.py
@@ -58,35 +58,6 @@
     real_part = a_cos * cos_quarter - a_sin * sin_quarter
     imag_part = -a_sin * cos_quarter - a_cos * sin_quarter
     return (real_part, imag_part)
-
-
-def finish_transform(first_real, first_imag, hops_total):
-    radix_count = first_real.shape[-2]
-    sub_total = first_real.shape[-1]
-    index_b = jnp.arange(radix_count, dtype=jnp.int32)[:, None]
-    index_p = jnp.arange(sub_total, dtype=jnp.int32)[None, :]
-    twist_angle = 2.0 * math.pi / hops_total * (index_b * index_p % hops_total).astype(jnp.float32)
-    twist_cos = jnp.cos(twist_angle)
-    twist_sin = jnp.sin(twist_angle)
-    twist_real = first_real * twist_cos + first_imag * twist_sin
-    twist_imag = first_imag * twist_cos - first_real * twist_sin
-    index_d = jnp.arange(radix_count, dtype=jnp.int32)[None, :]
-    section_angle = (
-        2.0 * math.pi / radix_count * (index_b * index_d % radix_count).astype(jnp.float32)
-    )
-    section_cos = jnp.cos(section_angle)
-    section_sin = jnp.sin(section_angle)
-    highest = lax.Precision.HIGHEST
-    norm_factor = 1.0 / math.sqrt(hops_total)
-    out_real = norm_factor * (
-        jnp.einsum("...bq,bd->...dq", twist_real, section_cos, precision=highest)
-        + jnp.einsum("...bq,bd->...dq", twist_imag, section_sin, precision=highest)
-    )
-    out_imag = norm_factor * (
-        jnp.einsum("...bq,bd->...dq", twist_imag, section_cos, precision=highest)
-        - jnp.einsum("...bq,bd->...dq", twist_real, section_sin, precision=highest)
-    )
-    return (out_real, out_imag)
 
 
 def section_mixers(radix_count, rows_per):
@@ -223,7 +194,7 @@
     )(*operands)
 
 
-def shards(frames, orders, owners, templates):
+def shards_body(frames, orders, owners, templates):
     rows_count = lax.axis_size("row")
     cols_count = lax.axis_size("col")
     devices_n = rows_count * cols_count
@@ -321,4 +292,4 @@
         P(None, None, None, ("row", "col"), None),
         P(("row", "col"), None, None, None, None),
     )
-    return jax.shard_map(shards, mesh=mesh, in_specs=in_specs, out_specs=out_specs, check_vma=False)
+    return jax.shard_map(shards_body, mesh=mesh, in_specs=in_specs, out_specs=out_specs, check_vma=False)

time: 161 us -> 161 us (level)
  no operation moved by 1% of the time
where the time goes in v10:
time: 161 us; the launch traced here: 160 us
  blocking collectives  59.1 us (37%)
  local copies, waits for them, and re-layouts  23.3 us (14%)
  Pallas kernels  19.8 us (12%)
  waiting for transfers between devices  15.7 us (10%)
  other arithmetic  15 us (9%)
  starting transfers between devices  13.6 us (8%)
  between operations  8.63 us (5%)
  matrix products  5.31 us (3%)
    all_to_all x1, blocking collectives, shards_body(): lax.all_to_all(outgoing, ('row', 'col'), split_axis=0, concat_axis=0, til...  59.1 us
    pallas_call x2, Pallas kernels, spectrum_call(): pl.pallas_call(spectrum_kernel, grid_spec=grid_spec, out_shape=[jax.Shape...  19.8 us
    ppermute x2, waiting for transfers between devices, from_behind_2(): return lax.ppermute(value, axis, pairs)  12.5 us
    reshape x2, local copies, waits for them, and re-layouts, shards_body(): ordered.reshape(2, part, per_device, sub_n, RADIX).transpose(0, 1, 2, 4, 3)  9.87 us
    all_to_all x1, starting transfers between devices, shards_body(): lax.all_to_all(demod, 'row', split_axis=2, concat_axis=3, tiled=True)  6.78 us
    slice x3, local copies, waits for them, and re-layouts, shards_body(): ordered = swapped[:, half * part:(half + 1) * part]  6.15 us
    another operation x2, other arithmetic  5.61 us
    ppermute x2, starting transfers between devices, from_behind_2(): return lax.ppermute(value, axis, pairs)  5.52 us
  transfers between devices with their start and end apart: 4, of which 3 were waited for; matrix products, arithmetic and copies ran while one was open for 14% of the time, Pallas kernels for 0%

profile of v10, /device:TPU:0, one launch (start us, length us, event | category | flops | bytes accessed | tf_op | source)
XLA Modules:
  0.0 160.4 jit_solution(3936892465927231870)
XLA Ops:
  0.6 0.8 slice.137
  1.4 1.3 collective-permute-start
  2.9 0.6 fusion.104
  4.1 1.2 multiply_add_fusion
  5.3 1.3 fusion
  6.7 0.7 fusion.71
  7.5 0.8 fusion.11
  8.3 0.8 fusion.9
  9.0 0.8 add_bitcast_fusion
  9.9 0.4 fusion.16
  10.4 1.8 %copy.84 = bf16[2,4,256,256]{3,1,0,2:T(4,128)(2,1)} copy(bf16[2,4,256,256]{3,2,1,0:T(8,128)(2,1)S(1)} %pad_maximum_fusion.2) | data formatting | bytes 2097152 | tf_op jit(solution)/shard_map/stack | solution.py:230
  12.2 6.8 %all-to-all-start = ((bf16[2,4,256,256]{3,1,0,2:T(4,128)(2,1)}), bf16[2,4,256,256]{3,1,0,2:T(4,128)(2,1)S(1)}, u32[]{:S(2)}, u32[]{:S(2)}) async-start(bf16[2,4,256,256]{3,1,0,2:T(4,128)(2,1)} %copy.84), calls=%async_computation | async-start | bytes 2097152 | tf_op jit(solution)/shard_map/all_to_all | solution.py:231
  19.0 0.7 fusion.130
  27.8 4.3 %sine_convert_fusion = (bf16[512,512]{1,0:T(8,128)(2,1)S(1)}, bf16[512,512]{1,0:T(8,128)(2,1)S(1)}) fusion(), kind=kLoop, calls=%fused_computation.83 | loop fusion | flops 4194304 | bytes 1048576 | tf_op jit(solution)/shard_map/convert.21
  32.2 3.2 %all-to-all-done = bf16[2,4,256,256]{3,1,0,2:T(4,128)(2,1)S(1)} async-done(((bf16[2,4,256,256]{3,1,0,2:T(4,128)(2,1)}), bf16[2,4,256,256]{3,1,0,2:T(4,128)(2,1)S(1)}, u32[]{:S(2)}, u32[]{:S(2)}) %all-to-all-start) | async-done | bytes 1048608 | tf_op jit(solution)/shard_map/all_to_all | solution.py:231
  35.4 0.6 copy.111
  36.0 0.5 all_to_all.19
  36.6 3.0 %copy.96 = bf16[2,2,16,4096]{2,3,1,0:T(8,128)(2,1)} copy(bf16[2,2,16,4096]{3,2,1,0:T(8,128)(2,1)S(1)} %get-tuple-element.32) | data formatting | bytes 1048576 | tf_op jit(solution)/shard_map/slice | solution.py:236
  39.6 4.9 %copy.97 = bf16[2,2,16,512,8]{3,4,2,1,0:T(8,128)(2,1)S(1)} copy(bf16[2,2,16,512,8]{2,4,3,1,0:T(8,128)(2,1)} %bitcast.126) | data formatting | bytes 1048576 | tf_op jit(solution)/shard_map/reshape | solution.py:237
  44.6 5.2 %collective-permute-start.2 = (bf16[2,2,16,8,512]{4,3,2,1,0:T(8,128)(2,1)S(1)}, bf16[2,2,16,8,512]{4,3,2,1,0:T(8,128)(2,1)}, u32[]{:S(2)}, u32[]{:S(2)}) collective-permute-start(bf16[2,2,16,8,512]{4,3,2,1,0:T(8,128)(2,1)S(1)} %bitcast.132), channel_id=1, source_target_pairs={{0,127},{1,0},{2,1},{3,2},{4,3},{5,4},{6,5},{7,6},{8,7},{9,8},{10,... | collective-permute-start | bytes 1572872 | tf_op jit(solution)/shard_map/ppermute | solution.py:23
  50.0 3.0 %copy.86 = bf16[2,2,16,4096]{2,3,1,0:T(8,128)(2,1)} copy(bf16[2,2,16,4096]{3,2,1,0:T(8,128)(2,1)S(1)} %get-tuple-element.33) | data formatting | bytes 1048576 | tf_op jit(solution)/shard_map/slice | solution.py:236
  53.0 4.9 %copy.87 = bf16[2,2,16,512,8]{3,4,2,1,0:T(8,128)(2,1)S(1)} copy(bf16[2,2,16,512,8]{2,4,3,1,0:T(8,128)(2,1)} %bitcast.127) | data formatting | bytes 1048576 | tf_op jit(solution)/shard_map/reshape | solution.py:237
  58.0 0.3 collective-permute-start.1
  58.3 3.5 %collective-permute-done.2 = bf16[2,2,16,8,512]{4,3,2,1,0:T(8,128)(2,1)} collective-permute-done((bf16[2,2,16,8,512]{4,3,2,1,0:T(8,128)(2,1)S(1)}, bf16[2,2,16,8,512]{4,3,2,1,0:T(8,128)(2,1)}, u32[]{:S(2)}, u32[]{:S(2)}) %collective-permute-start.2) | collective-permute-done | bytes 524320 | tf_op jit(solution)/shard_map/ppermute | solution.py:23
  61.8 2.3 %fusion.53 = (f32[2,2,16,8,512]{4,3,2,1,0:T(8,128)S(1)}, f32[2,2,16,8,512]{4,3,2,1,0:T(8,128)S(1)}, f32[2,2,16,8,512]{4,3,2,1,0:T(8,128)S(1)}, f32[2,2,16,8,512]{4,3,2,1,0:T(8,128)S(1)}) fusion(s32[]{:T(128)S(6)} %select_n.139, bf16[2,2,16,8,512]{4,3,2,1,0:T(8,128)(2,1)S(1)} %bitcast.133, bf16[2,2,16,8,512]{4,3,2,1,0:T(8,128)(2,1)} %collective-permute-done.2, ...), kind=kLoop, calls=%fused_computation.127 | loop fusion | flops 2097152 | bytes 5242896 | tf_op jit(solution)/shard_map/convert_element_type | solution.py:249
  65.3 9.1 %collective-permute-done.1 = bf16[2,2,16,8,512]{4,3,2,1,0:T(8,128)(2,1)S(1)} collective-permute-done((bf16[2,2,16,8,512]{4,3,2,1,0:T(8,128)(2,1)S(1)}, bf16[2,2,16,8,512]{4,3,2,1,0:T(8,128)(2,1)S(1)}, u32[]{:S(2)}, u32[]{:S(2)}) %collective-permute-start.1) | collective-permute-done | bytes 524320 | tf_op jit(solution)/shard_map/ppermute | solution.py:23
  74.3 1.3 fusion.61
  76.8 2.5 %broadcast_in_dim.8.refs_0_ = bf16[256,16,512]{2,1,0:T(8,128)(2,1)} broadcast(bf16[]{:T(256)} %constant.161.clone.1), dimensions={} | broadcast | bytes 4194306 | tf_op jit(solution)/shard_map/broadcast_in_dim | solution.py:267
  79.3 9.9 %shard_map.77 = (bf16[2,4,4,16,4096]{4,3,2,1,0:T(8,128)(2,1)}, bf16[256,16,512]{2,1,0:T(8,128)(2,1)}) custom-call(s32[64]{0:T(128)S(1)} %get-tuple-element.60.dest_ref, bf16[2,8,128,512]{3,2,1,0:T(8,128)(2,1)S(1)} %pad_maximum_fusion.1.prod_ref, bf16[512,1024]{1,0:T(8,128)(2,1)S(1)} %pad_maximum_fusion.5.cos_ref.sin_ref, ...), custom_call_target="tpu_custom_call", output_to_operand_aliasing={{1}: (7, {})} | custom-call | flops 3221225472 | bytes 6291456 | tf_op jit(solution)/shard_map/pallas_call | solution.py:177
  89.2 9.9 %shard_map.78 = (bf16[2,4,4,16,4096]{4,3,2,1,0:T(8,128)(2,1)}, bf16[256,16,512]{2,1,0:T(8,128)(2,1)}) custom-call(s32[64]{0:T(128)S(1)} %get-tuple-element.61.dest_ref, bf16[2,8,128,512]{3,2,1,0:T(8,128)(2,1)S(1)} %pad_maximum_fusion.prod_ref, bf16[512,1024]{1,0:T(8,128)(2,1)S(1)} %pad_maximum_fusion.5.cos_ref.sin_ref, ...), custom_call_target="tpu_custom_call", output_to_operand_aliasing={{1}: (7, {}), {0}: (8, {})} | custom-call | flops 3221225472 | bytes 6291456 | tf_op jit(solution)/shard_map/pallas_call | solution.py:177
  99.1 59.1 %all_to_all.23 = bf16[128,32,512]{2,1,0:T(8,128)(2,1)S(1)} all-to-all(bf16[128,32,512]{2,1,0:T(8,128)(2,1)} %bitcast.124), channel_id=1, replica_groups=mesh['row'=16,'col'=8] {'row','col'}, dimensions={0} | all-to-all | bytes 8388608 | tf_op jit(solution)/shard_map/all_to_all | solution.py:281
  158.2 2.2 %convolution_convert_fusion = bf16[4096,128]{1,0:T(8,128)(2,1)} fusion(bf16[4096,512]{1,0:T(8,128)(2,1)S(1)} %bitcast.125, bf16[1,512,128]{2,1,0:T(8,128)(2,1)S(1)} %copy-done), kind=kOutput, calls=%fused_computation | convolution fusion | flops 537395200 | bytes 5373952 | tf_op jit(solution)/shard_map/dot_general | solution.py:282
  (42 shorter events, 4.1 us)
Async XLA Ops:
  0.6 157.6 %copy-start = (bf16[1,512,128]{2,1,0:T(8,128)(2,1)S(1)}, bf16[1,512,128]{2,1,0:T(8,128)(2,1)}, u32[]{:S(2)}) copy-start(bf16[1,512,128]{2,1,0:T(8,128)(2,1)} %param.9) | copy-start | bytes 393220
  1.4 6.0 %collective-permute-start = (bf16[4,3,512]{2,1,0:T(4,128)(2,1)S(1)}, bf16[4,3,512]{2,1,0:T(4,128)(2,1)S(1)}, u32[]{:S(2)}, u32[]{:S(2)}) collective-permute-start(bf16[4,3,512]{2,1,0:T(4,128)(2,1)S(1)} %slice.137), channel_id=1, source_target_pairs={{8,0},{16,8},{24,16},{32,24},{40,32},{48,40},{56,48},{64,56},{72,6... | collective-permute-start | bytes 36872 | tf_op jit(solution)/shard_map/ppermute | solution.py:17
  5.3 1.3 copy-start.2
  10.4 8.6 %copy-start.3 = (s32[2,2]{1,0:T(2,128)S(1)}, s32[2,2]{1,0:T(2,128)}, u32[]{:S(2)}) copy-start(s32[2,2]{1,0:T(2,128)} %param.7) | copy-start | bytes 52
  10.4 14.3 %copy-start.4 = (s32[128,1]{0,1:T(1,128)S(1)}, s32[128,1]{0,1:T(1,128)}, u32[]{:S(2)}) copy-start(s32[128,1]{0,1:T(1,128)} %param.8) | copy-start | bytes 1540
  12.2 23.2 %all-to-all-start = ((bf16[2,4,256,256]{3,1,0,2:T(4,128)(2,1)}), bf16[2,4,256,256]{3,1,0,2:T(4,128)(2,1)S(1)}, u32[]{:S(2)}, u32[]{:S(2)}) async-start(bf16[2,4,256,256]{3,1,0,2:T(4,128)(2,1)} %copy.84), calls=%async_computation | async-start | bytes 2097152 | tf_op jit(solution)/shard_map/all_to_all | solution.py:231
  44.6 17.2 %collective-permute-start.2 = (bf16[2,2,16,8,512]{4,3,2,1,0:T(8,128)(2,1)S(1)}, bf16[2,2,16,8,512]{4,3,2,1,0:T(8,128)(2,1)}, u32[]{:S(2)}, u32[]{:S(2)}) collective-permute-start(bf16[2,2,16,8,512]{4,3,2,1,0:T(8,128)(2,1)S(1)} %bitcast.132), channel_id=1, source_target_pairs={{0,127},{1,0},{2,1},{3,2},{4,3},{5,4},{6,5},{7,6},{8,7},{9,8},{10,... | collective-permute-start | bytes 1572872 | tf_op jit(solution)/shard_map/ppermute | solution.py:23
  58.0 16.4 %collective-permute-start.1 = (bf16[2,2,16,8,512]{4,3,2,1,0:T(8,128)(2,1)S(1)}, bf16[2,2,16,8,512]{4,3,2,1,0:T(8,128)(2,1)S(1)}, u32[]{:S(2)}, u32[]{:S(2)}) collective-permute-start(bf16[2,2,16,8,512]{4,3,2,1,0:T(8,128)(2,1)S(1)} %bitcast.128), channel_id=1, source_target_pairs={{0,127},{1,0},{2,1},{3,2},{4,3},{5,4},{6,5},{7,6},{8,7},{9,8},{10,... | collective-permute-start | bytes 1572872 | tf_op jit(solution)/shard_map/ppermute | solution.py:23
  76.8 2.5 %copy-start.1 = (bf16[1,256,256]{2,1,0:T(8,128)(2,1)S(1)}, bf16[1,256,256]{2,1,0:T(8,128)(2,1)}, u32[]{:S(2)}) copy-start(bf16[1,256,256]{2,1,0:T(8,128)(2,1)} %constant.165.mix_ref) | copy-start | bytes 393220

commit v11 on v10

--- a/solution.py
+++ b/solution.py
@@ -228,12 +228,15 @@
         summed[:, :local_channels], summed[:, local_channels:], channel_ids, hop_ids
     )
     demod = jnp.stack([real_part, imag_part]).astype(jnp.bfloat16)
-    swapped = lax.all_to_all(demod, "row", split_axis=2, concat_axis=3, tiled=True)
+    split_parts = []
+    for half in range(2):
+        piece = demod[:, half * (sensors // 2) : (half + 1) * (sensors // 2)]
+        split_parts.append(lax.all_to_all(piece, "row", split_axis=2, concat_axis=3, tiled=True))
     halves = 2
     part = sensors // halves
     pieces = []
     for half in range(halves):
-        ordered = swapped[:, half * part : (half + 1) * part]
+        ordered = split_parts[half]
         ordered = ordered.reshape(2, part, per_device, sub_n, RADIX).transpose(0, 1, 2, 4, 3)
         above = from_behind_2(ordered, ("row", "col"), -1)
         extended = jnp.concatenate([ordered, above], axis=2)

time: 161 us -> 168 us (1.043)
  starting transfers between devices: 13.6 us -> 20.3 us
    all_to_all x2, local copies, waits for them, and re-layouts: 1.11 us -> 6.35 us  [shards_body(): lax.all_to_all(piece, 'row', split_axis=2, concat_axis=3, tiled=True)]
    all_to_all x1 -> x2, starting transfers between devices: 6.78 us -> 10.3 us  [shards_body(): lax.all_to_all(piece, 'row', split_axis=2, concat_axis=3, tiled=True)]
    slice x3 -> x2, local copies, waits for them, and re-layouts: 6.15 us -> 2.67 us  [shards_body(): piece = demod[:, half * (sensors // 2):(half + 1) * (sensors // 2)]]
    ppermute x2, starting transfers between devices: 5.52 us -> 8.64 us  [from_behind_2(): return lax.ppermute(value, axis, pairs)]
    ppermute x2, waiting for transfers between devices: 12.5 us -> 10.5 us  [from_behind_2(): return lax.ppermute(value, axis, pairs)]
    all_to_all x1 -> x2, waiting for transfers between devices: 3.16 us -> 5.04 us  [shards_body(): lax.all_to_all(piece, 'row', split_axis=2, concat_axis=3, tiled=True)]
    another operation x1 -> x0, local copies, waits for them, and re-layouts: 1.78 us -> none  [shards_body(): demod = jnp.stack([real_part, imag_part]).astype(jnp.bfloat16)]
  transfers between devices with their start and end apart: 4 -> 5, of which waited for: 3 -> 2; matrix products, arithmetic and copies ran while one was open for 14% -> 19% of each run, Pallas kernels for 0% -> 0%
where the time goes in v11:
time: 168 us; the launch traced here: 167 us
  blocking collectives  59.3 us (35%)
  local copies, waits for them, and re-layouts  24.5 us (15%)
  starting transfers between devices  20.3 us (12%)
  Pallas kernels  19.8 us (12%)
  waiting for transfers between devices  15.5 us (9%)
  other arithmetic  13.9 us (8%)
  between operations  8.76 us (5%)
  matrix products  5.32 us (3%)
    all_to_all x1, blocking collectives, shards_body(): lax.all_to_all(outgoing, ('row', 'col'), split_axis=0, concat_axis=0, til...  59.3 us
    pallas_call x2, Pallas kernels, spectrum_call(): pl.pallas_call(spectrum_kernel, grid_spec=grid_spec, out_shape=[jax.Shape...  19.8 us
    ppermute x2, waiting for transfers between devices, from_behind_2(): return lax.ppermute(value, axis, pairs)  10.5 us
    all_to_all x2, starting transfers between devices, shards_body(): lax.all_to_all(piece, 'row', split_axis=2, concat_axis=3, tiled=True)  10.3 us
    reshape x2, local copies, waits for them, and re-layouts, shards_body(): ordered.reshape(2, part, per_device, sub_n, RADIX).transpose(0, 1, 2, 4, 3)  9.88 us
    ppermute x2, starting transfers between devices, from_behind_2(): return lax.ppermute(value, axis, pairs)  8.64 us
    all_to_all x2, local copies, waits for them, and re-layouts, shards_body(): lax.all_to_all(piece, 'row', split_axis=2, concat_axis=3, tiled=True)  6.35 us
    another operation x2, other arithmetic  5.6 us
  transfers between devices with their start and end apart: 5, of which 2 were waited for; matrix products, arithmetic and copies ran while one was open for 19% of the time, Pallas kernels for 0%

profile of v11, /device:TPU:0, one launch (start us, length us, event | category | flops | bytes accessed | tf_op | source)
XLA Modules:
  0.0 167.4 jit_solution(9409838119936275207)
XLA Ops:
  0.7 0.8 slice.137
  1.5 1.3 collective-permute-start
  2.9 1.3 constant_dynamic-update-slice_fusion.1
  4.3 0.6 fusion.105
  5.9 1.2 multiply_add_fusion
  7.2 1.3 fusion
  8.5 0.7 fusion.72
  9.4 0.8 fusion.11
  10.1 0.8 fusion.9
  10.9 0.8 add_bitcast_fusion
  11.8 0.4 fusion.17
  12.2 1.3 copy.94
  13.6 6.8 %all-to-all-start.1 = ((bf16[2,2,256,256]{3,1,0,2:T(2,128)(2,1)}), bf16[2,2,256,256]{3,1,0,2:T(2,128)(2,1)S(1)}, u32[]{:S(2)}, u32[]{:S(2)}) async-start(bf16[2,2,256,256]{3,1,0,2:T(2,128)(2,1)} %copy.94), calls=%async_computation.1 | async-start | bytes 1048576 | tf_op jit(solution)/shard_map/all_to_all | solution.py:234
  20.3 4.3 %sine_convert_fusion = (bf16[512,512]{1,0:T(8,128)(2,1)S(1)}, bf16[512,512]{1,0:T(8,128)(2,1)S(1)}) fusion(), kind=kLoop, calls=%fused_computation.83 | loop fusion | flops 4194304 | bytes 1048576 | tf_op jit(solution)/shard_map/convert.21
  24.8 1.3 copy.83
  26.1 5.0 %all-to-all-done.1 = bf16[2,2,256,256]{3,1,0,2:T(2,128)(2,1)S(1)} async-done(((bf16[2,2,256,256]{3,1,0,2:T(2,128)(2,1)}), bf16[2,2,256,256]{3,1,0,2:T(2,128)(2,1)S(1)}, u32[]{:S(2)}, u32[]{:S(2)}) %all-to-all-start.1) | async-done | bytes 524320 | tf_op jit(solution)/shard_map/all_to_all | solution.py:234
  31.2 3.6 %all-to-all-start = ((bf16[2,2,256,256]{3,1,0,2:T(2,128)(2,1)}), bf16[2,2,256,256]{3,1,0,2:T(2,128)(2,1)S(1)}, u32[]{:S(2)}, u32[]{:S(2)}) async-start(bf16[2,2,256,256]{3,1,0,2:T(2,128)(2,1)} %copy.83), calls=%async_computation | async-start | bytes 1048576 | tf_op jit(solution)/shard_map/all_to_all | solution.py:234
  34.8 3.2 %copy.95 = bf16[2,2,16,16,256]{3,4,2,1,0:T(8,128)(2,1)} copy(bf16[2,2,16,16,256]{4,1,0,3,2:T(2,128)(2,1)S(1)} %bitcast.143) | data formatting | bytes 1048576 | tf_op jit(solution)/shard_map/all_to_all | solution.py:234
  37.9 4.9 %copy.96 = bf16[2,2,16,512,8]{3,4,2,1,0:T(8,128)(2,1)S(1)} copy(bf16[2,2,16,512,8]{2,4,3,1,0:T(8,128)(2,1)} %bitcast.126) | data formatting | bytes 1048576 | tf_op jit(solution)/shard_map/reshape | solution.py:240
  42.9 8.1 %collective-permute-start.2 = (bf16[2,2,16,8,512]{4,3,2,1,0:T(8,128)(2,1)S(1)}, bf16[2,2,16,8,512]{4,3,2,1,0:T(8,128)(2,1)S(1)}, u32[]{:S(2)}, u32[]{:S(2)}) collective-permute-start(bf16[2,2,16,8,512]{4,3,2,1,0:T(8,128)(2,1)S(1)} %bitcast.128), channel_id=1, source_target_pairs={{0,127},{1,0},{2,1},{3,2},{4,3},{5,4},{6,5},{7,6},{8,7},{9,8},{10,... | collective-permute-start | bytes 1572872 | tf_op jit(solution)/shard_map/ppermute | solution.py:23
  51.0 0.7 fusion.130
  59.5 3.2 %copy.84 = bf16[2,2,16,16,256]{3,4,2,1,0:T(8,128)(2,1)} copy(bf16[2,2,16,16,256]{4,1,0,3,2:T(2,128)(2,1)S(1)} %bitcast.142) | data formatting | bytes 1048576 | tf_op jit(solution)/shard_map/all_to_all | solution.py:234
  62.7 4.9 %copy.85 = bf16[2,2,16,512,8]{3,4,2,1,0:T(8,128)(2,1)S(1)} copy(bf16[2,2,16,512,8]{2,4,3,1,0:T(8,128)(2,1)} %bitcast.127) | data formatting | bytes 1048576 | tf_op jit(solution)/shard_map/reshape | solution.py:240
  67.7 0.5 collective-permute-start.1
  68.2 1.3 fusion.54
  70.6 10.5 %collective-permute-done.1 = bf16[2,2,16,8,512]{4,3,2,1,0:T(8,128)(2,1)S(1)} collective-permute-done((bf16[2,2,16,8,512]{4,3,2,1,0:T(8,128)(2,1)S(1)}, bf16[2,2,16,8,512]{4,3,2,1,0:T(8,128)(2,1)S(1)}, u32[]{:S(2)}, u32[]{:S(2)}) %collective-permute-start.1) | collective-permute-done | bytes 524320 | tf_op jit(solution)/shard_map/ppermute | solution.py:23
  81.1 1.3 fusion.62
  83.5 2.5 %broadcast_in_dim.8.refs_0_ = bf16[256,16,512]{2,1,0:T(8,128)(2,1)} broadcast(bf16[]{:T(256)} %constant.161.clone.1), dimensions={} | broadcast | bytes 4194306 | tf_op jit(solution)/shard_map/broadcast_in_dim | solution.py:270
  86.0 9.9 %shard_map.77 = (bf16[2,4,4,16,4096]{4,3,2,1,0:T(8,128)(2,1)}, bf16[256,16,512]{2,1,0:T(8,128)(2,1)}) custom-call(s32[64]{0:T(128)S(1)} %get-tuple-element.60.dest_ref, bf16[2,8,128,512]{3,2,1,0:T(8,128)(2,1)S(1)} %pad_maximum_fusion.1.prod_ref, bf16[512,1024]{1,0:T(8,128)(2,1)S(1)} %pad_maximum_fusion.4.cos_ref.sin_ref, ...), custom_call_target="tpu_custom_call", output_to_operand_aliasing={{1}: (7, {})} | custom-call | flops 3221225472 | bytes 6291456 | tf_op jit(solution)/shard_map/pallas_call | solution.py:177
  95.9 9.9 %shard_map.78 = (bf16[2,4,4,16,4096]{4,3,2,1,0:T(8,128)(2,1)}, bf16[256,16,512]{2,1,0:T(8,128)(2,1)}) custom-call(s32[64]{0:T(128)S(1)} %get-tuple-element.61.dest_ref, bf16[2,8,128,512]{3,2,1,0:T(8,128)(2,1)S(1)} %pad_maximum_fusion.prod_ref, bf16[512,1024]{1,0:T(8,128)(2,1)S(1)} %pad_maximum_fusion.4.cos_ref.sin_ref, ...), custom_call_target="tpu_custom_call", output_to_operand_aliasing={{1}: (7, {}), {0}: (8, {})} | custom-call | flops 3221225472 | bytes 6291456 | tf_op jit(solution)/shard_map/pallas_call | solution.py:177
  105.8 59.3 %all_to_all.35 = bf16[128,32,512]{2,1,0:T(8,128)(2,1)S(1)} all-to-all(bf16[128,32,512]{2,1,0:T(8,128)(2,1)} %bitcast.124), channel_id=1, replica_groups=mesh['row'=16,'col'=8] {'row','col'}, dimensions={0} | all-to-all | bytes 8388608 | tf_op jit(solution)/shard_map/all_to_all | solution.py:284
  165.1 2.2 %convolution_convert_fusion = bf16[4096,128]{1,0:T(8,128)(2,1)} fusion(bf16[4096,512]{1,0:T(8,128)(2,1)S(1)} %bitcast.125, bf16[1,512,128]{2,1,0:T(8,128)(2,1)S(1)} %copy-done), kind=kOutput, calls=%fused_computation | convolution fusion | flops 537395200 | bytes 5373952 | tf_op jit(solution)/shard_map/dot_general | solution.py:285
  (42 shorter events, 4.0 us)
Async XLA Ops:
  0.6 164.5 %copy-start = (bf16[1,512,128]{2,1,0:T(8,128)(2,1)S(1)}, bf16[1,512,128]{2,1,0:T(8,128)(2,1)}, u32[]{:S(2)}) copy-start(bf16[1,512,128]{2,1,0:T(8,128)(2,1)} %param.9) | copy-start | bytes 393220
  0.6 4.4 %copy-start.4 = (s32[128,1]{0,1:T(1,128)S(1)}, s32[128,1]{0,1:T(1,128)}, u32[]{:S(2)}) copy-start(s32[128,1]{0,1:T(1,128)} %param.8) | copy-start | bytes 1540
  1.5 7.9 %collective-permute-start = (bf16[4,3,512]{2,1,0:T(4,128)(2,1)S(1)}, bf16[4,3,512]{2,1,0:T(4,128)(2,1)S(1)}, u32[]{:S(2)}, u32[]{:S(2)}) collective-permute-start(bf16[4,3,512]{2,1,0:T(4,128)(2,1)S(1)} %slice.137), channel_id=1, source_target_pairs={{8,0},{16,8},{24,16},{32,24},{40,32},{48,40},{56,48},{64,56},{72,6... | collective-permute-start | bytes 36872 | tf_op jit(solution)/shard_map/ppermute | solution.py:17
  7.2 1.3 copy-start.2
  13.6 17.6 %all-to-all-start.1 = ((bf16[2,2,256,256]{3,1,0,2:T(2,128)(2,1)}), bf16[2,2,256,256]{3,1,0,2:T(2,128)(2,1)S(1)}, u32[]{:S(2)}, u32[]{:S(2)}) async-start(bf16[2,2,256,256]{3,1,0,2:T(2,128)(2,1)} %copy.94), calls=%async_computation.1 | async-start | bytes 1048576 | tf_op jit(solution)/shard_map/all_to_all | solution.py:234
  31.2 28.4 %all-to-all-start = ((bf16[2,2,256,256]{3,1,0,2:T(2,128)(2,1)}), bf16[2,2,256,256]{3,1,0,2:T(2,128)(2,1)S(1)}, u32[]{:S(2)}, u32[]{:S(2)}) async-start(bf16[2,2,256,256]{3,1,0,2:T(2,128)(2,1)} %copy.83), calls=%async_computation | async-start | bytes 1048576 | tf_op jit(solution)/shard_map/all_to_all | solution.py:234
  37.9 13.1 %copy-start.3 = (s32[2,2]{1,0:T(2,128)S(1)}, s32[2,2]{1,0:T(2,128)}, u32[]{:S(2)}) copy-start(s32[2,2]{1,0:T(2,128)} %param.7) | copy-start | bytes 52
  42.9 25.3 %collective-permute-start.2 = (bf16[2,2,16,8,512]{4,3,2,1,0:T(8,128)(2,1)S(1)}, bf16[2,2,16,8,512]{4,3,2,1,0:T(8,128)(2,1)S(1)}, u32[]{:S(2)}, u32[]{:S(2)}) collective-permute-start(bf16[2,2,16,8,512]{4,3,2,1,0:T(8,128)(2,1)S(1)} %bitcast.128), channel_id=1, source_target_pairs={{0,127},{1,0},{2,1},{3,2},{4,3},{5,4},{6,5},{7,6},{8,7},{9,8},{10,... | collective-permute-start | bytes 1572872 | tf_op jit(solution)/shard_map/ppermute | solution.py:23
  67.7 13.4 %collective-permute-start.1 = (bf16[2,2,16,8,512]{4,3,2,1,0:T(8,128)(2,1)S(1)}, bf16[2,2,16,8,512]{4,3,2,1,0:T(8,128)(2,1)S(1)}, u32[]{:S(2)}, u32[]{:S(2)}) collective-permute-start(bf16[2,2,16,8,512]{4,3,2,1,0:T(8,128)(2,1)S(1)} %bitcast.132), channel_id=1, source_target_pairs={{0,127},{1,0},{2,1},{3,2},{4,3},{5,4},{6,5},{7,6},{8,7},{9,8},{10,... | collective-permute-start | bytes 1572872 | tf_op jit(solution)/shard_map/ppermute | solution.py:23
  83.5 2.5 %copy-start.1 = (bf16[1,256,256]{2,1,0:T(8,128)(2,1)S(1)}, bf16[1,256,256]{2,1,0:T(8,128)(2,1)}, u32[]{:S(2)}) copy-start(bf16[1,256,256]{2,1,0:T(8,128)(2,1)} %constant.165.mix_ref) | copy-start | bytes 393220

commit v12 on v10

--- a/solution.py
+++ b/solution.py
@@ -95,11 +95,7 @@
     twist_imag = first_imag * twist_cos - first_real * twist_sin
 
     twist = jnp.concatenate([twist_real, twist_imag], axis=0)
-    high = twist.astype(jnp.bfloat16)
-    low = (twist - high.astype(f32)).astype(jnp.bfloat16)
-    mixed = jnp.dot(mix_ref[0], high, preferred_element_type=f32) + jnp.dot(
-        mix_ref[0], low, preferred_element_type=f32
-    )
+    mixed = jnp.dot(mix_ref[0], twist.astype(jnp.bfloat16), preferred_element_type=f32)
     out_real = mixed[:rows_all]
     out_imag = mixed[rows_all:]
     feature = jnp.log1p(out_real * out_real + out_imag * out_imag).astype(feat_scratch.dtype)
@@ -185,9 +181,10 @@
         compiler_params=pltpu.CompilerParams(
             vmem_limit_bytes=48 * 1024 * 1024,
             dimension_semantics=("arbitrary",),
+            allow_input_fusion=[index == 1 for index in range(len(operands))],
         ),
         cost_estimate=pl.CostEstimate(
-            flops=blocks * (8 * rows * sub_n * sub_n + 16 * rows * rows * sub_n),
+            flops=blocks * (8 * rows * sub_n * sub_n + 8 * rows * rows * sub_n),
             transcendentals=blocks * rows * sub_n,
             bytes_accessed=blocks * rows * sub_n * 2 * 5 + 4 * sub_n * sub_n,
         ),

time: 161 us -> 159 us (0.988)
  Pallas kernels: 19.8 us -> 18.1 us
    pallas_call x2, Pallas kernels: 19.8 us -> 18.1 us  [spectrum_call(): pl.pallas_call(spectrum_kernel, grid_spec=grid_spec, out_shape=[jax.Shape...]
where the time goes in v12:
time: 159 us
  blocking collectives  59.1 us (37%)
  local copies, waits for them, and re-layouts  23.3 us (15%)
  Pallas kernels  18.1 us (11%)
  waiting for transfers between devices  15.7 us (10%)
  other arithmetic  15 us (9%)
  starting transfers between devices  13.6 us (9%)
  between operations  8.63 us (5%)
  matrix products  5.31 us (3%)
    all_to_all x1, blocking collectives, shards_body(): lax.all_to_all(outgoing, ('row', 'col'), split_axis=0, concat_axis=0, til...  59.1 us
    pallas_call x2, Pallas kernels, spectrum_call(): pl.pallas_call(spectrum_kernel, grid_spec=grid_spec, out_shape=[jax.Shape...  18.1 us
    ppermute x2, waiting for transfers between devices, from_behind_2(): return lax.ppermute(value, axis, pairs)  12.5 us
    reshape x2, local copies, waits for them, and re-layouts, shards_body(): ordered.reshape(2, part, per_device, sub_n, RADIX).transpose(0, 1, 2, 4, 3)  9.87 us
    all_to_all x1, starting transfers between devices, shards_body(): lax.all_to_all(demod, 'row', split_axis=2, concat_axis=3, tiled=True)  6.78 us
    slice x3, local copies, waits for them, and re-layouts, shards_body(): ordered = swapped[:, half * part:(half + 1) * part]  6.15 us
    another operation x2, other arithmetic  5.61 us
    ppermute x2, starting transfers between devices, from_behind_2(): return lax.ppermute(value, axis, pairs)  5.52 us
  transfers between devices with their start and end apart: 4, of which 3 were waited for; matrix products, arithmetic and copies ran while one was open for 14% of the time, Pallas kernels for 0%

profile of v12, /device:TPU:0, one launch (start us, length us, event | category | flops | bytes accessed | tf_op | source)
XLA Modules:
  0.0 158.7 jit_solution(713224912675828197)
XLA Ops:
  0.6 0.8 slice.137
  1.4 1.3 collective-permute-start
  2.9 0.6 fusion.104
  4.1 1.2 multiply_add_fusion
  5.3 1.3 fusion
  6.7 0.7 fusion.71
  7.5 0.8 fusion.11
  8.3 0.8 fusion.9
  9.0 0.8 add_bitcast_fusion
  9.9 0.4 fusion.16
  10.4 1.8 %copy.84 = bf16[2,4,256,256]{3,1,0,2:T(4,128)(2,1)} copy(bf16[2,4,256,256]{3,2,1,0:T(8,128)(2,1)S(1)} %pad_maximum_fusion.2) | data formatting | bytes 2097152 | tf_op jit(solution)/shard_map/stack | solution.py:227
  12.2 6.8 %all-to-all-start = ((bf16[2,4,256,256]{3,1,0,2:T(4,128)(2,1)}), bf16[2,4,256,256]{3,1,0,2:T(4,128)(2,1)S(1)}, u32[]{:S(2)}, u32[]{:S(2)}) async-start(bf16[2,4,256,256]{3,1,0,2:T(4,128)(2,1)} %copy.84), calls=%async_computation | async-start | bytes 2097152 | tf_op jit(solution)/shard_map/all_to_all | solution.py:228
  19.0 0.7 fusion.130
  27.8 4.3 %sine_convert_fusion = (bf16[512,512]{1,0:T(8,128)(2,1)S(1)}, bf16[512,512]{1,0:T(8,128)(2,1)S(1)}) fusion(), kind=kLoop, calls=%fused_computation.83 | loop fusion | flops 4194304 | bytes 1048576 | tf_op jit(solution)/shard_map/convert.21
  32.2 3.2 %all-to-all-done = bf16[2,4,256,256]{3,1,0,2:T(4,128)(2,1)S(1)} async-done(((bf16[2,4,256,256]{3,1,0,2:T(4,128)(2,1)}), bf16[2,4,256,256]{3,1,0,2:T(4,128)(2,1)S(1)}, u32[]{:S(2)}, u32[]{:S(2)}) %all-to-all-start) | async-done | bytes 1048608 | tf_op jit(solution)/shard_map/all_to_all | solution.py:228
  35.4 0.6 copy.111
  36.0 0.5 all_to_all.19
  36.6 3.0 %copy.96 = bf16[2,2,16,4096]{2,3,1,0:T(8,128)(2,1)} copy(bf16[2,2,16,4096]{3,2,1,0:T(8,128)(2,1)S(1)} %get-tuple-element.32) | data formatting | bytes 1048576 | tf_op jit(solution)/shard_map/slice | solution.py:233
  39.6 4.9 %copy.97 = bf16[2,2,16,512,8]{3,4,2,1,0:T(8,128)(2,1)S(1)} copy(bf16[2,2,16,512,8]{2,4,3,1,0:T(8,128)(2,1)} %bitcast.126) | data formatting | bytes 1048576 | tf_op jit(solution)/shard_map/reshape | solution.py:234
  44.6 5.2 %collective-permute-start.2 = (bf16[2,2,16,8,512]{4,3,2,1,0:T(8,128)(2,1)S(1)}, bf16[2,2,16,8,512]{4,3,2,1,0:T(8,128)(2,1)}, u32[]{:S(2)}, u32[]{:S(2)}) collective-permute-start(bf16[2,2,16,8,512]{4,3,2,1,0:T(8,128)(2,1)S(1)} %bitcast.132), channel_id=1, source_target_pairs={{0,127},{1,0},{2,1},{3,2},{4,3},{5,4},{6,5},{7,6},{8,7},{9,8},{10,... | collective-permute-start | bytes 1572872 | tf_op jit(solution)/shard_map/ppermute | solution.py:23
  50.0 3.0 %copy.86 = bf16[2,2,16,4096]{2,3,1,0:T(8,128)(2,1)} copy(bf16[2,2,16,4096]{3,2,1,0:T(8,128)(2,1)S(1)} %get-tuple-element.33) | data formatting | bytes 1048576 | tf_op jit(solution)/shard_map/slice | solution.py:233
  53.0 4.9 %copy.87 = bf16[2,2,16,512,8]{3,4,2,1,0:T(8,128)(2,1)S(1)} copy(bf16[2,2,16,512,8]{2,4,3,1,0:T(8,128)(2,1)} %bitcast.127) | data formatting | bytes 1048576 | tf_op jit(solution)/shard_map/reshape | solution.py:234
  58.0 0.3 collective-permute-start.1
  58.3 3.5 %collective-permute-done.2 = bf16[2,2,16,8,512]{4,3,2,1,0:T(8,128)(2,1)} collective-permute-done((bf16[2,2,16,8,512]{4,3,2,1,0:T(8,128)(2,1)S(1)}, bf16[2,2,16,8,512]{4,3,2,1,0:T(8,128)(2,1)}, u32[]{:S(2)}, u32[]{:S(2)}) %collective-permute-start.2) | collective-permute-done | bytes 524320 | tf_op jit(solution)/shard_map/ppermute | solution.py:23
  61.8 2.3 %fusion.53 = (f32[2,2,16,8,512]{4,3,2,1,0:T(8,128)S(1)}, f32[2,2,16,8,512]{4,3,2,1,0:T(8,128)S(1)}, f32[2,2,16,8,512]{4,3,2,1,0:T(8,128)S(1)}, f32[2,2,16,8,512]{4,3,2,1,0:T(8,128)S(1)}) fusion(s32[]{:T(128)S(6)} %select_n.139, bf16[2,2,16,8,512]{4,3,2,1,0:T(8,128)(2,1)S(1)} %bitcast.133, bf16[2,2,16,8,512]{4,3,2,1,0:T(8,128)(2,1)} %collective-permute-done.2, ...), kind=kLoop, calls=%fused_computation.127 | loop fusion | flops 2097152 | bytes 5242896 | tf_op jit(solution)/shard_map/convert_element_type | solution.py:246
  65.3 9.1 %collective-permute-done.1 = bf16[2,2,16,8,512]{4,3,2,1,0:T(8,128)(2,1)S(1)} collective-permute-done((bf16[2,2,16,8,512]{4,3,2,1,0:T(8,128)(2,1)S(1)}, bf16[2,2,16,8,512]{4,3,2,1,0:T(8,128)(2,1)S(1)}, u32[]{:S(2)}, u32[]{:S(2)}) %collective-permute-start.1) | collective-permute-done | bytes 524320 | tf_op jit(solution)/shard_map/ppermute | solution.py:23
  74.3 1.3 fusion.61
  76.8 2.5 %broadcast_in_dim.8.refs_0_ = bf16[256,16,512]{2,1,0:T(8,128)(2,1)} broadcast(bf16[]{:T(256)} %constant.161.clone.1), dimensions={} | broadcast | bytes 4194306 | tf_op jit(solution)/shard_map/broadcast_in_dim | solution.py:264
  79.3 9.1 %shard_map.77 = (bf16[2,4,4,16,4096]{4,3,2,1,0:T(8,128)(2,1)}, bf16[256,16,512]{2,1,0:T(8,128)(2,1)}) custom-call(s32[64]{0:T(128)S(1)} %get-tuple-element.60.dest_ref, bf16[2,8,128,512]{3,2,1,0:T(8,128)(2,1)S(1)} %pad_maximum_fusion.1.prod_ref, bf16[512,1024]{1,0:T(8,128)(2,1)S(1)} %pad_maximum_fusion.5.cos_ref.sin_ref, ...), custom_call_target="tpu_custom_call", output_to_operand_aliasing={{1}: (7, {})} | custom-call | flops 2684354560 | bytes 6291456 | tf_op jit(solution)/shard_map/pallas_call | solution.py:173
  88.3 9.0 %shard_map.78 = (bf16[2,4,4,16,4096]{4,3,2,1,0:T(8,128)(2,1)}, bf16[256,16,512]{2,1,0:T(8,128)(2,1)}) custom-call(s32[64]{0:T(128)S(1)} %get-tuple-element.61.dest_ref, bf16[2,8,128,512]{3,2,1,0:T(8,128)(2,1)S(1)} %pad_maximum_fusion.prod_ref, bf16[512,1024]{1,0:T(8,128)(2,1)S(1)} %pad_maximum_fusion.5.cos_ref.sin_ref, ...), custom_call_target="tpu_custom_call", output_to_operand_aliasing={{1}: (7, {}), {0}: (8, {})} | custom-call | flops 2684354560 | bytes 6291456 | tf_op jit(solution)/shard_map/pallas_call | solution.py:173
  97.4 59.1 %all_to_all.23 = bf16[128,32,512]{2,1,0:T(8,128)(2,1)S(1)} all-to-all(bf16[128,32,512]{2,1,0:T(8,128)(2,1)} %bitcast.124), channel_id=1, replica_groups=mesh['row'=16,'col'=8] {'row','col'}, dimensions={0} | all-to-all | bytes 8388608 | tf_op jit(solution)/shard_map/all_to_all | solution.py:278
  156.5 2.2 %convolution_convert_fusion = bf16[4096,128]{1,0:T(8,128)(2,1)} fusion(bf16[4096,512]{1,0:T(8,128)(2,1)S(1)} %bitcast.125, bf16[1,512,128]{2,1,0:T(8,128)(2,1)S(1)} %copy-done), kind=kOutput, calls=%fused_computation | convolution fusion | flops 537395200 | bytes 5373952 | tf_op jit(solution)/shard_map/dot_general | solution.py:279
  (42 shorter events, 4.1 us)
Async XLA Ops:
  0.6 155.9 %copy-start = (bf16[1,512,128]{2,1,0:T(8,128)(2,1)S(1)}, bf16[1,512,128]{2,1,0:T(8,128)(2,1)}, u32[]{:S(2)}) copy-start(bf16[1,512,128]{2,1,0:T(8,128)(2,1)} %param.9) | copy-start | bytes 393220
  1.4 6.0 %collective-permute-start = (bf16[4,3,512]{2,1,0:T(4,128)(2,1)S(1)}, bf16[4,3,512]{2,1,0:T(4,128)(2,1)S(1)}, u32[]{:S(2)}, u32[]{:S(2)}) collective-permute-start(bf16[4,3,512]{2,1,0:T(4,128)(2,1)S(1)} %slice.137), channel_id=1, source_target_pairs={{8,0},{16,8},{24,16},{32,24},{40,32},{48,40},{56,48},{64,56},{72,6... | collective-permute-start | bytes 36872 | tf_op jit(solution)/shard_map/ppermute | solution.py:17
  5.3 1.3 copy-start.2
  10.4 8.6 %copy-start.3 = (s32[2,2]{1,0:T(2,128)S(1)}, s32[2,2]{1,0:T(2,128)}, u32[]{:S(2)}) copy-start(s32[2,2]{1,0:T(2,128)} %param.7) | copy-start | bytes 52
  10.4 14.3 %copy-start.4 = (s32[128,1]{0,1:T(1,128)S(1)}, s32[128,1]{0,1:T(1,128)}, u32[]{:S(2)}) copy-start(s32[128,1]{0,1:T(1,128)} %param.8) | copy-start | bytes 1540
  12.2 23.2 %all-to-all-start = ((bf16[2,4,256,256]{3,1,0,2:T(4,128)(2,1)}), bf16[2,4,256,256]{3,1,0,2:T(4,128)(2,1)S(1)}, u32[]{:S(2)}, u32[]{:S(2)}) async-start(bf16[2,4,256,256]{3,1,0,2:T(4,128)(2,1)} %copy.84), calls=%async_computation | async-start | bytes 2097152 | tf_op jit(solution)/shard_map/all_to_all | solution.py:228
  44.6 17.2 %collective-permute-start.2 = (bf16[2,2,16,8,512]{4,3,2,1,0:T(8,128)(2,1)S(1)}, bf16[2,2,16,8,512]{4,3,2,1,0:T(8,128)(2,1)}, u32[]{:S(2)}, u32[]{:S(2)}) collective-permute-start(bf16[2,2,16,8,512]{4,3,2,1,0:T(8,128)(2,1)S(1)} %bitcast.132), channel_id=1, source_target_pairs={{0,127},{1,0},{2,1},{3,2},{4,3},{5,4},{6,5},{7,6},{8,7},{9,8},{10,... | collective-permute-start | bytes 1572872 | tf_op jit(solution)/shard_map/ppermute | solution.py:23
  58.0 16.4 %collective-permute-start.1 = (bf16[2,2,16,8,512]{4,3,2,1,0:T(8,128)(2,1)S(1)}, bf16[2,2,16,8,512]{4,3,2,1,0:T(8,128)(2,1)S(1)}, u32[]{:S(2)}, u32[]{:S(2)}) collective-permute-start(bf16[2,2,16,8,512]{4,3,2,1,0:T(8,128)(2,1)S(1)} %bitcast.128), channel_id=1, source_target_pairs={{0,127},{1,0},{2,1},{3,2},{4,3},{5,4},{6,5},{7,6},{8,7},{9,8},{10,... | collective-permute-start | bytes 1572872 | tf_op jit(solution)/shard_map/ppermute | solution.py:23
  76.8 2.5 %copy-start.1 = (bf16[1,256,256]{2,1,0:T(8,128)(2,1)S(1)}, bf16[1,256,256]{2,1,0:T(8,128)(2,1)}, u32[]{:S(2)}) copy-start(bf16[1,256,256]{2,1,0:T(8,128)(2,1)} %constant.165.mix_ref) | copy-start | bytes 393220

commit v13 on v12

--- a/solution.py
+++ b/solution.py
@@ -234,22 +234,21 @@
         ordered = ordered.reshape(2, part, per_device, sub_n, RADIX).transpose(0, 1, 2, 4, 3)
         above = from_behind_2(ordered, ("row", "col"), -1)
         extended = jnp.concatenate([ordered, above], axis=2)
-        own_real = ordered[0].astype(jnp.float32)
-        own_imag = ordered[1].astype(jnp.float32)
-        prod_real = []
-        prod_imag = []
-        for wheel in range(orders.shape[0]):
-            for order_at in range(orders.shape[1]):
-                partner = lax.dynamic_slice_in_dim(
-                    extended, orders[wheel, order_at], per_device, axis=2
-                )
-                partner = partner.astype(jnp.float32)
-                prod_real.append(own_real * partner[0] + own_imag * partner[1])
-                prod_imag.append(own_imag * partner[0] - own_real * partner[1])
+        own = ordered.astype(jnp.float32)[:, :, None]
+        partner = jnp.stack(
+            [
+                lax.dynamic_slice_in_dim(extended, orders[wheel, order_at], per_device, axis=2)
+                for wheel in range(orders.shape[0])
+                for order_at in range(orders.shape[1])
+            ],
+            axis=2,
+        ).astype(jnp.float32)
+        prod_real = own[0] * partner[0] + own[1] * partner[1]
+        prod_imag = own[1] * partner[0] - own[0] * partner[1]
         pieces.append(
-            jnp.stack([jnp.stack(prod_real, axis=1), jnp.stack(prod_imag, axis=1)]).astype(
-                jnp.bfloat16
-            ).reshape(2, part, combos, per_device * RADIX, sub_n)
+            jnp.stack([prod_real, prod_imag])
+            .astype(jnp.bfloat16)
+            .reshape(2, part, combos, per_device * RADIX, sub_n)
         )
     tiles_dev = sensors * combos * RADIX
     capacity = max(2, 2 * tiles_dev // devices_n)

time: 159 us -> 193 us (1.21)
  local copies, waits for them, and re-layouts: 23.3 us -> 56.9 us
  other arithmetic: 15 us -> 28.9 us
  waiting for transfers between devices: 15.7 us -> 3.46 us
    mul x0 -> x6, local copies, waits for them, and re-layouts: none -> 27.3 us  [shards_body(): prod_real = own[0] * partner[0] + own[1] * partner[1]]
    ppermute x2, waiting for transfers between devices: 12.5 us -> 0.01 us  [from_behind_2(): return lax.ppermute(value, axis, pairs)]
    transpose x0 -> x2, local copies, waits for them, and re-layouts: none -> 11.3 us  [shards_body(): ordered.reshape(2, part, per_device, sub_n, RADIX).transpose(0, 1, 2, 4, 3)]
    reshape x2 -> x0, local copies, waits for them, and re-layouts: 9.87 us -> none  [shards_body(): ordered.reshape(2, part, per_device, sub_n, RADIX).transpose(0, 1, 2, 4, 3)]
    convert_element_type x2 -> x4, other arithmetic: 3.55 us -> 12.7 us  [the longest x2 12 us: shards_body(): own = ordered.astype(jnp.float32)[:, :, None]]
    another operation x8, other arithmetic: 6.54 us -> 12.6 us
    all_to_all x2, local copies, waits for them, and re-layouts: 1.11 us -> 3.11 us  [shards_body(): lax.all_to_all(demod, 'row', split_axis=2, concat_axis=3, tiled=True)]
  transfers between devices with their start and end apart: 4 -> 4, of which waited for: 3 -> 1; matrix products, arithmetic and copies ran while one was open for 14% -> 30% of each run, Pallas kernels for 0% -> 0%
where the time goes in v13:
time: 193 us; the launch traced here: 192 us
  blocking collectives  57.8 us (30%)
  local copies, waits for them, and re-layouts  56.9 us (29%)
  other arithmetic  28.9 us (15%)
  Pallas kernels  18 us (9%)
  starting transfers between devices  13 us (7%)
  between operations  8.79 us (5%)
  matrix products  5.32 us (3%)
  waiting for transfers between devices  3.46 us (2%)
    all_to_all x1, blocking collectives, shards_body(): lax.all_to_all(outgoing, ('row', 'col'), split_axis=0, concat_axis=0, til...  57.8 us
    mul x6, local copies, waits for them, and re-layouts, shards_body(): prod_real = own[0] * partner[0] + own[1] * partner[1]  27.3 us
    pallas_call x2, Pallas kernels, spectrum_call(): pl.pallas_call(spectrum_kernel, grid_spec=grid_spec, out_shape=[jax.Shape...  18 us
    convert_element_type x2, other arithmetic, shards_body(): own = ordered.astype(jnp.float32)[:, :, None]  12 us
    transpose x2, local copies, waits for them, and re-layouts, shards_body(): ordered.reshape(2, part, per_device, sub_n, RADIX).transpose(0, 1, 2, 4, 3)  11.3 us
    another operation x4, other arithmetic  7.18 us
    slice x3, local copies, waits for them, and re-layouts, shards_body(): ordered = swapped[:, half * part:(half + 1) * part]  6.92 us
    all_to_all x1, starting transfers between devices, shards_body(): lax.all_to_all(demod, 'row', split_axis=2, concat_axis=3, tiled=True)  6.78 us
  transfers between devices with their start and end apart: 4, of which 1 were waited for; matrix products, arithmetic and copies ran while one was open for 30% of the time, Pallas kernels for 0%

profile of v13, /device:TPU:0, one launch (start us, length us, event | category | flops | bytes accessed | tf_op | source)
XLA Modules:
  0.0 192.1 jit_solution(1610533516453155123)
XLA Ops:
  1.5 1.3 collective-permute-start
  2.7 1.3 constant_dynamic-update-slice_fusion.1
  5.7 1.2 multiply_add_fusion
  6.9 1.3 fusion
  10.9 0.8 add_bitcast_fusion
  12.2 1.8 copy.55
  14.0 6.8 %all-to-all-start = ((bf16[2,4,256,256]{3,1,0,2:T(4,128)(2,1)}), bf16[2,4,256,256]{3,1,0,2:T(4,128)(2,1)S(1)}, u32[]{:S(2)}, u32[]{:S(2)}) async-start(bf16[2,4,256,256]{3,1,0,2:T(4,128)(2,1)} %copy.55), calls=%async_computation | async-start | bytes 2097152 | tf_op jit(solution)/shard_map/all_to_all | solution.py:228
  29.2 4.3 %sine_convert_fusion = (bf16[512,512]{1,0:T(8,128)(2,1)S(1)}, bf16[512,512]{1,0:T(8,128)(2,1)S(1)}) fusion(), kind=kLoop, calls=%fused_computation.57 | loop fusion | flops 4194304 | bytes 1048576 | tf_op jit(solution)/shard_map/convert.5
  33.8 3.4 %all-to-all-done = bf16[2,4,256,256]{3,1,0,2:T(4,128)(2,1)S(1)} async-done(((bf16[2,4,256,256]{3,1,0,2:T(4,128)(2,1)}), bf16[2,4,256,256]{3,1,0,2:T(4,128)(2,1)S(1)}, u32[]{:S(2)}, u32[]{:S(2)}) %all-to-all-start) | async-done | bytes 1048608 | tf_op jit(solution)/shard_map/all_to_all | solution.py:228
  37.3 1.6 copy.76
  38.8 1.6 all_to_all.19
  40.4 0.9 fusion.81
  41.2 3.0 %copy.57 = bf16[2,2,16,4096]{2,3,1,0:T(8,128)(2,1)} copy(bf16[2,2,16,4096]{3,2,1,0:T(8,128)(2,1)S(1)} %get-tuple-element.25) | data formatting | bytes 1048576 | tf_op jit(solution)/shard_map/slice | solution.py:233
  44.3 6.0 %bitcast_convert_fusion.1 = f32[2,2,16,8,512]{2,3,4,1,0:T(8,128)} fusion(bf16[2,2,16,4096]{2,3,1,0:T(8,128)(2,1)} %copy.57), kind=kLoop, calls=%fused_computation.167 | loop fusion | flops 262144 | bytes 1572864 | tf_op jit(solution)/shard_map/convert_element_type | solution.py:237
  50.3 5.6 %copy.60 = bf16[2,2,16,8,512]{4,3,2,1,0:T(8,128)(2,1)} copy(bf16[2,2,16,8,512]{2,3,4,1,0:T(8,128)(2,1)} %bitcast.88) | data formatting | bytes 1048576 | tf_op jit(solution)/shard_map/transpose | solution.py:234
  55.9 4.6 %collective-permute-start.1 = (bf16[2,2,16,8,512]{4,3,2,1,0:T(8,128)(2,1)}, bf16[2,2,16,8,512]{4,3,2,1,0:T(8,128)(2,1)}, u32[]{:S(2)}, u32[]{:S(2)}) collective-permute-start(bf16[2,2,16,8,512]{4,3,2,1,0:T(8,128)(2,1)} %copy.60), channel_id=1, source_target_pairs={{0,127},{1,0},{2,1},{3,2},{4,3},{5,4},{6,5},{7,6},{8,7},{9,8},{10,... | collective-permute-start | bytes 1572872 | tf_op jit(solution)/shard_map/ppermute | solution.py:23
  60.5 7.4 %slice_bitcast_fusion.3 = (f32[2,16,8,512]{1,2,3,0:T(8,128)}, f32[2,16,8,512]{1,2,3,0:T(8,128)}) fusion(f32[2,2,16,8,512]{2,3,4,1,0:T(8,128)} %bitcast_convert_fusion.1), kind=kLoop, calls=%fused_computation.4 | loop fusion | bytes 2097152 | tf_op jit(solution)/shard_map/mul | solution.py:246
  67.9 3.0 %copy.61 = f32[2,16,8,512]{3,2,1,0:T(8,128)S(1)} copy(f32[2,16,8,512]{1,2,3,0:T(8,128)} %get-tuple-element.13) | data formatting | bytes 1048576 | tf_op jit(solution)/shard_map/mul | solution.py:246
  70.9 3.7 %copy.58 = f32[2,16,8,512]{3,2,1,0:T(8,128)} copy(f32[2,16,8,512]{1,2,3,0:T(8,128)} %get-tuple-element.12) | data formatting | bytes 1048576 | tf_op jit(solution)/shard_map/mul | solution.py:246
  74.6 3.0 %copy.64 = bf16[2,2,16,4096]{2,3,1,0:T(8,128)(2,1)} copy(bf16[2,2,16,4096]{3,2,1,0:T(8,128)(2,1)S(1)} %copy-done.4) | data formatting | bytes 1048576 | tf_op jit(solution)/shard_map/slice | solution.py:233
  77.6 6.0 %bitcast_convert_fusion = f32[2,2,16,8,512]{2,3,4,1,0:T(8,128)} fusion(bf16[2,2,16,4096]{2,3,1,0:T(8,128)(2,1)} %copy.64), kind=kLoop, calls=%fused_computation.166 | loop fusion | flops 262144 | bytes 1572864 | tf_op jit(solution)/shard_map/convert_element_type | solution.py:237
  83.6 5.6 %copy.67 = bf16[2,2,16,8,512]{4,3,2,1,0:T(8,128)(2,1)} copy(bf16[2,2,16,8,512]{2,3,4,1,0:T(8,128)(2,1)} %bitcast.89) | data formatting | bytes 1048576 | tf_op jit(solution)/shard_map/transpose | solution.py:234
  89.5 7.4 %slice_bitcast_fusion.1 = (f32[2,16,8,512]{1,2,3,0:T(8,128)}, f32[2,16,8,512]{1,2,3,0:T(8,128)}) fusion(f32[2,2,16,8,512]{2,3,4,1,0:T(8,128)} %bitcast_convert_fusion), kind=kLoop, calls=%fused_computation.2 | loop fusion | bytes 2097152 | tf_op jit(solution)/shard_map/mul | solution.py:246
  96.9 3.0 %copy.68 = f32[2,16,8,512]{3,2,1,0:T(8,128)S(1)} copy(f32[2,16,8,512]{1,2,3,0:T(8,128)} %get-tuple-element.11) | data formatting | bytes 1048576 | tf_op jit(solution)/shard_map/mul | solution.py:246
  99.8 3.0 %copy.65 = f32[2,16,8,512]{3,2,1,0:T(8,128)S(1)} copy(f32[2,16,8,512]{1,2,3,0:T(8,128)} %get-tuple-element.10) | data formatting | bytes 1048576 | tf_op jit(solution)/shard_map/mul | solution.py:246
  102.8 2.6 %fusion.29 = (bf16[2,2,1,16,8,512]{5,4,3,1,0,2:T(8,128)(2,1)S(1)}, bf16[2,2,1,16,8,512]{5,4,3,1,0,2:T(8,128)(2,1)S(1)}, bf16[2,2,1,16,8,512]{5,4,3,1,0,2:T(8,128)(2,1)S(1)}, bf16[2,2,1,16,8,512]{5,4,3,1,0,2:T(8,128)(2,1)S(1)}) fusion(s32[]{:T(128)S(6)} %select_n.139, bf16[2,2,16,8,512]{4,3,2,1,0:T(8,128)(2,1)} %copy.60, ...), kind=kLoop, calls=%fused_computation.77 | loop fusion | flops 1048576 | bytes 3145744 | tf_op jit(solution)/shard_map/stack | solution.py:238
  107.4 2.5 %fusion.21 = (bf16[2,2,1,16,8,512]{5,4,3,1,0,2:T(8,128)(2,1)S(1)}, bf16[2,2,1,16,8,512]{5,4,3,1,0,2:T(8,128)(2,1)S(1)}, bf16[2,2,1,16,8,512]{5,4,3,1,0,2:T(8,128)(2,1)S(1)}, bf16[2,2,1,16,8,512]{5,4,3,1,0,2:T(8,128)(2,1)S(1)}) fusion(s32[]{:T(128)S(6)} %select_n.139, bf16[2,2,16,8,512]{4,3,2,1,0:T(8,128)(2,1)} %copy.67, ...), kind=kLoop, calls=%fused_computation.69 | loop fusion | flops 1048576 | bytes 3145744 | tf_op jit(solution)/shard_map/stack | solution.py:238
  111.6 2.5 %broadcast_in_dim.8.refs_0_ = bf16[256,16,512]{2,1,0:T(8,128)(2,1)} broadcast(bf16[]{:T(256)} %constant.161.clone.1), dimensions={} | broadcast | bytes 4194306 | tf_op jit(solution)/shard_map/broadcast_in_dim | solution.py:263
  114.1 9.0 %shard_map.77 = (bf16[2,4,4,16,4096]{4,3,2,1,0:T(8,128)(2,1)}, bf16[256,16,512]{2,1,0:T(8,128)(2,1)}) custom-call(s32[64]{0:T(128)S(1)} %get-tuple-element.44.dest_ref, bf16[2,8,128,512]{3,2,1,0:T(8,128)(2,1)S(1)} %pad_maximum_fusion.1.prod_ref, bf16[512,1024]{1,0:T(8,128)(2,1)S(1)} %pad_maximum_fusion.3.cos_ref.sin_ref, ...), custom_call_target="tpu_custom_call", output_to_operand_aliasing={{1}: (7, {})} | custom-call | flops 2684354560 | bytes 6291456 | tf_op jit(solution)/shard_map/pallas_call | solution.py:173
  123.1 9.0 %shard_map.78 = (bf16[2,4,4,16,4096]{4,3,2,1,0:T(8,128)(2,1)}, bf16[256,16,512]{2,1,0:T(8,128)(2,1)}) custom-call(s32[64]{0:T(128)S(1)} %get-tuple-element.45.dest_ref, bf16[2,8,128,512]{3,2,1,0:T(8,128)(2,1)S(1)} %pad_maximum_fusion.prod_ref, bf16[512,1024]{1,0:T(8,128)(2,1)S(1)} %pad_maximum_fusion.3.cos_ref.sin_ref, ...), custom_call_target="tpu_custom_call", output_to_operand_aliasing={{1}: (7, {}), {0}: (8, {})} | custom-call | flops 2684354560 | bytes 6291456 | tf_op jit(solution)/shard_map/pallas_call | solution.py:173
  132.2 57.8 %all_to_all.23 = bf16[128,32,512]{2,1,0:T(8,128)(2,1)S(1)} all-to-all(bf16[128,32,512]{2,1,0:T(8,128)(2,1)} %bitcast.90), channel_id=1, replica_groups=mesh['row'=16,'col'=8] {'row','col'}, dimensions={0} | all-to-all | bytes 8388608 | tf_op jit(solution)/shard_map/all_to_all | solution.py:277
  189.9 2.2 %convolution_convert_fusion = bf16[4096,128]{1,0:T(8,128)(2,1)} fusion(bf16[4096,512]{1,0:T(8,128)(2,1)S(1)} %bitcast.91, bf16[1,512,128]{2,1,0:T(8,128)(2,1)S(1)} %copy-done), kind=kOutput, calls=%fused_computation | convolution fusion | flops 537395200 | bytes 5373952 | tf_op jit(solution)/shard_map/dot_general | solution.py:278
  (54 shorter events, 10.3 us)
Async XLA Ops:
  0.6 189.3 %copy-start = (bf16[1,512,128]{2,1,0:T(8,128)(2,1)S(1)}, bf16[1,512,128]{2,1,0:T(8,128)(2,1)}, u32[]{:S(2)}) copy-start(bf16[1,512,128]{2,1,0:T(8,128)(2,1)} %param.9) | copy-start | bytes 393220
  0.6 3.6 %copy-start.6 = (s32[128,1]{0,1:T(1,128)S(1)}, s32[128,1]{0,1:T(1,128)}, u32[]{:S(2)}) copy-start(s32[128,1]{0,1:T(1,128)} %param.8) | copy-start | bytes 1540
  1.5 7.9 %collective-permute-start = (bf16[4,3,512]{2,1,0:T(4,128)(2,1)S(1)}, bf16[4,3,512]{2,1,0:T(4,128)(2,1)S(1)}, u32[]{:S(2)}, u32[]{:S(2)}) collective-permute-start(bf16[4,3,512]{2,1,0:T(4,128)(2,1)S(1)} %slice.97), channel_id=1, source_target_pairs={{8,0},{16,8},{24,16},{32,24},{40,32},{48,40},{56,48},{64,56},{72,6... | collective-permute-start | bytes 36872 | tf_op jit(solution)/shard_map/ppermute | solution.py:17
  6.9 1.3 copy-start.2
  12.2 8.6 %copy-start.5 = (s32[2,2]{1,0:T(2,128)S(1)}, s32[2,2]{1,0:T(2,128)}, u32[]{:S(2)}) copy-start(s32[2,2]{1,0:T(2,128)} %param.7) | copy-start | bytes 52
  14.0 23.2 %all-to-all-start = ((bf16[2,4,256,256]{3,1,0,2:T(4,128)(2,1)}), bf16[2,4,256,256]{3,1,0,2:T(4,128)(2,1)S(1)}, u32[]{:S(2)}, u32[]{:S(2)}) async-start(bf16[2,4,256,256]{3,1,0,2:T(4,128)(2,1)} %copy.55), calls=%async_computation | async-start | bytes 2097152 | tf_op jit(solution)/shard_map/all_to_all | solution.py:228
  55.9 46.9 %collective-permute-start.1 = (bf16[2,2,16,8,512]{4,3,2,1,0:T(8,128)(2,1)}, bf16[2,2,16,8,512]{4,3,2,1,0:T(8,128)(2,1)}, u32[]{:S(2)}, u32[]{:S(2)}) collective-permute-start(bf16[2,2,16,8,512]{4,3,2,1,0:T(8,128)(2,1)} %copy.60), channel_id=1, source_target_pairs={{0,127},{1,0},{2,1},{3,2},{4,3},{5,4},{6,5},{7,6},{8,7},{9,8},{10,... | collective-permute-start | bytes 1572872 | tf_op jit(solution)/shard_map/ppermute | solution.py:23
  70.9 3.7 %copy-start.4 = (bf16[2,2,16,4096]{3,2,1,0:T(8,128)(2,1)S(1)}, bf16[2,2,16,4096]{3,2,1,0:T(8,128)(2,1)}, u32[]{:S(2)}) copy-start(bf16[2,2,16,4096]{3,2,1,0:T(8,128)(2,1)} %get-tuple-element.24) | copy-start | bytes 1572868
  89.2 18.2 %collective-permute-start.2 = (bf16[2,2,16,8,512]{4,3,2,1,0:T(8,128)(2,1)}, bf16[2,2,16,8,512]{4,3,2,1,0:T(8,128)(2,1)}, u32[]{:S(2)}, u32[]{:S(2)}) collective-permute-start(bf16[2,2,16,8,512]{4,3,2,1,0:T(8,128)(2,1)} %copy.67), channel_id=1, source_target_pairs={{0,127},{1,0},{2,1},{3,2},{4,3},{5,4},{6,5},{7,6},{8,7},{9,8},{10,... | collective-permute-start | bytes 1572872 | tf_op jit(solution)/shard_map/ppermute | solution.py:23
  105.4 1.0 copy-start.3
  111.6 2.5 %copy-start.1 = (bf16[1,256,256]{2,1,0:T(8,128)(2,1)S(1)}, bf16[1,256,256]{2,1,0:T(8,128)(2,1)}, u32[]{:S(2)}) copy-start(bf16[1,256,256]{2,1,0:T(8,128)(2,1)} %constant.165.mix_ref) | copy-start | bytes 393220
